TPU v7x, 512 devices: a whole 4x4x16 slice. The times are simulated.
512 devices in a mesh: rep: 4 (over z_hi), exp: 16 (over x, y), mdl: 8 (over z_lo, core).
Axes of the slice: x: 4, y: 4, z: 16 (z_hi: 4, z_lo: 4; z = z_hi * 4 + z_lo), core: 2. Of those that a mesh axis runs over, the one named last changes fastest.
Arguments:
- inner_experts: bfloat16 [4, 16, 2, 768, 2048], P('rep', 'exp', None, None, 'mdl'), may hold values from -6 to 6
- inner_dense: bfloat16 [4, 9216, 768], P('rep', ('exp', 'mdl')), may hold values from -6 to 6
- inner_small: bfloat16 [4, 18, 768], P('rep'), may hold values from -6 to 6
- inner_embed: bfloat16 [4, 8192, 768], P('rep', ('exp', 'mdl')), may hold values from -6 to 6
- outer_experts: float32 [16, 2, 768, 2048], P('exp', None, ('rep', 'mdl')), may hold values from -6 to 6
- outer_dense: float32 [9216, 768], P(('exp', 'mdl'), 'rep'), may hold values from -6 to 6
- outer_small: float32 [18, 768], P(None, 'rep'), may hold values from -6 to 6
- outer_embed: float32 [8192, 768], P(('exp', 'mdl'), 'rep'), may hold values from -6 to 6
- moment_experts: float32 [16, 2, 768, 2048], P('exp', None, ('rep', 'mdl')), may hold values from -3 to 3
- moment_dense: float32 [9216, 768], P(('exp', 'mdl'), 'rep'), may hold values from -3 to 3
- moment_small: float32 [18, 768], P(None, 'rep'), may hold values from -3 to 3
- moment_embed: float32 [8192, 768], P(('exp', 'mdl'), 'rep'), may hold values from -3 to 3
- embed_basis: float32 [768, 64], replicated, may hold values from -0.21875 to 0.21875
Outputs:
- new_outer_experts: float32 [16, 2, 768, 2048], P('exp', None, ('rep', 'mdl'))
- new_moment_experts: float32 [16, 2, 768, 2048], P('exp', None, ('rep', 'mdl'))
- copy_experts: bfloat16 [16, 2, 768, 2048], P('exp', None, None, 'mdl')
- new_outer_dense: float32 [9216, 768], P(('exp', 'mdl'), 'rep')
- new_moment_dense: float32 [9216, 768], P(('exp', 'mdl'), 'rep')
- copy_dense: bfloat16 [9216, 768], P(('exp', 'mdl'))
- new_outer_small: float32 [18, 768], P(None, 'rep')
- new_moment_small: float32 [18, 768], P(None, 'rep')
- copy_small: bfloat16 [18, 768], replicated
- new_outer_embed: float32 [8192, 768], P(('exp', 'mdl'), 'rep')
- new_moment_embed: float32 [8192, 768], P(('exp', 'mdl'), 'rep')
- copy_embed: bfloat16 [8192, 768], P(('exp', 'mdl'))
All inputs are finite; a program needn't handle non-finite values.
Results may differ from a plain program's by a relative error of at most 0.012.
Values may be sent and summed in bfloat16 or wider, within the bound.
No kernel may reach another device: no remote copies, remote signals or barrier semaphores. Data moves between devices by JAX's collectives and lax.ppermute only.
A program may use at most 64 MiB of HBM per device.

v0:
```python
import jax
import jax.numpy as jnp
from jax import lax
from jax.sharding import PartitionSpec as P

decay_rate = 0.5
outer_rate = 0.7


def nesterov(outer, moment, grad_value):
    moment_new = decay_rate * moment + grad_value
    outer_new = outer - outer_rate * (grad_value + decay_rate * moment_new)
    return (outer_new, moment_new)


def on_device(
    inner_experts,
    inner_dense,
    inner_small,
    inner_embed,
    outer_experts,
    outer_dense,
    outer_small,
    outer_embed,
    moment_experts,
    moment_dense,
    moment_small,
    moment_embed,
    embed_basis,
):
    groups = lax.axis_size("rep")
    own_shard = inner_experts[0, 0]
    row_count = outer_experts.shape[2]
    full_width = outer_experts.shape[3]
    pieces = lax.all_to_all(own_shard, ("rep", "mdl"), split_axis=1, concat_axis=2, tiled=True)
    expert_sum = jnp.sum(
        pieces.reshape(2, row_count, groups, full_width), axis=2, dtype=jnp.float32
    )
    grad_experts = outer_experts[0] - expert_sum / groups
    dense_sum, small_sum = (
        lax.psum_scatter(
            inner_dense[0].astype(jnp.float32).astype(jnp.bfloat16),
            "rep",
            scatter_dimension=1,
            tiled=True,
        ).astype(jnp.float32),
        lax.psum_scatter(
            inner_small[0].astype(jnp.float32).astype(jnp.bfloat16),
            "rep",
            scatter_dimension=1,
            tiled=True,
        ).astype(jnp.float32),
    )
    grad_dense = outer_dense - dense_sum / groups
    grad_small = outer_small - small_sum / groups
    col_count = outer_embed.shape[1]
    offset = lax.axis_index("rep") * col_count
    basis_part = lax.dynamic_slice_in_dim(embed_basis, offset, col_count, 0)
    partial_value = jnp.dot(
        outer_embed, basis_part, precision=lax.Precision.HIGHEST, preferred_element_type=jnp.float32
    )
    partial_value = (
        partial_value
        - jnp.dot(
            inner_embed[0].astype(jnp.float32),
            embed_basis,
            precision=lax.Precision.HIGHEST,
            preferred_element_type=jnp.float32,
        )
        / groups
    )
    coefficient = lax.psum(partial_value, "rep")
    grad_embed = jnp.dot(
        coefficient,
        basis_part.T,
        precision=lax.Precision.HIGHEST,
        preferred_element_type=jnp.float32,
    )
    expert_outer, expert_moment = nesterov(outer_experts[0], moment_experts[0], grad_experts)
    dense_outer, dense_moment = nesterov(outer_dense, moment_dense, grad_dense)
    small_outer, small_moment = nesterov(outer_small, moment_small, grad_small)
    embed_outer, embed_moment = nesterov(outer_embed, moment_embed, grad_embed)
    spread = lax.all_to_all(
        expert_outer.astype(jnp.bfloat16), "mdl", split_axis=2, concat_axis=1, tiled=True
    )
    copies = (
        lax.all_gather(spread, "rep", axis=1, tiled=True),
        lax.all_gather(dense_outer.astype(jnp.bfloat16), "rep", axis=1, tiled=True),
        lax.all_gather(small_outer.astype(jnp.bfloat16), "rep", axis=1, tiled=True),
        lax.all_gather(embed_outer.astype(jnp.bfloat16), "rep", axis=1, tiled=True),
    )
    return (
        expert_outer[None],
        expert_moment[None],
        copies[0][None],
        dense_outer,
        dense_moment,
        copies[1],
        small_outer,
        small_moment,
        copies[2],
        embed_outer,
        embed_moment,
        copies[3],
    )


def solution(mesh):
    placed = (
        P("rep", "exp", None, None, "mdl"),
        P("rep", ("exp", "mdl"), None),
        P("rep", None, None),
        P("rep", ("exp", "mdl"), None),
        P("exp", None, ("rep", "mdl"), None),
        P(("exp", "mdl"), "rep"),
        P(None, "rep"),
        P(("exp", "mdl"), "rep"),
        P("exp", None, ("rep", "mdl"), None),
        P(("exp", "mdl"), "rep"),
        P(None, "rep"),
        P(("exp", "mdl"), "rep"),
        P(),
    )
    return jax.shard_map(
        on_device,
        mesh=mesh,
        in_specs=placed,
        out_specs=(
            P("exp", None, ("rep", "mdl"), None),
            P("exp", None, ("rep", "mdl"), None),
            P("exp", None, None, "mdl"),
            P(("exp", "mdl"), "rep"),
            P(("exp", "mdl"), "rep"),
            P(("exp", "mdl"), None),
            P(None, "rep"),
            P(None, "rep"),
            P(),
            P(("exp", "mdl"), "rep"),
            P(("exp", "mdl"), "rep"),
            P(("exp", "mdl"), None),
        ),
        check_vma=False,
    )
```

profile of v0, /device:TPU:104, one launch (start us, length us, event | category | flops | bytes accessed | tf_op | source)
XLA Modules:
  0.0 201.4 jit_solution(756205942519219298)
XLA Ops:
  7.2 2.9 %copy.73 = bf16[1,1,2,768,256]{4,2,3,1,0:T(2,128)(2,1)} copy(bf16[1,1,2,768,256]{4,3,2,1,0:T(8,128)(2,1)} %param.13) | data formatting | bytes 1572864 | tf_op args[0]
  10.1 14.6 %all-to-all-start = ((bf16[2,768,256]{2,0,1:T(2,128)(2,1)}), bf16[2,768,256]{2,0,1:T(2,128)(2,1)S(1)}, u32[]{:S(2)}, u32[]{:S(2)}) async-start(bf16[2,768,256]{2,0,1:T(2,128)(2,1)} %bitcast.75), calls=%async_computation | async-start | bytes 1572864 | tf_op jit(solution)/shard_map/all_to_all | solution.py:35
  24.8 0.8 copy.68
  25.7 0.8 copy.66
  26.5 0.3 convolution_bitcast_fusion
  26.8 0.2 fusion
  27.1 57.0 %psum.7 = f32[64,64]{0,1:T(8,128)S(1)} all-reduce(f32[64,64]{0,1:T(8,128)S(1)} %fusion), channel_id=1, replica_groups=mesh['rep'=4,'exp'=16,'mdl'=8] {'rep'}, use_global_device_ids=true, to_apply=%region_3.0 | all-reduce | flops 4096 | bytes 32768 | tf_op jit(solution)/shard_map/psum | solution.py:72
  84.0 1.0 convert_bitcast_fusion.1
  85.0 18.8 %all-gather.2 = bf16[4,192,64]{1,2,0:T(8,128)(2,1)S(1)} all-gather(bf16[1,192,64]{1,2,0:T(8,128)(2,1)S(1)} %get-tuple-element.36), channel_id=1, replica_groups=mesh['rep'=4,'exp'=16,'mdl'=8] {'rep'}, dimensions={0}, use_global_device_ids=true | all-gather | bytes 122880 | tf_op jit(solution)/shard_map/all_gather | solution.py:90
  103.8 0.1 copy.64
  103.9 0.8 reshape.49
  104.6 0.9 copy.69
  105.5 0.6 convert_bitcast_fusion.2
  106.2 17.4 %all-gather.1 = bf16[4,192,18]{1,2,0:T(8,128)(2,1)S(1)} all-gather(bf16[1,192,18]{1,2,0:T(8,128)(2,1)S(1)} %get-tuple-element.39), channel_id=1, replica_groups=mesh['rep'=4,'exp'=16,'mdl'=8] {'rep'}, dimensions={0}, use_global_device_ids=true | all-gather | bytes 34560 | tf_op jit(solution)/shard_map/all_gather | solution.py:89
  123.6 0.7 reshape.47
  124.3 0.9 copy.67
  125.2 0.3 copy.72
  125.5 0.7 reshape.42
  126.2 1.0 reduce_sum.9
  127.2 0.1 copy-done.2
  127.3 0.1 fusion.5
  127.5 0.7 copy.59
  128.2 2.0 reshape.54
  130.2 8.7 %all-to-all-start.1 = ((bf16[8,2,6144]{2,1,0:T(2,128)(2,1)}), bf16[8,2,6144]{2,1,0:T(2,128)(2,1)S(1)}, u32[]{:S(2)}, u32[]{:S(2)}) async-start(bf16[8,2,6144]{2,1,0:T(2,128)(2,1)} %reshape.54), calls=%async_computation.1 | async-start | bytes 393216 | tf_op jit(solution)/shard_map/all_to_all | solution.py:83
  138.9 0.7 convert_bitcast_fusion
  139.6 18.1 %all-gather = bf16[4,192,72]{1,2,0:T(8,128)(2,1)S(1)} all-gather(bf16[1,192,72]{1,2,0:T(8,128)(2,1)S(1)} %get-tuple-element.42), channel_id=1, replica_groups=mesh['rep'=4,'exp'=16,'mdl'=8] {'rep'}, dimensions={0}, use_global_device_ids=true | all-gather | bytes 138240 | tf_op jit(solution)/shard_map/all_gather | solution.py:88
  157.7 0.8 reshape.45
  158.5 1.0 multiply_subtract_fusion
  159.5 1.5 reshape.55
  161.0 0.6 copy.60
  161.6 32.1 %all_gather.12 = bf16[2,768,256]{2,1,0:T(8,128)(2,1)S(1)} all-gather(bf16[2,192,256]{2,1,0:T(8,128)(2,1)S(1)} %bitcast.83), channel_id=1, replica_groups=mesh['rep'=4,'exp'=16,'mdl'=8] {'rep'}, dimensions={1}, use_global_device_ids=true | all-gather | bytes 983040 | tf_op jit(solution)/shard_map/all_gather | solution.py:87
  193.7 0.9 copy.75
  (33 shorter events, 0.3 us)
Async XLA Ops:
  7.2 19.3 %copy-start = (f32[768,64]{0,1:T(8,128)S(1)}, f32[768,64]{0,1:T(8,128)}, u32[]{:S(2)}) copy-start(f32[768,64]{0,1:T(8,128)} %param.25) | copy-start | bytes 589828
  7.2 17.6 %copy-start.9 = (bf16[1,18,768]{2,1,0:T(8,128)(2,1)S(1)}, bf16[1,18,768]{2,1,0:T(8,128)(2,1)}, u32[]{:S(2)}) copy-start(bf16[1,18,768]{2,1,0:T(8,128)(2,1)} %param.15) | copy-start | bytes 82948
  7.2 18.5 %copy-start.4 = (bf16[1,72,768]{2,1,0:T(8,128)(2,1)S(1)}, bf16[1,72,768]{2,1,0:T(8,128)(2,1)}, u32[]{:S(2)}) copy-start(bf16[1,72,768]{2,1,0:T(8,128)(2,1)} %param.14) | copy-start | bytes 331780
  10.1 16.5 %copy-start.3 = (f32[64,192]{1,0:T(8,128)S(1)}, f32[64,192]{1,0:T(8,128)}, u32[]{:S(2)}) copy-start(f32[64,192]{1,0:T(8,128)} %param.20) | copy-start | bytes 147460
  10.1 16.7 %copy-start.5 = (bf16[1,64,768]{2,1,0:T(8,128)(2,1)S(1)}, bf16[1,64,768]{2,1,0:T(8,128)(2,1)}, u32[]{:S(2)}) copy-start(bf16[1,64,768]{2,1,0:T(8,128)(2,1)} %param.16) | copy-start | bytes 294916
  10.1 74.0 %copy-start.8 = (f32[64,192]{1,0:T(8,128)S(1)}, f32[64,192]{1,0:T(8,128)}, u32[]{:S(2)}) copy-start(f32[64,192]{1,0:T(8,128)} %param.24) | copy-start | bytes 147460
  10.1 115.1 %all-to-all-start = ((bf16[2,768,256]{2,0,1:T(2,128)(2,1)}), bf16[2,768,256]{2,0,1:T(2,128)(2,1)S(1)}, u32[]{:S(2)}, u32[]{:S(2)}) async-start(bf16[2,768,256]{2,0,1:T(2,128)(2,1)} %bitcast.75), calls=%async_computation | async-start | bytes 1572864 | tf_op jit(solution)/shard_map/all_to_all | solution.py:35
  24.7 80.8 %copy-start.10 = (f32[18,192]{1,0:T(8,128)S(1)}, f32[18,192]{1,0:T(8,128)}, u32[]{:S(2)}) copy-start(f32[18,192]{1,0:T(8,128)} %param.19) | copy-start | bytes 41476
  24.7 80.8 %copy-start.11 = (f32[18,192]{1,0:T(8,128)S(1)}, f32[18,192]{1,0:T(8,128)}, u32[]{:S(2)}) copy-start(f32[18,192]{1,0:T(8,128)} %param.23) | copy-start | bytes 41476
  24.7 79.9 %reduce-scatter.9.cloned.1.call-start = ((), (), s32[]{:S(2)}) async-start(), calls=%async_computation.5 | async-start | bytes 245760
  25.6 98.7 %reduce-scatter.7.cloned.1.call-start = ((), (), s32[]{:S(2)}) async-start(), calls=%async_computation.4 | async-start | bytes 245760
  126.2 1.0 copy-start.1
  126.2 1.1 copy-start.2
  127.4 11.5 %copy-start.6 = (f32[72,192]{1,0:T(8,128)S(1)}, f32[72,192]{1,0:T(8,128)}, u32[]{:S(2)}) copy-start(f32[72,192]{1,0:T(8,128)} %param.18) | copy-start | bytes 165892
  127.5 11.5 %copy-start.7 = (f32[72,192]{1,0:T(8,128)S(1)}, f32[72,192]{1,0:T(8,128)}, u32[]{:S(2)}) copy-start(f32[72,192]{1,0:T(8,128)} %param.22) | copy-start | bytes 165892
  130.2 29.3 %all-to-all-start.1 = ((bf16[8,2,6144]{2,1,0:T(2,128)(2,1)}), bf16[8,2,6144]{2,1,0:T(2,128)(2,1)S(1)}, u32[]{:S(2)}, u32[]{:S(2)}) async-start(bf16[8,2,6144]{2,1,0:T(2,128)(2,1)} %reshape.54), calls=%async_computation.1 | async-start | bytes 393216 | tf_op jit(solution)/shard_map/all_to_all | solution.py:83
Sparse Core Ops, SparseCore 0:
  28.9 41.6 reduce-scatter.8
  73.9 34.5 reduce-scatter.6
where the time goes:
time: 203 us; the launch traced here: 201 us
  blocking collectives  143 us (70%)
  starting transfers between devices  23.4 us (12%)
  local copies, waits for them, and re-layouts  15.6 us (8%)
  between operations  14.3 us (7%)
  other arithmetic  3.39 us (2%)
    psum x1, blocking collectives, on_device(): coefficient = lax.psum(partial_value, 'rep')  57 us
    all_gather x1, blocking collectives, on_device(): lax.all_gather(spread, 'rep', axis=1, tiled=True)  32.1 us
    all_gather x1, blocking collectives, on_device(): lax.all_gather(embed_outer.astype(jnp.bfloat16), 'rep', axis=1, tiled=True)  18.8 us
    all_gather x1, blocking collectives, on_device(): lax.all_gather(dense_outer.astype(jnp.bfloat16), 'rep', axis=1, tiled=True)  18.1 us
    all_gather x1, blocking collectives, on_device(): lax.all_gather(small_outer.astype(jnp.bfloat16), 'rep', axis=1, tiled=True)  17.4 us
    all_to_all x1, starting transfers between devices, on_device(): lax.all_to_all(own_shard, ('rep', 'mdl'), split_axis=1, concat_axis=2, ti...  14.6 us
    unnamed x35, local copies, waits for them, and re-layouts  13.1 us
    all_to_all x1, starting transfers between devices, on_device(): lax.all_to_all(expert_outer.astype(jnp.bfloat16), 'mdl', split_axis=2, co...  8.7 us
  transfers between devices with their start and end apart: 4, of which 0 were waited for; matrix products, arithmetic and copies ran while one was open for 5% of the time, Pallas kernels for 0%

commit v1 on v0

v1 whole, which is shorter than its diff:
```python
import jax
import jax.numpy as jnp
from jax import lax
from jax.sharding import PartitionSpec as P

decay_rate = 0.5
outer_rate = 0.7


def nesterov(outer, moment, grad_value):
    moment_new = decay_rate * moment + grad_value
    outer_new = outer - outer_rate * (grad_value + decay_rate * moment_new)
    return (outer_new, moment_new)


def split_rows(x, parts):
    rows, cols = x.shape
    return x.reshape(rows, parts, cols // parts).transpose(1, 0, 2).reshape(parts, -1)


def on_device(
    inner_experts,
    inner_dense,
    inner_small,
    inner_embed,
    outer_experts,
    outer_dense,
    outer_small,
    outer_embed,
    moment_experts,
    moment_dense,
    moment_small,
    moment_embed,
    embed_basis,
):
    groups = lax.axis_size("rep")
    hi_prec = lax.Precision.HIGHEST

    own_shard = inner_experts[0, 0]
    halves, all_rows, my_cols = own_shard.shape
    rep_rows = all_rows // groups
    ex_send = (
        own_shard.reshape(halves, groups, rep_rows, my_cols)
        .transpose(1, 0, 2, 3)
        .reshape(groups, -1)
    )
    de_send = split_rows(inner_dense[0], groups)
    sm_send = split_rows(inner_small[0], groups)

    col_count = outer_embed.shape[1]
    offset = lax.axis_index("rep") * col_count
    basis_part = lax.dynamic_slice_in_dim(embed_basis, offset, col_count, 0)
    partial_value = jnp.dot(
        outer_embed, basis_part, precision=hi_prec, preferred_element_type=jnp.float32
    ) - jnp.dot(
        inner_embed[0].astype(jnp.float32),
        embed_basis,
        precision=hi_prec,
        preferred_element_type=jnp.float32,
    ) / groups
    part_hi = partial_value.astype(jnp.bfloat16)
    part_lo = (partial_value - part_hi.astype(jnp.float32)).astype(jnp.bfloat16)
    pp = jnp.concatenate([part_hi.reshape(-1), part_lo.reshape(-1)])
    pp_send = jnp.broadcast_to(pp[None], (groups, pp.shape[0]))

    sizes = [ex_send.shape[1], de_send.shape[1], sm_send.shape[1], pp.shape[0]]
    send = jnp.concatenate([ex_send, de_send, sm_send, pp_send], axis=1)
    recv = lax.all_to_all(send, "rep", split_axis=0, concat_axis=0, tiled=True)
    bounds = [0]
    for s in sizes:
        bounds.append(bounds[-1] + s)
    parts = [recv[:, bounds[i] : bounds[i + 1]] for i in range(4)]

    ex_sum = jnp.sum(parts[0].astype(jnp.float32), axis=0).reshape(halves, rep_rows, my_cols)
    dense_sum = jnp.sum(parts[1].astype(jnp.float32), axis=0).reshape(outer_dense.shape)
    small_sum = jnp.sum(parts[2].astype(jnp.float32), axis=0).reshape(outer_small.shape)
    pp_recv = parts[3].astype(jnp.float32)
    nco = partial_value.size
    coefficient = jnp.sum(pp_recv[:, :nco] + pp_recv[:, nco:], axis=0).reshape(
        partial_value.shape
    )

    expert_sum = lax.all_to_all(ex_sum, "mdl", split_axis=1, concat_axis=2, tiled=True)
    grad_experts = outer_experts[0] - expert_sum / groups
    grad_dense = outer_dense - dense_sum / groups
    grad_small = outer_small - small_sum / groups
    grad_embed = jnp.dot(
        coefficient, basis_part.T, precision=hi_prec, preferred_element_type=jnp.float32
    )
    expert_outer, expert_moment = nesterov(outer_experts[0], moment_experts[0], grad_experts)
    dense_outer, dense_moment = nesterov(outer_dense, moment_dense, grad_dense)
    small_outer, small_moment = nesterov(outer_small, moment_small, grad_small)
    embed_outer, embed_moment = nesterov(outer_embed, moment_embed, grad_embed)
    spread = lax.all_to_all(
        expert_outer.astype(jnp.bfloat16), "mdl", split_axis=2, concat_axis=1, tiled=True
    )

    pieces = [
        spread,
        dense_outer.astype(jnp.bfloat16),
        small_outer.astype(jnp.bfloat16),
        embed_outer.astype(jnp.bfloat16),
    ]
    flat = jnp.concatenate([p.reshape(-1) for p in pieces])
    gathered = lax.all_gather(flat, "rep", axis=0, tiled=False)
    outs = []
    start = 0
    for p in pieces:
        n = p.size
        g = gathered[:, start : start + n].reshape((groups,) + p.shape)
        start += n
        if p.ndim == 3:
            g = g.transpose(1, 0, 2, 3).reshape(p.shape[0], groups * p.shape[1], p.shape[2])
        else:
            g = g.transpose(1, 0, 2).reshape(p.shape[0], groups * p.shape[1])
        outs.append(g)

    return (
        expert_outer[None],
        expert_moment[None],
        outs[0][None],
        dense_outer,
        dense_moment,
        outs[1],
        small_outer,
        small_moment,
        outs[2],
        embed_outer,
        embed_moment,
        outs[3],
    )


def solution(mesh):
    placed = (
        P("rep", "exp", None, None, "mdl"),
        P("rep", ("exp", "mdl"), None),
        P("rep", None, None),
        P("rep", ("exp", "mdl"), None),
        P("exp", None, ("rep", "mdl"), None),
        P(("exp", "mdl"), "rep"),
        P(None, "rep"),
        P(("exp", "mdl"), "rep"),
        P("exp", None, ("rep", "mdl"), None),
        P(("exp", "mdl"), "rep"),
        P(None, "rep"),
        P(("exp", "mdl"), "rep"),
        P(),
    )
    return jax.shard_map(
        on_device,
        mesh=mesh,
        in_specs=placed,
        out_specs=(
            P("exp", None, ("rep", "mdl"), None),
            P("exp", None, ("rep", "mdl"), None),
            P("exp", None, None, "mdl"),
            P(("exp", "mdl"), "rep"),
            P(("exp", "mdl"), "rep"),
            P(("exp", "mdl"), None),
            P(None, "rep"),
            P(None, "rep"),
            P(),
            P(("exp", "mdl"), "rep"),
            P(("exp", "mdl"), "rep"),
            P(("exp", "mdl"), None),
        ),
        check_vma=False,
    )
```

time: 203 us -> 194 us (0.956)
  the two profiles are of different devices: /device:TPU:104 before, /device:TPU:4 now
where the time goes in v1:
time: 194 us
  blocking collectives  138 us (71%)
  local copies, waits for them, and re-layouts  20.8 us (11%)
  waiting for transfers between devices  16.3 us (8%)
  other arithmetic  7.41 us (4%)
  starting transfers between devices  7.16 us (4%)
  matrix products  3.17 us (2%)
    all_gather x1, blocking collectives, on_device(): gathered = lax.all_gather(flat, 'rep', axis=0, tiled=False)  70.5 us
    all_to_all x1, blocking collectives, on_device(): recv = lax.all_to_all(send, 'rep', split_axis=0, concat_axis=0, tiled=True)  67.2 us
    unnamed x34, local copies, waits for them, and re-layouts  10.8 us
    all_to_all x1, waiting for transfers between devices, on_device(): lax.all_to_all(ex_sum, 'mdl', split_axis=1, concat_axis=2, tiled=True)  10.2 us
    all_to_all x1, waiting for transfers between devices, on_device(): lax.all_to_all(expert_outer.astype(jnp.bfloat16), 'mdl', split_axis=2, co...  6.13 us
  transfers between devices with their start and end apart: 2, of which 2 were waited for; matrix products, arithmetic and copies ran while one was open for 2% of the time, Pallas kernels for 0%

profile of v1, /device:TPU:4, one launch (start us, length us, event | category | flops | bytes accessed | tf_op | source)
XLA Modules:
  0.0 193.7 jit_solution(14872040050201057963)
XLA Ops:
  0.7 0.9 copy-done
  1.6 1.1 convolution_bitcast_fusion
  2.7 1.1 subtract_convert_fusion
  4.2 1.2 copy.62
  5.4 0.6 copy.83
  6.7 0.6 maximum_bitcast_fusion
  7.3 0.5 broadcast.73
  7.8 2.0 %reduce = bf16[4,123776]{1,0:T(4,128)(2,1)S(1)} reduce(bf16[4,1,123776]{2,0,1:T(4,128)(2,1)S(1)} %maximum_bitcast_fusion, bf16[]{:T(256)} %broadcast.73), dimensions={1}, to_apply=%copy.68.reduce_sub_computation | reduce | bytes 1980418 | tf_op jit(solution)/shard_map/all_to_all | solution.py:68
  9.8 1.1 reshape.132
  10.8 67.2 %all_to_all.36 = bf16[4,2,61888]{2,1,0:T(2,128)(2,1)S(1)} all-to-all(bf16[4,2,61888]{2,1,0:T(2,128)(2,1)S(1)} %reshape.132), channel_id=1, replica_groups=mesh['rep'=4,'exp'=16,'mdl'=8] {'rep'}, dimensions={0} | all-to-all | bytes 1980416 | tf_op jit(solution)/shard_map/all_to_all | solution.py:68
  78.0 3.1 %reshape.133 = bf16[4,1,123776]{2,1,0:T(2,128)(2,1)S(1)} reshape(bf16[4,2,61888]{2,1,0:T(2,128)(2,1)S(1)} %all_to_all.36) | data formatting | bytes 1980416
  81.6 1.1 convert_reduce_fusion
  83.0 1.1 copy.69
  84.1 3.6 %all-to-all-start.1 = ((f32[2,192,256]{2,0,1:T(2,128)}), f32[2,192,256]{2,0,1:T(2,128)S(1)}, u32[]{:S(2)}, u32[]{:S(2)}) async-start(f32[2,192,256]{2,0,1:T(2,128)} %copy.69), calls=%async_computation.1 | async-start | bytes 786432 | tf_op jit(solution)/shard_map/all_to_all | solution.py:83
  87.7 0.9 fusion.15
  89.0 0.7 fusion.13
  89.9 10.2 %all-to-all-done.1 = f32[2,192,256]{2,0,1:T(2,128)S(1)} async-done(((f32[2,192,256]{2,0,1:T(2,128)}), f32[2,192,256]{2,0,1:T(2,128)S(1)}, u32[]{:S(2)}, u32[]{:S(2)}) %all-to-all-start.1) | async-done | bytes 393248 | tf_op jit(solution)/shard_map/all_to_all | solution.py:83
  100.2 1.1 fusion.5
  101.3 0.7 copy.73
  102.1 2.0 %reshape.134 = bf16[8,2,6144]{2,1,0:T(2,128)(2,1)} reshape(bf16[2048,2,24]{2,1,0:T(2,128)(2,1)S(1)} %bitcast.68) | data formatting | bytes 393216
  104.1 3.6 %all-to-all-start.2 = ((bf16[8,2,6144]{2,1,0:T(2,128)(2,1)}), bf16[8,2,6144]{2,1,0:T(2,128)(2,1)S(1)}, u32[]{:S(2)}, u32[]{:S(2)}) async-start(bf16[8,2,6144]{2,1,0:T(2,128)(2,1)} %reshape.134), calls=%async_computation.2 | async-start | bytes 393216 | tf_op jit(solution)/shard_map/all_to_all | solution.py:94
  107.7 0.6 fusion.14
  108.6 1.0 multiply_subtract_fusion
  109.6 6.1 %all-to-all-done.2 = bf16[8,2,6144]{2,1,0:T(2,128)(2,1)S(1)} async-done(((bf16[8,2,6144]{2,1,0:T(2,128)(2,1)}), bf16[8,2,6144]{2,1,0:T(2,128)(2,1)S(1)}, u32[]{:S(2)}, u32[]{:S(2)}) %all-to-all-start.2) | async-done | bytes 196640 | tf_op jit(solution)/shard_map/all_to_all | solution.py:94
  115.7 1.5 reshape.135
  117.2 0.6 copy.74
  118.3 70.5 %all-gather.1 = bf16[4,1,127872]{2,1,0:T(2,128)(2,1)S(1)} all-gather(bf16[1,1,127872]{2,1,0:T(2,128)(2,1)S(1)} %reshape.128), channel_id=2, replica_groups=mesh['rep'=4,'exp'=16,'mdl'=8] {'rep'}, dimensions={0}, use_global_device_ids=true | all-gather | bytes 1278720 | tf_op jit(solution)/shard_map/all_gather | solution.py:105
  188.9 0.5 copy.91
  189.9 0.9 copy.75
  191.0 0.8 reshape.122
  192.1 0.8 reshape.126
  193.0 0.7 reshape.124
  (66 shorter events, 4.1 us)
Async XLA Ops:
  0.6 0.9 copy-start
  0.7 5.4 %copy-start.5 = (bf16[1,72,768]{2,1,0:T(8,128)(2,1)S(1)}, bf16[1,72,768]{2,1,0:T(8,128)(2,1)}, u32[]{:S(2)}) copy-start(bf16[1,72,768]{2,1,0:T(8,128)(2,1)} %param.14) | copy-start | bytes 331780
  4.2 2.2 %copy-start.9 = (bf16[1,18,768]{2,1,0:T(8,128)(2,1)S(1)}, bf16[1,18,768]{2,1,0:T(8,128)(2,1)}, u32[]{:S(2)}) copy-start(bf16[1,18,768]{2,1,0:T(8,128)(2,1)} %param.15) | copy-start | bytes 82948
  81.6 6.1 %copy-start.4 = (f32[64,192]{1,0:T(8,128)S(1)}, f32[64,192]{1,0:T(8,128)}, u32[]{:S(2)}) copy-start(f32[64,192]{1,0:T(8,128)} %param.20) | copy-start | bytes 147460
  81.6 6.1 %copy-start.8 = (f32[64,192]{1,0:T(8,128)S(1)}, f32[64,192]{1,0:T(8,128)}, u32[]{:S(2)}) copy-start(f32[64,192]{1,0:T(8,128)} %param.24) | copy-start | bytes 147460
  82.8 6.2 %copy-start.6 = (f32[72,192]{1,0:T(8,128)S(1)}, f32[72,192]{1,0:T(8,128)}, u32[]{:S(2)}) copy-start(f32[72,192]{1,0:T(8,128)} %param.18) | copy-start | bytes 165892
  82.8 6.2 %copy-start.7 = (f32[72,192]{1,0:T(8,128)S(1)}, f32[72,192]{1,0:T(8,128)}, u32[]{:S(2)}) copy-start(f32[72,192]{1,0:T(8,128)} %param.22) | copy-start | bytes 165892
  84.1 16.1 %copy-start.1 = (f32[1,2,24,2048]{3,2,1,0:T(8,128)S(1)}, f32[1,2,24,2048]{3,2,1,0:T(8,128)}, u32[]{:S(2)}) copy-start(f32[1,2,24,2048]{3,2,1,0:T(8,128)} %param.17) | copy-start | bytes 1179652
  84.1 16.0 %all-to-all-start.1 = ((f32[2,192,256]{2,0,1:T(2,128)}), f32[2,192,256]{2,0,1:T(2,128)S(1)}, u32[]{:S(2)}, u32[]{:S(2)}) async-start(f32[2,192,256]{2,0,1:T(2,128)} %copy.69), calls=%async_computation.1 | async-start | bytes 786432 | tf_op jit(solution)/shard_map/all_to_all | solution.py:83
  100.2 7.5 %copy-start.10 = (f32[18,192]{1,0:T(8,128)S(1)}, f32[18,192]{1,0:T(8,128)}, u32[]{:S(2)}) copy-start(f32[18,192]{1,0:T(8,128)} %param.19) | copy-start | bytes 41476
  100.2 7.5 %copy-start.11 = (f32[18,192]{1,0:T(8,128)S(1)}, f32[18,192]{1,0:T(8,128)}, u32[]{:S(2)}) copy-start(f32[18,192]{1,0:T(8,128)} %param.23) | copy-start | bytes 41476
  102.1 6.6 %copy-start.2 = (f32[1,2,24,2048]{3,2,1,0:T(8,128)S(1)}, f32[1,2,24,2048]{3,2,1,0:T(8,128)}, u32[]{:S(2)}) copy-start(f32[1,2,24,2048]{3,2,1,0:T(8,128)} %param.17) | copy-start | bytes 1179652
  102.1 6.5 %copy-start.3 = (f32[1,2,24,2048]{3,2,1,0:T(8,128)S(1)}, f32[1,2,24,2048]{3,2,1,0:T(8,128)}, u32[]{:S(2)}) copy-start(f32[1,2,24,2048]{3,2,1,0:T(8,128)} %param.21) | copy-start | bytes 1179652
  104.1 11.6 %all-to-all-start.2 = ((bf16[8,2,6144]{2,1,0:T(2,128)(2,1)}), bf16[8,2,6144]{2,1,0:T(2,128)(2,1)S(1)}, u32[]{:S(2)}, u32[]{:S(2)}) async-start(bf16[8,2,6144]{2,1,0:T(2,128)(2,1)} %reshape.134), calls=%async_computation.2 | async-start | bytes 393216 | tf_op jit(solution)/shard_map/all_to_all | solution.py:94

commit v2 on v1

--- a/solution.py
+++ b/solution.py
@@ -16,6 +16,44 @@
 def split_rows(x, parts):
     rows, cols = x.shape
     return x.reshape(rows, parts, cols // parts).transpose(1, 0, 2).reshape(parts, -1)
+
+
+def to_next(x, groups):
+    return lax.ppermute(x, "rep", [(i, (i + 1) % groups) for i in range(groups)])
+
+
+def to_prev(x, groups):
+    return lax.ppermute(x, "rep", [(i, (i - 1) % groups) for i in range(groups)])
+
+
+def rep_exchange(send, groups):
+    assert groups == 4
+    me = lax.axis_index("rep")
+    rel = [lax.dynamic_index_in_dim(send, (me + d) % groups, 0, False) for d in range(groups)]
+    k = send.shape[1]
+    half = k // 2
+    fwd = to_next(jnp.concatenate([rel[1], rel[2][:half]]), groups)
+    bwd = to_prev(jnp.concatenate([rel[3], rel[2][half:]]), groups)
+    far_a = to_next(fwd[k:], groups)
+    far_b = to_prev(bwd[k:], groups)
+    far = jnp.concatenate([far_a, far_b])
+    return jnp.stack([rel[0], fwd[:k], bwd[:k], far])
+
+
+def rep_gather(flat, groups):
+    assert groups == 4
+    me = lax.axis_index("rep")
+    n = flat.shape[0]
+    half = n // 2
+    from_prev = to_next(flat, groups)
+    from_next = to_prev(flat, groups)
+    far_a = to_next(from_prev[:half], groups)
+    far_b = to_prev(from_next[half:], groups)
+    far = jnp.concatenate([far_a, far_b])
+    out = jnp.zeros((groups, n), flat.dtype)
+    for d, row in enumerate([flat, from_next, far, from_prev]):
+        out = lax.dynamic_update_index_in_dim(out, row, (me + d) % groups, 0)
+    return out
 
 
 def on_device(
@@ -65,7 +103,7 @@
 
     sizes = [ex_send.shape[1], de_send.shape[1], sm_send.shape[1], pp.shape[0]]
     send = jnp.concatenate([ex_send, de_send, sm_send, pp_send], axis=1)
-    recv = lax.all_to_all(send, "rep", split_axis=0, concat_axis=0, tiled=True)
+    recv = rep_exchange(send, groups)
     bounds = [0]
     for s in sizes:
         bounds.append(bounds[-1] + s)
@@ -102,7 +140,7 @@
         embed_outer.astype(jnp.bfloat16),
     ]
     flat = jnp.concatenate([p.reshape(-1) for p in pieces])
-    gathered = lax.all_gather(flat, "rep", axis=0, tiled=False)
+    gathered = rep_gather(flat, groups)
     outs = []
     start = 0
     for p in pieces:

time: 194 us -> 197 us (1.015)
  the two profiles are of different devices: /device:TPU:4 before, /device:TPU:1 now
where the time goes in v2:
time: 197 us; the launch traced here: 196 us
  starting transfers between devices  73.8 us (37%)
  waiting for transfers between devices  54.6 us (28%)
  local copies, waits for them, and re-layouts  54 us (27%)
  other arithmetic  9.23 us (5%)
  matrix products  3.17 us (2%)
    ppermute x4, starting transfers between devices, to_next(): lax.ppermute(x, 'rep', [(i, (i + 1) % groups) for i in range(groups)])  41.8 us
    ppermute x4, waiting for transfers between devices, to_next(): lax.ppermute(x, 'rep', [(i, (i + 1) % groups) for i in range(groups)])  32.1 us
    dynamic_update_slice x4, local copies, waits for them, and re-layouts, rep_gather(): out = lax.dynamic_update_index_in_dim(out, row, (me + d) % groups, 0)  28.4 us
    ppermute x4, starting transfers between devices, to_prev(): lax.ppermute(x, 'rep', [(i, (i - 1) % groups) for i in range(groups)])  19.9 us
    ppermute x4, waiting for transfers between devices, to_prev(): lax.ppermute(x, 'rep', [(i, (i - 1) % groups) for i in range(groups)])  9.38 us
    all_to_all x1, waiting for transfers between devices, on_device(): lax.all_to_all(ex_sum, 'mdl', split_axis=1, concat_axis=2, tiled=True)  8.43 us
    all_to_all x1, starting transfers between devices, on_device(): lax.all_to_all(ex_sum, 'mdl', split_axis=1, concat_axis=2, tiled=True)  7.61 us
    unnamed x38, local copies, waits for them, and re-layouts  7.5 us
  transfers between devices with their start and end apart: 10, of which 8 were waited for; matrix products, arithmetic and copies ran while one was open for 11% of the time, Pallas kernels for 0%

profile of v2, /device:TPU:1, one launch (start us, length us, event | category | flops | bytes accessed | tf_op | source)
XLA Modules:
  0.0 196.2 jit_solution(11644947169087100469)
XLA Ops:
  1.6 1.1 convolution_bitcast_fusion
  2.7 1.1 subtract_convert_fusion
  4.2 1.2 copy.61
  7.6 1.6 dynamic-slice_reduce_fusion.3
  9.2 3.5 %dynamic-slice_reduce_fusion.1 = (bf16[123776]{0:T(1024)(128)(2,1)S(1)}, bf16[123776]{0:T(1024)(128)(2,1)S(1)}, bf16[1,123776]{1,0:T(2,128)(2,1)S(1)}) fusion(bf16[4,123776]{1,0:T(4,128)(2,1)S(1)} %maximum_maximum_fusion, s32[]{:T(128)S(6)} %select_n.52, s32[]{:T(128)S(6)} %select_n.56, s32[]{:T(128)S(6)} %select_n.50), kind=kLoop, calls=%fused_computation.7 | loop fusion | bytes 1485324 | tf_op jit(solution)/shard_map/jit(dynamic_index_in_dim)/dynamic_slice | solution.py:32
  12.8 9.6 %collective-permute-start = (bf16[185664]{0:T(1024)(128)(2,1)S(1)}, bf16[185664]{0:T(1024)(128)(2,1)S(1)}, u32[]{:S(2)}, u32[]{:S(2)}) collective-permute-start(bf16[185664]{0:T(1024)(128)(2,1)S(1)} %pad_maximum_fusion.1), channel_id=1, source_target_pairs={{0,128},{128,256},{256,384},{384,0},{1,129},{129,257},{257,385},{3... | collective-permute-start | bytes 1113992 | tf_op jit(solution)/shard_map/ppermute | solution.py:22
  22.5 5.6 %collective-permute-start.1 = (bf16[185664]{0:T(1024)(128)(2,1)S(1)}, bf16[185664]{0:T(1024)(128)(2,1)S(1)}, u32[]{:S(2)}, u32[]{:S(2)}) collective-permute-start(bf16[185664]{0:T(1024)(128)(2,1)S(1)} %pad_maximum_fusion.2), channel_id=1, source_target_pairs={{0,384},{128,0},{256,128},{384,256},{1,385},{129,1},{257,129},{385... | collective-permute-start | bytes 1113992 | tf_op jit(solution)/shard_map/ppermute | solution.py:26
  28.1 10.7 %collective-permute-done = bf16[185664]{0:T(1024)(128)(2,1)S(1)} collective-permute-done((bf16[185664]{0:T(1024)(128)(2,1)S(1)}, bf16[185664]{0:T(1024)(128)(2,1)S(1)}, u32[]{:S(2)}, u32[]{:S(2)}) %collective-permute-start) | collective-permute-done | bytes 371360 | tf_op jit(solution)/shard_map/ppermute | solution.py:22
  38.8 24.0 %collective-permute-start.2 = (bf16[61888]{0:T(1024)(128)(2,1)S(1)}, bf16[61888]{0:T(1024)(128)(2,1)S(1)}, u32[]{:S(2)}, u32[]{:S(2)}) collective-permute-start(bf16[61888]{0:T(1024)(128)(2,1)S(1)} %slice.82), channel_id=1, source_target_pairs={{0,128},{128,256},{256,384},{384,0},{1,129},{129,257},{257,385},{3... | collective-permute-start | bytes 371336 | tf_op jit(solution)/shard_map/ppermute | solution.py:22
  62.9 1.2 collective-permute-done.1
  64.1 4.2 %collective-permute-start.3 = (bf16[61888]{0:T(1024)(128)(2,1)S(1)}, bf16[61888]{0:T(1024)(128)(2,1)S(1)}, u32[]{:S(2)}, u32[]{:S(2)}) collective-permute-start(bf16[61888]{0:T(1024)(128)(2,1)S(1)} %slice.83), channel_id=1, source_target_pairs={{0,384},{128,0},{256,128},{384,256},{1,385},{129,1},{257,129},{385... | collective-permute-start | bytes 371336 | tf_op jit(solution)/shard_map/ppermute | solution.py:26
  68.9 4.8 %collective-permute-done.2 = bf16[61888]{0:T(1024)(128)(2,1)S(1)} collective-permute-done((bf16[61888]{0:T(1024)(128)(2,1)S(1)}, bf16[61888]{0:T(1024)(128)(2,1)S(1)}, u32[]{:S(2)}, u32[]{:S(2)}) %collective-permute-start.2) | collective-permute-done | bytes 123808 | tf_op jit(solution)/shard_map/ppermute | solution.py:22
  73.7 3.8 %collective-permute-done.3 = bf16[61888]{0:T(1024)(128)(2,1)S(1)} collective-permute-done((bf16[61888]{0:T(1024)(128)(2,1)S(1)}, bf16[61888]{0:T(1024)(128)(2,1)S(1)}, u32[]{:S(2)}, u32[]{:S(2)}) %collective-permute-start.3) | collective-permute-done | bytes 123808 | tf_op jit(solution)/shard_map/ppermute | solution.py:26
  78.0 2.3 %pad_maximum_fusion = bf16[4,123776]{1,0:T(4,128)(2,1)S(1)} fusion(bf16[1,123776]{1,0:T(2,128)(2,1)S(1)} %stack.15, bf16[1,123776]{1,0:T(2,128)(2,1)S(1)} %stack.14, bf16[1,123776]{1,0:T(2,128)(2,1)S(1)} %stack.13, bf16[1,123776]{1,0:T(2,128)(2,1)S(1)} %get-tuple-element.29), kind=kLoop, calls=%fused_computation.5 | loop fusion | flops 3960832 | bytes 1980416 | tf_op jit(solution)/shard_map/stack | solution.py:40
  80.3 1.1 convert_reduce_fusion
  82.6 7.6 %all-to-all-start = ((f32[2,192,256]{2,0,1:T(2,128)}), f32[2,192,256]{2,0,1:T(2,128)S(1)}, u32[]{:S(2)}, u32[]{:S(2)}) async-start(f32[2,192,256]{2,0,1:T(2,128)} %copy.67), calls=%async_computation | async-start | bytes 786432 | tf_op jit(solution)/shard_map/all_to_all | solution.py:121
  90.7 1.4 fusion.14
  93.1 8.4 %all-to-all-done = f32[2,192,256]{2,0,1:T(2,128)S(1)} async-done(((f32[2,192,256]{2,0,1:T(2,128)}), f32[2,192,256]{2,0,1:T(2,128)S(1)}, u32[]{:S(2)}, u32[]{:S(2)}) %all-to-all-start) | async-done | bytes 393248 | tf_op jit(solution)/shard_map/all_to_all | solution.py:121
  103.2 2.0 %reshape.132 = bf16[8,2,6144]{2,1,0:T(2,128)(2,1)} reshape(bf16[2048,2,24]{2,1,0:T(2,128)(2,1)S(1)} %bitcast.60) | data formatting | bytes 393216
  105.2 4.5 %all-to-all-start.1 = ((bf16[8,2,6144]{2,1,0:T(2,128)(2,1)}), bf16[8,2,6144]{2,1,0:T(2,128)(2,1)S(1)}, u32[]{:S(2)}, u32[]{:S(2)}) async-start(bf16[8,2,6144]{2,1,0:T(2,128)(2,1)} %reshape.132), calls=%async_computation.1 | async-start | bytes 393216 | tf_op jit(solution)/shard_map/all_to_all | solution.py:132
  111.6 4.7 %all-to-all-done.1 = bf16[8,2,6144]{2,1,0:T(2,128)(2,1)S(1)} async-done(((bf16[8,2,6144]{2,1,0:T(2,128)(2,1)}), bf16[8,2,6144]{2,1,0:T(2,128)(2,1)S(1)}, u32[]{:S(2)}, u32[]{:S(2)}) %all-to-all-start.1) | async-done | bytes 196640 | tf_op jit(solution)/shard_map/all_to_all | solution.py:132
  116.2 1.5 reshape.133
  119.9 4.4 %collective-permute-start.5 = (bf16[127872]{0:T(1024)(128)(2,1)S(1)}, bf16[127872]{0:T(1024)(128)(2,1)S(1)}, u32[]{:S(2)}, u32[]{:S(2)}) collective-permute-start(bf16[127872]{0:T(1024)(128)(2,1)S(1)} %dynamic-update-slice.3), channel_id=1, source_target_pairs={{0,128},{128,256},{256,384},{384,0},{1,129},{129,257},{257,385},{3... | collective-permute-start | bytes 767240 | tf_op jit(solution)/shard_map/ppermute | solution.py:22
  124.3 4.9 %collective-permute-start.4 = (bf16[127872]{0:T(1024)(128)(2,1)S(1)}, bf16[127872]{0:T(1024)(128)(2,1)S(1)}, u32[]{:S(2)}, u32[]{:S(2)}) collective-permute-start(bf16[127872]{0:T(1024)(128)(2,1)S(1)} %dynamic-update-slice.3), channel_id=1, source_target_pairs={{0,384},{128,0},{256,128},{384,256},{1,385},{129,1},{257,129},{385... | collective-permute-start | bytes 767240 | tf_op jit(solution)/shard_map/ppermute | solution.py:26
  129.4 16.6 %collective-permute-done.5 = bf16[127872]{0:T(1024)(128)(2,1)S(1)} collective-permute-done((bf16[127872]{0:T(1024)(128)(2,1)S(1)}, bf16[127872]{0:T(1024)(128)(2,1)S(1)}, u32[]{:S(2)}, u32[]{:S(2)}) %collective-permute-start.5) | collective-permute-done | bytes 255776 | tf_op jit(solution)/shard_map/ppermute | solution.py:22
  146.0 3.7 %collective-permute-start.6 = (bf16[63936]{0:T(1024)(128)(2,1)S(1)}, bf16[63936]{0:T(1024)(128)(2,1)S(1)}, u32[]{:S(2)}, u32[]{:S(2)}) collective-permute-start(bf16[63936]{0:T(1024)(128)(2,1)S(1)} %slice.87), channel_id=1, source_target_pairs={{0,128},{128,256},{256,384},{384,0},{1,129},{129,257},{257,385},{3... | collective-permute-start | bytes 383624 | tf_op jit(solution)/shard_map/ppermute | solution.py:22
  149.7 4.4 %collective-permute-done.4 = bf16[127872]{0:T(1024)(128)(2,1)S(1)} collective-permute-done((bf16[127872]{0:T(1024)(128)(2,1)S(1)}, bf16[127872]{0:T(1024)(128)(2,1)S(1)}, u32[]{:S(2)}, u32[]{:S(2)}) %collective-permute-start.4) | collective-permute-done | bytes 255776 | tf_op jit(solution)/shard_map/ppermute | solution.py:26
  154.9 5.2 %collective-permute-start.7 = (bf16[63936]{0:T(1024)(128)(2,1)}, bf16[63936]{0:T(1024)(128)(2,1)}, u32[]{:S(2)}, u32[]{:S(2)}) collective-permute-start(bf16[63936]{0:T(1024)(128)(2,1)} %slice.88), channel_id=1, source_target_pairs={{0,384},{128,0},{256,128},{384,256},{1,385},{129,1},{257,129},{385... | collective-permute-start | bytes 383624 | tf_op jit(solution)/shard_map/ppermute | solution.py:26
  161.6 7.1 %dynamic_update_slice.13 = bf16[4,127872]{1,0:T(4,128)(2,1)S(1)} dynamic-update-slice(bf16[4,127872]{1,0:T(4,128)(2,1)S(1)} %broadcast_in_dim.25, bf16[1,127872]{1,0:T(2,128)(2,1)S(1)} %broadcast_in_dim.26, s32[]{:T(128)S(6)} %select_n.50, s32[]{:T(128)} %constant.81.clone.1) | dynamic-update-slice | bytes 511492 | tf_op jit(solution)/shard_map/jit(dynamic_update_index_in_dim)/dynamic_update_slice | solution.py:55
  169.0 7.1 %dynamic_update_slice.14 = bf16[4,127872]{1,0:T(4,128)(2,1)S(1)} dynamic-update-slice(bf16[4,127872]{1,0:T(4,128)(2,1)S(1)} %dynamic_update_slice.13, bf16[1,127872]{1,0:T(2,128)(2,1)S(1)} %broadcast_in_dim.27, s32[]{:T(128)S(6)} %select_n.52, s32[]{:T(128)} %constant.81.clone.1) | dynamic-update-slice | bytes 511492 | tf_op jit(solution)/shard_map/jit(dynamic_update_index_in_dim)/dynamic_update_slice | solution.py:55
  177.7 7.1 %dynamic_update_slice.15 = bf16[4,127872]{1,0:T(4,128)(2,1)S(1)} dynamic-update-slice(bf16[4,127872]{1,0:T(4,128)(2,1)S(1)} %dynamic_update_slice.14, bf16[1,127872]{1,0:T(2,128)(2,1)S(1)} %broadcast_in_dim.28, s32[]{:T(128)S(6)} %select_n.54, s32[]{:T(128)} %constant.81.clone.1) | dynamic-update-slice | bytes 511492 | tf_op jit(solution)/shard_map/jit(dynamic_update_index_in_dim)/dynamic_update_slice | solution.py:55
  184.8 7.1 %dynamic_update_slice.16 = bf16[4,127872]{1,0:T(4,128)(2,1)S(1)} dynamic-update-slice(bf16[4,127872]{1,0:T(4,128)(2,1)S(1)} %dynamic_update_slice.15, bf16[1,127872]{1,0:T(2,128)(2,1)S(1)} %broadcast_in_dim.29, s32[]{:T(128)S(6)} %select_n.56, s32[]{:T(128)} %constant.81.clone.1) | dynamic-update-slice | bytes 511492 | tf_op jit(solution)/shard_map/jit(dynamic_update_index_in_dim)/dynamic_update_slice | solution.py:55
  (107 shorter events, 21.1 us)
Async XLA Ops:
  0.6 0.9 copy-start
  5.4 0.9 copy-start.9
  5.4 1.3 copy-start.14
  12.8 26.0 %collective-permute-start = (bf16[185664]{0:T(1024)(128)(2,1)S(1)}, bf16[185664]{0:T(1024)(128)(2,1)S(1)}, u32[]{:S(2)}, u32[]{:S(2)}) collective-permute-start(bf16[185664]{0:T(1024)(128)(2,1)S(1)} %pad_maximum_fusion.1), channel_id=1, source_target_pairs={{0,128},{128,256},{256,384},{384,0},{1,129},{129,257},{257,385},{3... | collective-permute-start | bytes 1113992 | tf_op jit(solution)/shard_map/ppermute | solution.py:22
  22.5 41.5 %collective-permute-start.1 = (bf16[185664]{0:T(1024)(128)(2,1)S(1)}, bf16[185664]{0:T(1024)(128)(2,1)S(1)}, u32[]{:S(2)}, u32[]{:S(2)}) collective-permute-start(bf16[185664]{0:T(1024)(128)(2,1)S(1)} %pad_maximum_fusion.2), channel_id=1, source_target_pairs={{0,384},{128,0},{256,128},{384,256},{1,385},{129,1},{257,129},{385... | collective-permute-start | bytes 1113992 | tf_op jit(solution)/shard_map/ppermute | solution.py:26
  38.8 34.9 %collective-permute-start.2 = (bf16[61888]{0:T(1024)(128)(2,1)S(1)}, bf16[61888]{0:T(1024)(128)(2,1)S(1)}, u32[]{:S(2)}, u32[]{:S(2)}) collective-permute-start(bf16[61888]{0:T(1024)(128)(2,1)S(1)} %slice.82), channel_id=1, source_target_pairs={{0,128},{128,256},{256,384},{384,0},{1,129},{129,257},{257,385},{3... | collective-permute-start | bytes 371336 | tf_op jit(solution)/shard_map/ppermute | solution.py:22
  64.1 13.5 %collective-permute-start.3 = (bf16[61888]{0:T(1024)(128)(2,1)S(1)}, bf16[61888]{0:T(1024)(128)(2,1)S(1)}, u32[]{:S(2)}, u32[]{:S(2)}) collective-permute-start(bf16[61888]{0:T(1024)(128)(2,1)S(1)} %slice.83), channel_id=1, source_target_pairs={{0,384},{128,0},{256,128},{384,256},{1,385},{129,1},{257,129},{385... | collective-permute-start | bytes 371336 | tf_op jit(solution)/shard_map/ppermute | solution.py:26
  82.6 18.9 %all-to-all-start = ((f32[2,192,256]{2,0,1:T(2,128)}), f32[2,192,256]{2,0,1:T(2,128)S(1)}, u32[]{:S(2)}, u32[]{:S(2)}) async-start(f32[2,192,256]{2,0,1:T(2,128)} %copy.67), calls=%async_computation | async-start | bytes 786432 | tf_op jit(solution)/shard_map/all_to_all | solution.py:121
  90.5 1.6 copy-start.7
  90.5 1.6 copy-start.12
  90.7 11.7 %copy-start.3 = (f32[1,2,24,2048]{3,2,1,0:T(8,128)S(1)}, f32[1,2,24,2048]{3,2,1,0:T(8,128)}, u32[]{:S(2)}) copy-start(f32[1,2,24,2048]{3,2,1,0:T(8,128)} %param.17) | copy-start | bytes 1179652
  90.7 11.7 %copy-start.5 = (f32[1,2,24,2048]{3,2,1,0:T(8,128)S(1)}, f32[1,2,24,2048]{3,2,1,0:T(8,128)}, u32[]{:S(2)}) copy-start(f32[1,2,24,2048]{3,2,1,0:T(8,128)} %param.21) | copy-start | bytes 1179652
  101.5 0.7 copy-start.1
  105.2 11.0 %all-to-all-start.1 = ((bf16[8,2,6144]{2,1,0:T(2,128)(2,1)}), bf16[8,2,6144]{2,1,0:T(2,128)(2,1)S(1)}, u32[]{:S(2)}, u32[]{:S(2)}) async-start(bf16[8,2,6144]{2,1,0:T(2,128)(2,1)} %reshape.132), calls=%async_computation.1 | async-start | bytes 393216 | tf_op jit(solution)/shard_map/all_to_all | solution.py:132
  109.7 0.8 copy-start.8
  109.7 0.9 copy-start.13
  109.7 1.1 copy-start.10
  109.7 1.1 copy-start.11
  117.7 11.5 %copy-start.2 = (f32[2,192,256]{2,1,0:T(8,128)S(1)}, f32[2,192,256]{2,1,0:T(8,128)}, u32[]{:S(2)}) copy-start(f32[2,192,256]{2,1,0:T(8,128)} %copy-done.1) | copy-start | bytes 1179652
  119.9 40.2 %copy-start.4 = (f32[1,2,24,2048]{3,2,1,0:T(8,128)S(1)}, f32[1,2,24,2048]{3,2,1,0:T(8,128)}, u32[]{:S(2)}) copy-start(f32[1,2,24,2048]{3,2,1,0:T(8,128)} %param.17) | copy-start | bytes 1179652
  119.9 40.2 %copy-start.6 = (f32[1,2,24,2048]{3,2,1,0:T(8,128)S(1)}, f32[1,2,24,2048]{3,2,1,0:T(8,128)}, u32[]{:S(2)}) copy-start(f32[1,2,24,2048]{3,2,1,0:T(8,128)} %param.21) | copy-start | bytes 1179652
  119.9 26.1 %collective-permute-start.5 = (bf16[127872]{0:T(1024)(128)(2,1)S(1)}, bf16[127872]{0:T(1024)(128)(2,1)S(1)}, u32[]{:S(2)}, u32[]{:S(2)}) collective-permute-start(bf16[127872]{0:T(1024)(128)(2,1)S(1)} %dynamic-update-slice.3), channel_id=1, source_target_pairs={{0,128},{128,256},{256,384},{384,0},{1,129},{129,257},{257,385},{3... | collective-permute-start | bytes 767240 | tf_op jit(solution)/shard_map/ppermute | solution.py:22
  124.3 29.7 %collective-permute-start.4 = (bf16[127872]{0:T(1024)(128)(2,1)S(1)}, bf16[127872]{0:T(1024)(128)(2,1)S(1)}, u32[]{:S(2)}, u32[]{:S(2)}) collective-permute-start(bf16[127872]{0:T(1024)(128)(2,1)S(1)} %dynamic-update-slice.3), channel_id=1, source_target_pairs={{0,384},{128,0},{256,128},{384,256},{1,385},{129,1},{257,129},{385... | collective-permute-start | bytes 767240 | tf_op jit(solution)/shard_map/ppermute | solution.py:26
  146.0 30.4 %collective-permute-start.6 = (bf16[63936]{0:T(1024)(128)(2,1)S(1)}, bf16[63936]{0:T(1024)(128)(2,1)S(1)}, u32[]{:S(2)}, u32[]{:S(2)}) collective-permute-start(bf16[63936]{0:T(1024)(128)(2,1)S(1)} %slice.87), channel_id=1, source_target_pairs={{0,128},{128,256},{256,384},{384,0},{1,129},{129,257},{257,385},{3... | collective-permute-start | bytes 383624 | tf_op jit(solution)/shard_map/ppermute | solution.py:22
  154.9 21.5 %collective-permute-start.7 = (bf16[63936]{0:T(1024)(128)(2,1)}, bf16[63936]{0:T(1024)(128)(2,1)}, u32[]{:S(2)}, u32[]{:S(2)}) collective-permute-start(bf16[63936]{0:T(1024)(128)(2,1)} %slice.88), channel_id=1, source_target_pairs={{0,384},{128,0},{256,128},{384,256},{1,385},{129,1},{257,129},{385... | collective-permute-start | bytes 383624 | tf_op jit(solution)/shard_map/ppermute | solution.py:26

commit v3 on v2

--- a/solution.py
+++ b/solution.py
@@ -36,8 +36,9 @@
     bwd = to_prev(jnp.concatenate([rel[3], rel[2][half:]]), groups)
     far_a = to_next(fwd[k:], groups)
     far_b = to_prev(bwd[k:], groups)
-    far = jnp.concatenate([far_a, far_b])
-    return jnp.stack([rel[0], fwd[:k], bwd[:k], far])
+    f32 = jnp.float32
+    near = rel[0].astype(f32) + fwd[:k].astype(f32) + bwd[:k].astype(f32)
+    return near + jnp.concatenate([far_a, far_b]).astype(f32)
 
 
 def rep_gather(flat, groups):
@@ -50,10 +51,8 @@
     far_a = to_next(from_prev[:half], groups)
     far_b = to_prev(from_next[half:], groups)
     far = jnp.concatenate([far_a, far_b])
-    out = jnp.zeros((groups, n), flat.dtype)
-    for d, row in enumerate([flat, from_next, far, from_prev]):
-        out = lax.dynamic_update_index_in_dim(out, row, (me + d) % groups, 0)
-    return out
+    rel = jnp.stack([flat, from_next, far, from_prev])
+    return [lax.dynamic_index_in_dim(rel, (j - me) % groups, 0, False) for j in range(groups)]
 
 
 def on_device(
@@ -74,16 +73,17 @@
     groups = lax.axis_size("rep")
     hi_prec = lax.Precision.HIGHEST
 
+    lanes = 128
     own_shard = inner_experts[0, 0]
     halves, all_rows, my_cols = own_shard.shape
     rep_rows = all_rows // groups
     ex_send = (
         own_shard.reshape(halves, groups, rep_rows, my_cols)
         .transpose(1, 0, 2, 3)
-        .reshape(groups, -1)
-    )
-    de_send = split_rows(inner_dense[0], groups)
-    sm_send = split_rows(inner_small[0], groups)
+        .reshape(groups, -1, lanes)
+    )
+    de_send = split_rows(inner_dense[0], groups).reshape(groups, -1, lanes)
+    sm_send = split_rows(inner_small[0], groups).reshape(groups, -1, lanes)
 
     col_count = outer_embed.shape[1]
     offset = lax.axis_index("rep") * col_count
@@ -98,25 +98,22 @@
     ) / groups
     part_hi = partial_value.astype(jnp.bfloat16)
     part_lo = (partial_value - part_hi.astype(jnp.float32)).astype(jnp.bfloat16)
-    pp = jnp.concatenate([part_hi.reshape(-1), part_lo.reshape(-1)])
-    pp_send = jnp.broadcast_to(pp[None], (groups, pp.shape[0]))
+    pp = jnp.concatenate([part_hi.reshape(-1, lanes), part_lo.reshape(-1, lanes)])
+    pp_send = jnp.broadcast_to(pp[None], (groups,) + pp.shape)
 
     sizes = [ex_send.shape[1], de_send.shape[1], sm_send.shape[1], pp.shape[0]]
     send = jnp.concatenate([ex_send, de_send, sm_send, pp_send], axis=1)
-    recv = rep_exchange(send, groups)
+    total = rep_exchange(send, groups)
     bounds = [0]
     for s in sizes:
         bounds.append(bounds[-1] + s)
-    parts = [recv[:, bounds[i] : bounds[i + 1]] for i in range(4)]
-
-    ex_sum = jnp.sum(parts[0].astype(jnp.float32), axis=0).reshape(halves, rep_rows, my_cols)
-    dense_sum = jnp.sum(parts[1].astype(jnp.float32), axis=0).reshape(outer_dense.shape)
-    small_sum = jnp.sum(parts[2].astype(jnp.float32), axis=0).reshape(outer_small.shape)
-    pp_recv = parts[3].astype(jnp.float32)
-    nco = partial_value.size
-    coefficient = jnp.sum(pp_recv[:, :nco] + pp_recv[:, nco:], axis=0).reshape(
-        partial_value.shape
-    )
+    parts = [total[bounds[i] : bounds[i + 1]] for i in range(4)]
+
+    ex_sum = parts[0].reshape(halves, rep_rows, my_cols)
+    dense_sum = parts[1].reshape(outer_dense.shape)
+    small_sum = parts[2].reshape(outer_small.shape)
+    nhalf = parts[3].shape[0] // 2
+    coefficient = (parts[3][:nhalf] + parts[3][nhalf:]).reshape(partial_value.shape)
 
     expert_sum = lax.all_to_all(ex_sum, "mdl", split_axis=1, concat_axis=2, tiled=True)
     grad_experts = outer_experts[0] - expert_sum / groups
@@ -139,13 +136,13 @@
         small_outer.astype(jnp.bfloat16),
         embed_outer.astype(jnp.bfloat16),
     ]
-    flat = jnp.concatenate([p.reshape(-1) for p in pieces])
-    gathered = rep_gather(flat, groups)
+    flat = jnp.concatenate([p.reshape(-1, lanes) for p in pieces])
+    blocks = rep_gather(flat, groups)
     outs = []
     start = 0
     for p in pieces:
-        n = p.size
-        g = gathered[:, start : start + n].reshape((groups,) + p.shape)
+        n = p.size // lanes
+        g = jnp.stack([b[start : start + n] for b in blocks]).reshape((groups,) + p.shape)
         start += n
         if p.ndim == 3:
             g = g.transpose(1, 0, 2, 3).reshape(p.shape[0], groups * p.shape[1], p.shape[2])

time: 197 us -> 166 us (0.84)
  the two profiles are of different devices: /device:TPU:1 before, /device:TPU:62 now
where the time goes in v3:
time: 166 us
  waiting for transfers between devices  89.2 us (54%)
  starting transfers between devices  52.7 us (32%)
  local copies, waits for them, and re-layouts  16 us (10%)
  other arithmetic  3.24 us (2%)
  matrix products  3.16 us (2%)
    ppermute x4, waiting for transfers between devices, to_prev(): lax.ppermute(x, 'rep', [(i, (i - 1) % groups) for i in range(groups)])  38.9 us
    ppermute x4, waiting for transfers between devices, to_next(): lax.ppermute(x, 'rep', [(i, (i + 1) % groups) for i in range(groups)])  36.5 us
    ppermute x4, starting transfers between devices, to_prev(): lax.ppermute(x, 'rep', [(i, (i - 1) % groups) for i in range(groups)])  28.4 us
    ppermute x4, starting transfers between devices, to_next(): lax.ppermute(x, 'rep', [(i, (i + 1) % groups) for i in range(groups)])  15.2 us
    all_to_all x1, waiting for transfers between devices, on_device(): lax.all_to_all(ex_sum, 'mdl', split_axis=1, concat_axis=2, tiled=True)  9.11 us
    all_to_all x1, starting transfers between devices, on_device(): lax.all_to_all(expert_outer.astype(jnp.bfloat16), 'mdl', split_axis=2, co...  5.81 us
    unnamed x24, local copies, waits for them, and re-layouts  5.04 us
    all_to_all x1, waiting for transfers between devices, on_device(): lax.all_to_all(expert_outer.astype(jnp.bfloat16), 'mdl', split_axis=2, co...  4.68 us
  transfers between devices with their start and end apart: 10, of which 7 were waited for; matrix products, arithmetic and copies ran while one was open for 3% of the time, Pallas kernels for 0%

profile of v3, /device:TPU:62, one launch (start us, length us, event | category | flops | bytes accessed | tf_op | source)
XLA Modules:
  0.0 165.8 jit_solution(7133276187906420134)
XLA Ops:
  0.7 0.9 copy-done
  1.6 1.1 convolution_bitcast_fusion
  2.7 1.1 subtract_convert_fusion
  4.2 1.2 copy.65
  7.3 11.8 %collective-permute-start.1 = (bf16[1451,128]{1,0:T(8,128)(2,1)S(1)}, bf16[1451,128]{1,0:T(8,128)(2,1)S(1)}, u32[]{:S(2)}, u32[]{:S(2)}) collective-permute-start(bf16[1451,128]{1,0:T(8,128)(2,1)S(1)} %pad_maximum_fusion.3), channel_id=1, source_target_pairs={{0,384},{128,0},{256,128},{384,256},{1,385},{129,1},{257,129},{385... | collective-permute-start | bytes 1114376 | tf_op jit(solution)/shard_map/ppermute | solution.py:26
  19.2 1.9 %collective-permute-start = (bf16[1450,128]{1,0:T(8,128)(2,1)S(1)}, bf16[1450,128]{1,0:T(8,128)(2,1)S(1)}, u32[]{:S(2)}, u32[]{:S(2)}) collective-permute-start(bf16[1450,128]{1,0:T(8,128)(2,1)S(1)} %pad_maximum_fusion.2), channel_id=1, source_target_pairs={{0,128},{128,256},{256,384},{384,0},{1,129},{129,257},{257,385},{3... | collective-permute-start | bytes 1113608 | tf_op jit(solution)/shard_map/ppermute | solution.py:22
  21.1 29.8 %collective-permute-done.1 = bf16[1451,128]{1,0:T(8,128)(2,1)S(1)} collective-permute-done((bf16[1451,128]{1,0:T(8,128)(2,1)S(1)}, bf16[1451,128]{1,0:T(8,128)(2,1)S(1)}, u32[]{:S(2)}, u32[]{:S(2)}) %collective-permute-start.1) | collective-permute-done | bytes 371488 | tf_op jit(solution)/shard_map/ppermute | solution.py:26
  51.0 8.4 %collective-permute-start.3 = (bf16[484,128]{1,0:T(8,128)(2,1)S(1)}, bf16[484,128]{1,0:T(8,128)(2,1)S(1)}, u32[]{:S(2)}, u32[]{:S(2)}) collective-permute-start(bf16[484,128]{1,0:T(8,128)(2,1)S(1)} %slice.146), channel_id=1, source_target_pairs={{0,384},{128,0},{256,128},{384,256},{1,385},{129,1},{257,129},{385... | collective-permute-start | bytes 371720 | tf_op jit(solution)/shard_map/ppermute | solution.py:26
  59.4 1.9 %collective-permute-start.2 = (bf16[483,128]{1,0:T(8,128)(2,1)S(1)}, bf16[483,128]{1,0:T(8,128)(2,1)S(1)}, u32[]{:S(2)}, u32[]{:S(2)}) collective-permute-start(bf16[483,128]{1,0:T(8,128)(2,1)S(1)} %slice.145), channel_id=1, source_target_pairs={{0,128},{128,256},{256,384},{384,0},{1,129},{129,257},{257,385},{3... | collective-permute-start | bytes 370952 | tf_op jit(solution)/shard_map/ppermute | solution.py:22
  61.4 15.1 %collective-permute-done.2 = bf16[483,128]{1,0:T(8,128)(2,1)S(1)} collective-permute-done((bf16[483,128]{1,0:T(8,128)(2,1)S(1)}, bf16[483,128]{1,0:T(8,128)(2,1)S(1)}, u32[]{:S(2)}, u32[]{:S(2)}) %collective-permute-start.2) | collective-permute-done | bytes 123680 | tf_op jit(solution)/shard_map/ppermute | solution.py:22
  76.8 1.1 copy.71
  77.9 3.4 %all-to-all-start = ((f32[2,192,256]{2,0,1:T(2,128)}), f32[2,192,256]{2,0,1:T(2,128)S(1)}, u32[]{:S(2)}, u32[]{:S(2)}) async-start(f32[2,192,256]{2,0,1:T(2,128)} %copy.71), calls=%async_computation | async-start | bytes 786432 | tf_op jit(solution)/shard_map/all_to_all | solution.py:118
  81.4 0.7 fusion.14
  82.1 9.1 %all-to-all-done = f32[2,192,256]{2,0,1:T(2,128)S(1)} async-done(((f32[2,192,256]{2,0,1:T(2,128)}), f32[2,192,256]{2,0,1:T(2,128)S(1)}, u32[]{:S(2)}, u32[]{:S(2)}) %all-to-all-start) | async-done | bytes 393248 | tf_op jit(solution)/shard_map/all_to_all | solution.py:118
  91.4 0.7 copy.75
  92.2 2.0 %reshape.158 = bf16[8,2,6144]{2,1,0:T(2,128)(2,1)} reshape(bf16[2048,2,24]{2,1,0:T(2,128)(2,1)S(1)} %bitcast.77) | data formatting | bytes 393216
  94.2 5.8 %all-to-all-start.1 = ((bf16[8,2,6144]{2,1,0:T(2,128)(2,1)}), bf16[8,2,6144]{2,1,0:T(2,128)(2,1)S(1)}, u32[]{:S(2)}, u32[]{:S(2)}) async-start(bf16[8,2,6144]{2,1,0:T(2,128)(2,1)} %reshape.158), calls=%async_computation.1 | async-start | bytes 393216 | tf_op jit(solution)/shard_map/all_to_all | solution.py:129
  100.2 0.9 fusion.16
  102.1 4.7 %all-to-all-done.1 = bf16[8,2,6144]{2,1,0:T(2,128)(2,1)S(1)} async-done(((bf16[8,2,6144]{2,1,0:T(2,128)(2,1)}), bf16[8,2,6144]{2,1,0:T(2,128)(2,1)S(1)}, u32[]{:S(2)}, u32[]{:S(2)}) %all-to-all-start.1) | async-done | bytes 196640 | tf_op jit(solution)/shard_map/all_to_all | solution.py:129
  106.8 1.5 reshape.159
  109.0 5.4 %collective-permute-start.5 = (bf16[999,128]{1,0:T(8,128)(2,1)S(1)}, bf16[999,128]{1,0:T(8,128)(2,1)S(1)}, u32[]{:S(2)}, u32[]{:S(2)}) collective-permute-start(bf16[999,128]{1,0:T(8,128)(2,1)S(1)} %pad_maximum_fusion.4), channel_id=1, source_target_pairs={{0,128},{128,256},{256,384},{384,0},{1,129},{129,257},{257,385},{3... | collective-permute-start | bytes 767240 | tf_op jit(solution)/shard_map/ppermute | solution.py:22
  114.4 4.3 %collective-permute-start.4 = (bf16[999,128]{1,0:T(8,128)(2,1)S(1)}, bf16[999,128]{1,0:T(8,128)(2,1)S(1)}, u32[]{:S(2)}, u32[]{:S(2)}) collective-permute-start(bf16[999,128]{1,0:T(8,128)(2,1)S(1)} %pad_maximum_fusion.4), channel_id=1, source_target_pairs={{0,384},{128,0},{256,128},{384,256},{1,385},{129,1},{257,129},{385... | collective-permute-start | bytes 767240 | tf_op jit(solution)/shard_map/ppermute | solution.py:26
  119.1 19.6 %collective-permute-done.5 = bf16[999,128]{1,0:T(8,128)(2,1)S(1)} collective-permute-done((bf16[999,128]{1,0:T(8,128)(2,1)S(1)}, bf16[999,128]{1,0:T(8,128)(2,1)S(1)}, u32[]{:S(2)}, u32[]{:S(2)}) %collective-permute-start.5) | collective-permute-done | bytes 255776 | tf_op jit(solution)/shard_map/ppermute | solution.py:22
  138.7 5.9 %collective-permute-start.6 = (bf16[499,128]{1,0:T(8,128)(2,1)S(1)}, bf16[499,128]{1,0:T(8,128)(2,1)S(1)}, u32[]{:S(2)}, u32[]{:S(2)}) collective-permute-start(bf16[499,128]{1,0:T(8,128)(2,1)S(1)} %slice.152), channel_id=1, source_target_pairs={{0,128},{128,256},{256,384},{384,0},{1,129},{129,257},{257,385},{3... | collective-permute-start | bytes 383240 | tf_op jit(solution)/shard_map/ppermute | solution.py:22
  144.7 3.8 %collective-permute-start.7 = (bf16[500,128]{1,0:T(8,128)(2,1)S(1)}, bf16[500,128]{1,0:T(8,128)(2,1)S(1)}, u32[]{:S(2)}, u32[]{:S(2)}) collective-permute-start(bf16[500,128]{1,0:T(8,128)(2,1)S(1)} %slice.153), channel_id=1, source_target_pairs={{0,384},{128,0},{256,128},{384,256},{1,385},{129,1},{257,129},{385... | collective-permute-start | bytes 384008 | tf_op jit(solution)/shard_map/ppermute | solution.py:26
  148.5 1.0 multiply_subtract_fusion
  149.6 1.8 %collective-permute-done.6 = bf16[499,128]{1,0:T(8,128)(2,1)S(1)} collective-permute-done((bf16[499,128]{1,0:T(8,128)(2,1)S(1)}, bf16[499,128]{1,0:T(8,128)(2,1)S(1)}, u32[]{:S(2)}, u32[]{:S(2)}) %collective-permute-start.6) | collective-permute-done | bytes 127776 | tf_op jit(solution)/shard_map/ppermute | solution.py:22
  151.3 9.0 %collective-permute-done.7 = bf16[500,128]{1,0:T(8,128)(2,1)S(1)} collective-permute-done((bf16[500,128]{1,0:T(8,128)(2,1)S(1)}, bf16[500,128]{1,0:T(8,128)(2,1)S(1)}, u32[]{:S(2)}, u32[]{:S(2)}) %collective-permute-start.7) | collective-permute-done | bytes 128032 | tf_op jit(solution)/shard_map/ppermute | solution.py:26
  161.2 0.8 reshape.156
  162.4 0.7 reshape.155
  163.6 0.8 reshape.154
  164.8 0.9 copy.77
  (98 shorter events, 7.0 us)
Async XLA Ops:
  0.6 0.9 copy-start
  5.4 0.9 copy-start.4
  5.4 1.3 copy-start.8
  7.3 43.7 %collective-permute-start.1 = (bf16[1451,128]{1,0:T(8,128)(2,1)S(1)}, bf16[1451,128]{1,0:T(8,128)(2,1)S(1)}, u32[]{:S(2)}, u32[]{:S(2)}) collective-permute-start(bf16[1451,128]{1,0:T(8,128)(2,1)S(1)} %pad_maximum_fusion.3), channel_id=1, source_target_pairs={{0,384},{128,0},{256,128},{384,256},{1,385},{129,1},{257,129},{385... | collective-permute-start | bytes 1114376 | tf_op jit(solution)/shard_map/ppermute | solution.py:26
  19.2 40.2 %collective-permute-start = (bf16[1450,128]{1,0:T(8,128)(2,1)S(1)}, bf16[1450,128]{1,0:T(8,128)(2,1)S(1)}, u32[]{:S(2)}, u32[]{:S(2)}) collective-permute-start(bf16[1450,128]{1,0:T(8,128)(2,1)S(1)} %pad_maximum_fusion.2), channel_id=1, source_target_pairs={{0,128},{128,256},{256,384},{384,0},{1,129},{129,257},{257,385},{3... | collective-permute-start | bytes 1113608 | tf_op jit(solution)/shard_map/ppermute | solution.py:22
  51.0 25.5 %collective-permute-start.3 = (bf16[484,128]{1,0:T(8,128)(2,1)S(1)}, bf16[484,128]{1,0:T(8,128)(2,1)S(1)}, u32[]{:S(2)}, u32[]{:S(2)}) collective-permute-start(bf16[484,128]{1,0:T(8,128)(2,1)S(1)} %slice.146), channel_id=1, source_target_pairs={{0,384},{128,0},{256,128},{384,256},{1,385},{129,1},{257,129},{385... | collective-permute-start | bytes 371720 | tf_op jit(solution)/shard_map/ppermute | solution.py:26
  59.4 17.0 %collective-permute-start.2 = (bf16[483,128]{1,0:T(8,128)(2,1)S(1)}, bf16[483,128]{1,0:T(8,128)(2,1)S(1)}, u32[]{:S(2)}, u32[]{:S(2)}) collective-permute-start(bf16[483,128]{1,0:T(8,128)(2,1)S(1)} %slice.145), channel_id=1, source_target_pairs={{0,128},{128,256},{256,384},{384,0},{1,129},{129,257},{257,385},{3... | collective-permute-start | bytes 370952 | tf_op jit(solution)/shard_map/ppermute | solution.py:22
  76.8 4.6 %copy-start.5 = (f32[72,192]{1,0:T(8,128)S(1)}, f32[72,192]{1,0:T(8,128)}, u32[]{:S(2)}) copy-start(f32[72,192]{1,0:T(8,128)} %param.18) | copy-start | bytes 165892
  76.8 4.6 %copy-start.6 = (f32[72,192]{1,0:T(8,128)S(1)}, f32[72,192]{1,0:T(8,128)}, u32[]{:S(2)}) copy-start(f32[72,192]{1,0:T(8,128)} %param.22) | copy-start | bytes 165892
  77.9 13.3 %all-to-all-start = ((f32[2,192,256]{2,0,1:T(2,128)}), f32[2,192,256]{2,0,1:T(2,128)S(1)}, u32[]{:S(2)}, u32[]{:S(2)}) async-start(f32[2,192,256]{2,0,1:T(2,128)} %copy.71), calls=%async_computation | async-start | bytes 786432 | tf_op jit(solution)/shard_map/all_to_all | solution.py:118
  81.3 10.0 %copy-start.1 = (f32[1,2,24,2048]{3,2,1,0:T(8,128)S(1)}, f32[1,2,24,2048]{3,2,1,0:T(8,128)}, u32[]{:S(2)}) copy-start(f32[1,2,24,2048]{3,2,1,0:T(8,128)} %param.17) | copy-start | bytes 1179652
  81.3 10.0 %copy-start.2 = (f32[1,2,24,2048]{3,2,1,0:T(8,128)S(1)}, f32[1,2,24,2048]{3,2,1,0:T(8,128)}, u32[]{:S(2)}) copy-start(f32[1,2,24,2048]{3,2,1,0:T(8,128)} %param.21) | copy-start | bytes 1179652
  92.2 8.1 %copy-start.3 = (f32[64,192]{1,0:T(8,128)S(1)}, f32[64,192]{1,0:T(8,128)}, u32[]{:S(2)}) copy-start(f32[64,192]{1,0:T(8,128)} %param.20) | copy-start | bytes 147460
  92.2 8.1 %copy-start.7 = (f32[64,192]{1,0:T(8,128)S(1)}, f32[64,192]{1,0:T(8,128)}, u32[]{:S(2)}) copy-start(f32[64,192]{1,0:T(8,128)} %param.24) | copy-start | bytes 147460
  92.2 9.2 %copy-start.9 = (f32[18,192]{1,0:T(8,128)S(1)}, f32[18,192]{1,0:T(8,128)}, u32[]{:S(2)}) copy-start(f32[18,192]{1,0:T(8,128)} %param.19) | copy-start | bytes 41476
  92.2 9.2 %copy-start.10 = (f32[18,192]{1,0:T(8,128)S(1)}, f32[18,192]{1,0:T(8,128)}, u32[]{:S(2)}) copy-start(f32[18,192]{1,0:T(8,128)} %param.23) | copy-start | bytes 41476
  94.2 12.5 %all-to-all-start.1 = ((bf16[8,2,6144]{2,1,0:T(2,128)(2,1)}), bf16[8,2,6144]{2,1,0:T(2,128)(2,1)S(1)}, u32[]{:S(2)}, u32[]{:S(2)}) async-start(bf16[8,2,6144]{2,1,0:T(2,128)(2,1)} %reshape.158), calls=%async_computation.1 | async-start | bytes 393216 | tf_op jit(solution)/shard_map/all_to_all | solution.py:129
  109.0 29.7 %collective-permute-start.5 = (bf16[999,128]{1,0:T(8,128)(2,1)S(1)}, bf16[999,128]{1,0:T(8,128)(2,1)S(1)}, u32[]{:S(2)}, u32[]{:S(2)}) collective-permute-start(bf16[999,128]{1,0:T(8,128)(2,1)S(1)} %pad_maximum_fusion.4), channel_id=1, source_target_pairs={{0,128},{128,256},{256,384},{384,0},{1,129},{129,257},{257,385},{3... | collective-permute-start | bytes 767240 | tf_op jit(solution)/shard_map/ppermute | solution.py:22
  114.4 30.2 %collective-permute-start.4 = (bf16[999,128]{1,0:T(8,128)(2,1)S(1)}, bf16[999,128]{1,0:T(8,128)(2,1)S(1)}, u32[]{:S(2)}, u32[]{:S(2)}) collective-permute-start(bf16[999,128]{1,0:T(8,128)(2,1)S(1)} %pad_maximum_fusion.4), channel_id=1, source_target_pairs={{0,384},{128,0},{256,128},{384,256},{1,385},{129,1},{257,129},{385... | collective-permute-start | bytes 767240 | tf_op jit(solution)/shard_map/ppermute | solution.py:26
  138.7 12.6 %collective-permute-start.6 = (bf16[499,128]{1,0:T(8,128)(2,1)S(1)}, bf16[499,128]{1,0:T(8,128)(2,1)S(1)}, u32[]{:S(2)}, u32[]{:S(2)}) collective-permute-start(bf16[499,128]{1,0:T(8,128)(2,1)S(1)} %slice.152), channel_id=1, source_target_pairs={{0,128},{128,256},{256,384},{384,0},{1,129},{129,257},{257,385},{3... | collective-permute-start | bytes 383240 | tf_op jit(solution)/shard_map/ppermute | solution.py:22
  144.7 15.7 %collective-permute-start.7 = (bf16[500,128]{1,0:T(8,128)(2,1)S(1)}, bf16[500,128]{1,0:T(8,128)(2,1)S(1)}, u32[]{:S(2)}, u32[]{:S(2)}) collective-permute-start(bf16[500,128]{1,0:T(8,128)(2,1)S(1)} %slice.153), channel_id=1, source_target_pairs={{0,384},{128,0},{256,128},{384,256},{1,385},{129,1},{257,129},{385... | collective-permute-start | bytes 384008 | tf_op jit(solution)/shard_map/ppermute | solution.py:26

commit v4 on v3

--- a/solution.py
+++ b/solution.py
@@ -26,19 +26,33 @@
     return lax.ppermute(x, "rep", [(i, (i - 1) % groups) for i in range(groups)])
 
 
-def rep_exchange(send, groups):
+def rep_exchange(send, raw_rows, groups):
     assert groups == 4
     me = lax.axis_index("rep")
     rel = [lax.dynamic_index_in_dim(send, (me + d) % groups, 0, False) for d in range(groups)]
     k = send.shape[1]
-    half = k // 2
-    fwd = to_next(jnp.concatenate([rel[1], rel[2][:half]]), groups)
-    bwd = to_prev(jnp.concatenate([rel[3], rel[2][half:]]), groups)
-    far_a = to_next(fwd[k:], groups)
-    far_b = to_prev(bwd[k:], groups)
+    m = k - raw_rows
+    h = m // 2
+    rh = raw_rows // 2
     f32 = jnp.float32
-    near = rel[0].astype(f32) + fwd[:k].astype(f32) + bwd[:k].astype(f32)
-    return near + jnp.concatenate([far_a, far_b]).astype(f32)
+    bf = send.dtype
+    a = to_next(jnp.concatenate([rel[2][:h], rel[2][m : m + rh]]), groups)
+    b = to_prev(jnp.concatenate([rel[2][h:m], rel[2][m + rh :]]), groups)
+    x = to_next(
+        jnp.concatenate(
+            [(rel[1][:h].astype(f32) + a[:h].astype(f32)).astype(bf), rel[1][h:], a[h:]]
+        ),
+        groups,
+    )
+    y = to_prev(
+        jnp.concatenate(
+            [rel[3][:h], (rel[3][h:m].astype(f32) + b[: m - h].astype(f32)).astype(bf), rel[3][m:], b[m - h :]]
+        ),
+        groups,
+    )
+    near = rel[0].astype(f32) + x[:k].astype(f32) + y[:k].astype(f32)
+    far_raw = jnp.concatenate([x[k:], y[k:]]).astype(f32)
+    return jnp.concatenate([near[:m], near[m:] + far_raw])
 
 
 def rep_gather(flat, groups):
@@ -103,7 +117,7 @@
 
     sizes = [ex_send.shape[1], de_send.shape[1], sm_send.shape[1], pp.shape[0]]
     send = jnp.concatenate([ex_send, de_send, sm_send, pp_send], axis=1)
-    total = rep_exchange(send, groups)
+    total = rep_exchange(send, pp.shape[0], groups)
     bounds = [0]
     for s in sizes:
         bounds.append(bounds[-1] + s)

time: 166 us -> 158 us (0.952)
  the two profiles are of different devices: /device:TPU:62 before, /device:TPU:1 now
where the time goes in v4:
time: 158 us; the launch traced here: 157 us
  waiting for transfers between devices  71.9 us (46%)
  starting transfers between devices  61.1 us (39%)
  local copies, waits for them, and re-layouts  16 us (10%)
  other arithmetic  3.32 us (2%)
  matrix products  3.16 us (2%)
    ppermute x4, starting transfers between devices, to_next(): lax.ppermute(x, 'rep', [(i, (i + 1) % groups) for i in range(groups)])  35.5 us
    ppermute x4, waiting for transfers between devices, to_next(): lax.ppermute(x, 'rep', [(i, (i + 1) % groups) for i in range(groups)])  29.9 us
    ppermute x4, waiting for transfers between devices, to_prev(): lax.ppermute(x, 'rep', [(i, (i - 1) % groups) for i in range(groups)])  27.1 us
    ppermute x4, starting transfers between devices, to_prev(): lax.ppermute(x, 'rep', [(i, (i - 1) % groups) for i in range(groups)])  15.4 us
    all_to_all x1, waiting for transfers between devices, on_device(): lax.all_to_all(ex_sum, 'mdl', split_axis=1, concat_axis=2, tiled=True)  10.2 us
    all_to_all x1, starting transfers between devices, on_device(): lax.all_to_all(ex_sum, 'mdl', split_axis=1, concat_axis=2, tiled=True)  5.65 us
    unnamed x24, local copies, waits for them, and re-layouts  5.05 us
    all_to_all x1, waiting for transfers between devices, on_device(): lax.all_to_all(expert_outer.astype(jnp.bfloat16), 'mdl', split_axis=2, co...  4.72 us
  transfers between devices with their start and end apart: 10, of which 10 were waited for; matrix products, arithmetic and copies ran while one was open for 3% of the time, Pallas kernels for 0%

profile of v4, /device:TPU:1, one launch (start us, length us, event | category | flops | bytes accessed | tf_op | source)
XLA Modules:
  0.0 156.9 jit_solution(513413688974592265)
XLA Ops:
  0.7 0.9 copy-done
  1.6 1.1 convolution_bitcast_fusion
  2.7 1.1 subtract_convert_fusion
  4.2 1.2 copy.65
  7.2 9.6 %collective-permute-start = (bf16[483,128]{1,0:T(8,128)(2,1)S(1)}, bf16[483,128]{1,0:T(8,128)(2,1)S(1)}, u32[]{:S(2)}, u32[]{:S(2)}) collective-permute-start(bf16[483,128]{1,0:T(8,128)(2,1)S(1)} %pad_maximum_fusion.5), channel_id=1, source_target_pairs={{0,128},{128,256},{256,384},{384,0},{1,129},{129,257},{257,385},{3... | collective-permute-start | bytes 370952 | tf_op jit(solution)/shard_map/ppermute | solution.py:22
  16.9 5.6 %collective-permute-start.2 = (bf16[484,128]{1,0:T(8,128)(2,1)S(1)}, bf16[484,128]{1,0:T(8,128)(2,1)S(1)}, u32[]{:S(2)}, u32[]{:S(2)}) collective-permute-start(bf16[484,128]{1,0:T(8,128)(2,1)S(1)} %pad_maximum_fusion.6), channel_id=1, source_target_pairs={{0,384},{128,0},{256,128},{384,256},{1,385},{129,1},{257,129},{385... | collective-permute-start | bytes 371720 | tf_op jit(solution)/shard_map/ppermute | solution.py:26
  23.3 12.8 %collective-permute-start.1 = (bf16[999,128]{1,0:T(8,128)(2,1)S(1)}, bf16[999,128]{1,0:T(8,128)(2,1)S(1)}, u32[]{:S(2)}, u32[]{:S(2)}) collective-permute-start(bf16[999,128]{1,0:T(8,128)(2,1)S(1)} %pad_maximum_fusion.2), channel_id=1, source_target_pairs={{0,128},{128,256},{256,384},{384,0},{1,129},{129,257},{257,385},{3... | collective-permute-start | bytes 767240 | tf_op jit(solution)/shard_map/ppermute | solution.py:22
  36.1 1.1 collective-permute-done.2
  37.3 4.0 %collective-permute-start.3 = (bf16[999,128]{1,0:T(8,128)(2,1)S(1)}, bf16[999,128]{1,0:T(8,128)(2,1)S(1)}, u32[]{:S(2)}, u32[]{:S(2)}) collective-permute-start(bf16[999,128]{1,0:T(8,128)(2,1)S(1)} %pad_maximum_fusion.3), channel_id=1, source_target_pairs={{0,384},{128,0},{256,128},{384,256},{1,385},{129,1},{257,129},{385... | collective-permute-start | bytes 767240 | tf_op jit(solution)/shard_map/ppermute | solution.py:26
  41.4 15.7 %collective-permute-done.1 = bf16[999,128]{1,0:T(8,128)(2,1)S(1)} collective-permute-done((bf16[999,128]{1,0:T(8,128)(2,1)S(1)}, bf16[999,128]{1,0:T(8,128)(2,1)S(1)}, u32[]{:S(2)}, u32[]{:S(2)}) %collective-permute-start.1) | collective-permute-done | bytes 255776 | tf_op jit(solution)/shard_map/ppermute | solution.py:22
  57.0 8.1 %collective-permute-done.3 = bf16[999,128]{1,0:T(8,128)(2,1)S(1)} collective-permute-done((bf16[999,128]{1,0:T(8,128)(2,1)S(1)}, bf16[999,128]{1,0:T(8,128)(2,1)S(1)}, u32[]{:S(2)}, u32[]{:S(2)}) %collective-permute-start.3) | collective-permute-done | bytes 255776 | tf_op jit(solution)/shard_map/ppermute | solution.py:26
  65.4 1.1 copy.71
  66.5 5.6 %all-to-all-start = ((f32[2,192,256]{2,0,1:T(2,128)}), f32[2,192,256]{2,0,1:T(2,128)S(1)}, u32[]{:S(2)}, u32[]{:S(2)}) async-start(f32[2,192,256]{2,0,1:T(2,128)} %copy.71), calls=%async_computation | async-start | bytes 786432 | tf_op jit(solution)/shard_map/all_to_all | solution.py:132
  72.3 0.9 fusion.17
  73.2 10.2 %all-to-all-done = f32[2,192,256]{2,0,1:T(2,128)S(1)} async-done(((f32[2,192,256]{2,0,1:T(2,128)}), f32[2,192,256]{2,0,1:T(2,128)S(1)}, u32[]{:S(2)}, u32[]{:S(2)}) %all-to-all-start) | async-done | bytes 393248 | tf_op jit(solution)/shard_map/all_to_all | solution.py:132
  83.6 0.7 copy.75
  84.4 2.0 %reshape.171 = bf16[8,2,6144]{2,1,0:T(2,128)(2,1)} reshape(bf16[2048,2,24]{2,1,0:T(2,128)(2,1)S(1)} %bitcast.93) | data formatting | bytes 393216
  86.4 4.5 %all-to-all-start.1 = ((bf16[8,2,6144]{2,1,0:T(2,128)(2,1)}), bf16[8,2,6144]{2,1,0:T(2,128)(2,1)S(1)}, u32[]{:S(2)}, u32[]{:S(2)}) async-start(bf16[8,2,6144]{2,1,0:T(2,128)(2,1)} %reshape.171), calls=%async_computation.1 | async-start | bytes 393216 | tf_op jit(solution)/shard_map/all_to_all | solution.py:143
  92.8 4.7 %all-to-all-done.1 = bf16[8,2,6144]{2,1,0:T(2,128)(2,1)S(1)} async-done(((bf16[8,2,6144]{2,1,0:T(2,128)(2,1)}), bf16[8,2,6144]{2,1,0:T(2,128)(2,1)S(1)}, u32[]{:S(2)}, u32[]{:S(2)}) %all-to-all-start.1) | async-done | bytes 196640 | tf_op jit(solution)/shard_map/all_to_all | solution.py:143
  97.5 1.5 reshape.172
  99.7 6.2 %collective-permute-start.5 = (bf16[999,128]{1,0:T(8,128)(2,1)S(1)}, bf16[999,128]{1,0:T(8,128)(2,1)S(1)}, u32[]{:S(2)}, u32[]{:S(2)}) collective-permute-start(bf16[999,128]{1,0:T(8,128)(2,1)S(1)} %pad_maximum_fusion.4), channel_id=1, source_target_pairs={{0,128},{128,256},{256,384},{384,0},{1,129},{129,257},{257,385},{3... | collective-permute-start | bytes 767240 | tf_op jit(solution)/shard_map/ppermute | solution.py:22
  106.0 3.0 %collective-permute-start.4 = (bf16[999,128]{1,0:T(8,128)(2,1)S(1)}, bf16[999,128]{1,0:T(8,128)(2,1)S(1)}, u32[]{:S(2)}, u32[]{:S(2)}) collective-permute-start(bf16[999,128]{1,0:T(8,128)(2,1)S(1)} %pad_maximum_fusion.4), channel_id=1, source_target_pairs={{0,384},{128,0},{256,128},{384,256},{1,385},{129,1},{257,129},{385... | collective-permute-start | bytes 767240 | tf_op jit(solution)/shard_map/ppermute | solution.py:26
  109.2 12.9 %collective-permute-done.5 = bf16[999,128]{1,0:T(8,128)(2,1)S(1)} collective-permute-done((bf16[999,128]{1,0:T(8,128)(2,1)S(1)}, bf16[999,128]{1,0:T(8,128)(2,1)S(1)}, u32[]{:S(2)}, u32[]{:S(2)}) %collective-permute-start.5) | collective-permute-done | bytes 255776 | tf_op jit(solution)/shard_map/ppermute | solution.py:22
  122.1 6.9 %collective-permute-start.6 = (bf16[499,128]{1,0:T(8,128)(2,1)S(1)}, bf16[499,128]{1,0:T(8,128)(2,1)S(1)}, u32[]{:S(2)}, u32[]{:S(2)}) collective-permute-start(bf16[499,128]{1,0:T(8,128)(2,1)S(1)} %slice.228), channel_id=1, source_target_pairs={{0,128},{128,256},{256,384},{384,0},{1,129},{129,257},{257,385},{3... | collective-permute-start | bytes 383240 | tf_op jit(solution)/shard_map/ppermute | solution.py:22
  129.0 7.1 %collective-permute-done.4 = bf16[999,128]{1,0:T(8,128)(2,1)S(1)} collective-permute-done((bf16[999,128]{1,0:T(8,128)(2,1)S(1)}, bf16[999,128]{1,0:T(8,128)(2,1)S(1)}, u32[]{:S(2)}, u32[]{:S(2)}) %collective-permute-start.4) | collective-permute-done | bytes 255776 | tf_op jit(solution)/shard_map/ppermute | solution.py:26
  136.2 2.9 %collective-permute-start.7 = (bf16[500,128]{1,0:T(8,128)(2,1)S(1)}, bf16[500,128]{1,0:T(8,128)(2,1)S(1)}, u32[]{:S(2)}, u32[]{:S(2)}) collective-permute-start(bf16[500,128]{1,0:T(8,128)(2,1)S(1)} %slice.229), channel_id=1, source_target_pairs={{0,384},{128,0},{256,128},{384,256},{1,385},{129,1},{257,129},{385... | collective-permute-start | bytes 384008 | tf_op jit(solution)/shard_map/ppermute | solution.py:26
  139.1 1.0 multiply_subtract_fusion
  140.8 10.7 %collective-permute-done.7 = bf16[500,128]{1,0:T(8,128)(2,1)S(1)} collective-permute-done((bf16[500,128]{1,0:T(8,128)(2,1)S(1)}, bf16[500,128]{1,0:T(8,128)(2,1)S(1)}, u32[]{:S(2)}, u32[]{:S(2)}) %collective-permute-start.7) | collective-permute-done | bytes 128032 | tf_op jit(solution)/shard_map/ppermute | solution.py:26
  152.3 0.8 reshape.167
  153.6 0.7 reshape.166
  154.8 0.8 reshape.165
  156.0 0.9 copy.77
  (107 shorter events, 9.1 us)
Async XLA Ops:
  0.6 0.9 copy-start
  5.4 0.9 copy-start.4
  5.4 1.3 copy-start.8
  7.2 16.0 %collective-permute-start = (bf16[483,128]{1,0:T(8,128)(2,1)S(1)}, bf16[483,128]{1,0:T(8,128)(2,1)S(1)}, u32[]{:S(2)}, u32[]{:S(2)}) collective-permute-start(bf16[483,128]{1,0:T(8,128)(2,1)S(1)} %pad_maximum_fusion.5), channel_id=1, source_target_pairs={{0,128},{128,256},{256,384},{384,0},{1,129},{129,257},{257,385},{3... | collective-permute-start | bytes 370952 | tf_op jit(solution)/shard_map/ppermute | solution.py:22
  16.9 20.3 %collective-permute-start.2 = (bf16[484,128]{1,0:T(8,128)(2,1)S(1)}, bf16[484,128]{1,0:T(8,128)(2,1)S(1)}, u32[]{:S(2)}, u32[]{:S(2)}) collective-permute-start(bf16[484,128]{1,0:T(8,128)(2,1)S(1)} %pad_maximum_fusion.6), channel_id=1, source_target_pairs={{0,384},{128,0},{256,128},{384,256},{1,385},{129,1},{257,129},{385... | collective-permute-start | bytes 371720 | tf_op jit(solution)/shard_map/ppermute | solution.py:26
  23.3 33.7 %collective-permute-start.1 = (bf16[999,128]{1,0:T(8,128)(2,1)S(1)}, bf16[999,128]{1,0:T(8,128)(2,1)S(1)}, u32[]{:S(2)}, u32[]{:S(2)}) collective-permute-start(bf16[999,128]{1,0:T(8,128)(2,1)S(1)} %pad_maximum_fusion.2), channel_id=1, source_target_pairs={{0,128},{128,256},{256,384},{384,0},{1,129},{129,257},{257,385},{3... | collective-permute-start | bytes 767240 | tf_op jit(solution)/shard_map/ppermute | solution.py:22
  37.3 27.8 %collective-permute-start.3 = (bf16[999,128]{1,0:T(8,128)(2,1)S(1)}, bf16[999,128]{1,0:T(8,128)(2,1)S(1)}, u32[]{:S(2)}, u32[]{:S(2)}) collective-permute-start(bf16[999,128]{1,0:T(8,128)(2,1)S(1)} %pad_maximum_fusion.3), channel_id=1, source_target_pairs={{0,384},{128,0},{256,128},{384,256},{1,385},{129,1},{257,129},{385... | collective-permute-start | bytes 767240 | tf_op jit(solution)/shard_map/ppermute | solution.py:26
  65.4 6.9 %copy-start.3 = (f32[64,192]{1,0:T(8,128)S(1)}, f32[64,192]{1,0:T(8,128)}, u32[]{:S(2)}) copy-start(f32[64,192]{1,0:T(8,128)} %param.20) | copy-start | bytes 147460
  65.4 6.9 %copy-start.7 = (f32[64,192]{1,0:T(8,128)S(1)}, f32[64,192]{1,0:T(8,128)}, u32[]{:S(2)}) copy-start(f32[64,192]{1,0:T(8,128)} %param.24) | copy-start | bytes 147460
  66.5 17.0 %all-to-all-start = ((f32[2,192,256]{2,0,1:T(2,128)}), f32[2,192,256]{2,0,1:T(2,128)S(1)}, u32[]{:S(2)}, u32[]{:S(2)}) async-start(f32[2,192,256]{2,0,1:T(2,128)} %copy.71), calls=%async_computation | async-start | bytes 786432 | tf_op jit(solution)/shard_map/all_to_all | solution.py:132
  72.2 11.3 %copy-start.1 = (f32[1,2,24,2048]{3,2,1,0:T(8,128)S(1)}, f32[1,2,24,2048]{3,2,1,0:T(8,128)}, u32[]{:S(2)}) copy-start(f32[1,2,24,2048]{3,2,1,0:T(8,128)} %param.17) | copy-start | bytes 1179652
  72.2 11.3 %copy-start.2 = (f32[1,2,24,2048]{3,2,1,0:T(8,128)S(1)}, f32[1,2,24,2048]{3,2,1,0:T(8,128)}, u32[]{:S(2)}) copy-start(f32[1,2,24,2048]{3,2,1,0:T(8,128)} %param.21) | copy-start | bytes 1179652
  84.4 6.8 %copy-start.5 = (f32[72,192]{1,0:T(8,128)S(1)}, f32[72,192]{1,0:T(8,128)}, u32[]{:S(2)}) copy-start(f32[72,192]{1,0:T(8,128)} %param.18) | copy-start | bytes 165892
  84.4 6.8 %copy-start.6 = (f32[72,192]{1,0:T(8,128)S(1)}, f32[72,192]{1,0:T(8,128)}, u32[]{:S(2)}) copy-start(f32[72,192]{1,0:T(8,128)} %param.22) | copy-start | bytes 165892
  84.4 7.6 %copy-start.9 = (f32[18,192]{1,0:T(8,128)S(1)}, f32[18,192]{1,0:T(8,128)}, u32[]{:S(2)}) copy-start(f32[18,192]{1,0:T(8,128)} %param.19) | copy-start | bytes 41476
  84.4 7.6 %copy-start.10 = (f32[18,192]{1,0:T(8,128)S(1)}, f32[18,192]{1,0:T(8,128)}, u32[]{:S(2)}) copy-start(f32[18,192]{1,0:T(8,128)} %param.23) | copy-start | bytes 41476
  86.4 11.0 %all-to-all-start.1 = ((bf16[8,2,6144]{2,1,0:T(2,128)(2,1)}), bf16[8,2,6144]{2,1,0:T(2,128)(2,1)S(1)}, u32[]{:S(2)}, u32[]{:S(2)}) async-start(bf16[8,2,6144]{2,1,0:T(2,128)(2,1)} %reshape.171), calls=%async_computation.1 | async-start | bytes 393216 | tf_op jit(solution)/shard_map/all_to_all | solution.py:143
  99.7 22.3 %collective-permute-start.5 = (bf16[999,128]{1,0:T(8,128)(2,1)S(1)}, bf16[999,128]{1,0:T(8,128)(2,1)S(1)}, u32[]{:S(2)}, u32[]{:S(2)}) collective-permute-start(bf16[999,128]{1,0:T(8,128)(2,1)S(1)} %pad_maximum_fusion.4), channel_id=1, source_target_pairs={{0,128},{128,256},{256,384},{384,0},{1,129},{129,257},{257,385},{3... | collective-permute-start | bytes 767240 | tf_op jit(solution)/shard_map/ppermute | solution.py:22
  106.0 30.2 %collective-permute-start.4 = (bf16[999,128]{1,0:T(8,128)(2,1)S(1)}, bf16[999,128]{1,0:T(8,128)(2,1)S(1)}, u32[]{:S(2)}, u32[]{:S(2)}) collective-permute-start(bf16[999,128]{1,0:T(8,128)(2,1)S(1)} %pad_maximum_fusion.4), channel_id=1, source_target_pairs={{0,384},{128,0},{256,128},{384,256},{1,385},{129,1},{257,129},{385... | collective-permute-start | bytes 767240 | tf_op jit(solution)/shard_map/ppermute | solution.py:26
  122.1 18.7 %collective-permute-start.6 = (bf16[499,128]{1,0:T(8,128)(2,1)S(1)}, bf16[499,128]{1,0:T(8,128)(2,1)S(1)}, u32[]{:S(2)}, u32[]{:S(2)}) collective-permute-start(bf16[499,128]{1,0:T(8,128)(2,1)S(1)} %slice.228), channel_id=1, source_target_pairs={{0,128},{128,256},{256,384},{384,0},{1,129},{129,257},{257,385},{3... | collective-permute-start | bytes 383240 | tf_op jit(solution)/shard_map/ppermute | solution.py:22
  136.2 15.3 %collective-permute-start.7 = (bf16[500,128]{1,0:T(8,128)(2,1)S(1)}, bf16[500,128]{1,0:T(8,128)(2,1)S(1)}, u32[]{:S(2)}, u32[]{:S(2)}) collective-permute-start(bf16[500,128]{1,0:T(8,128)(2,1)S(1)} %slice.229), channel_id=1, source_target_pairs={{0,384},{128,0},{256,128},{384,256},{1,385},{129,1},{257,129},{385... | collective-permute-start | bytes 384008 | tf_op jit(solution)/shard_map/ppermute | solution.py:26

commit v5 on v4

--- a/solution.py
+++ b/solution.py
@@ -86,88 +86,101 @@
 ):
     groups = lax.axis_size("rep")
     hi_prec = lax.Precision.HIGHEST
-
     lanes = 128
+    f32 = jnp.float32
+    bf = jnp.bfloat16
+
     own_shard = inner_experts[0, 0]
     halves, all_rows, my_cols = own_shard.shape
     rep_rows = all_rows // groups
-    ex_send = (
-        own_shard.reshape(halves, groups, rep_rows, my_cols)
-        .transpose(1, 0, 2, 3)
-        .reshape(groups, -1, lanes)
-    )
+
+    def expert_send(h):
+        return own_shard[h].reshape(groups, rep_rows * my_cols // lanes, lanes)
+
     de_send = split_rows(inner_dense[0], groups).reshape(groups, -1, lanes)
     sm_send = split_rows(inner_small[0], groups).reshape(groups, -1, lanes)
-
     col_count = outer_embed.shape[1]
     offset = lax.axis_index("rep") * col_count
     basis_part = lax.dynamic_slice_in_dim(embed_basis, offset, col_count, 0)
     partial_value = jnp.dot(
-        outer_embed, basis_part, precision=hi_prec, preferred_element_type=jnp.float32
+        outer_embed, basis_part, precision=hi_prec, preferred_element_type=f32
     ) - jnp.dot(
-        inner_embed[0].astype(jnp.float32),
-        embed_basis,
-        precision=hi_prec,
-        preferred_element_type=jnp.float32,
+        inner_embed[0].astype(f32), embed_basis, precision=hi_prec, preferred_element_type=f32
     ) / groups
-    part_hi = partial_value.astype(jnp.bfloat16)
-    part_lo = (partial_value - part_hi.astype(jnp.float32)).astype(jnp.bfloat16)
+    part_hi = partial_value.astype(bf)
+    part_lo = (partial_value - part_hi.astype(f32)).astype(bf)
     pp = jnp.concatenate([part_hi.reshape(-1, lanes), part_lo.reshape(-1, lanes)])
     pp_send = jnp.broadcast_to(pp[None], (groups,) + pp.shape)
 
-    sizes = [ex_send.shape[1], de_send.shape[1], sm_send.shape[1], pp.shape[0]]
-    send = jnp.concatenate([ex_send, de_send, sm_send, pp_send], axis=1)
-    total = rep_exchange(send, pp.shape[0], groups)
+    ex_rows = rep_rows * my_cols // lanes
+    send_a = jnp.concatenate([expert_send(0), de_send, sm_send, pp_send], axis=1)
+    send_b = expert_send(1)
+    total_a = rep_exchange(send_a, pp.shape[0], groups)
+    send_b, total_a = lax.optimization_barrier((send_b, total_a))
+    total_b = rep_exchange(send_b, 0, groups)
+
+    sizes = [ex_rows, de_send.shape[1], sm_send.shape[1], pp.shape[0]]
     bounds = [0]
-    for s in sizes:
-        bounds.append(bounds[-1] + s)
-    parts = [total[bounds[i] : bounds[i + 1]] for i in range(4)]
-
-    ex_sum = parts[0].reshape(halves, rep_rows, my_cols)
+    for n in sizes:
+        bounds.append(bounds[-1] + n)
+    parts = [total_a[bounds[i] : bounds[i + 1]] for i in range(4)]
     dense_sum = parts[1].reshape(outer_dense.shape)
     small_sum = parts[2].reshape(outer_small.shape)
     nhalf = parts[3].shape[0] // 2
     coefficient = (parts[3][:nhalf] + parts[3][nhalf:]).reshape(partial_value.shape)
 
-    expert_sum = lax.all_to_all(ex_sum, "mdl", split_axis=1, concat_axis=2, tiled=True)
-    grad_experts = outer_experts[0] - expert_sum / groups
+    def expert_half(ex_total, h):
+        ex_sum = ex_total.reshape(rep_rows, my_cols)
+        expert_sum = lax.all_to_all(ex_sum, "mdl", split_axis=0, concat_axis=1, tiled=True)
+        grad = outer_experts[0, h] - expert_sum / groups
+        e_outer, e_moment = nesterov(outer_experts[0, h], moment_experts[0, h], grad)
+        spread = lax.all_to_all(e_outer.astype(bf), "mdl", split_axis=1, concat_axis=0, tiled=True)
+        return e_outer, e_moment, spread
+
+    ea_outer, ea_moment, spread_a = expert_half(parts[0], 0)
+    eb_outer, eb_moment, spread_b = expert_half(total_b, 1)
+
     grad_dense = outer_dense - dense_sum / groups
     grad_small = outer_small - small_sum / groups
-    grad_embed = jnp.dot(
-        coefficient, basis_part.T, precision=hi_prec, preferred_element_type=jnp.float32
-    )
-    expert_outer, expert_moment = nesterov(outer_experts[0], moment_experts[0], grad_experts)
+    grad_embed = jnp.dot(coefficient, basis_part.T, precision=hi_prec, preferred_element_type=f32)
     dense_outer, dense_moment = nesterov(outer_dense, moment_dense, grad_dense)
     small_outer, small_moment = nesterov(outer_small, moment_small, grad_small)
     embed_outer, embed_moment = nesterov(outer_embed, moment_embed, grad_embed)
-    spread = lax.all_to_all(
-        expert_outer.astype(jnp.bfloat16), "mdl", split_axis=2, concat_axis=1, tiled=True
-    )
-
-    pieces = [
-        spread,
-        dense_outer.astype(jnp.bfloat16),
-        small_outer.astype(jnp.bfloat16),
-        embed_outer.astype(jnp.bfloat16),
+
+    pieces_a = [
+        spread_a,
+        dense_outer.astype(bf),
+        small_outer.astype(bf),
+        embed_outer.astype(bf),
     ]
-    flat = jnp.concatenate([p.reshape(-1, lanes) for p in pieces])
-    blocks = rep_gather(flat, groups)
+    flat_a = jnp.concatenate([p.reshape(-1, lanes) for p in pieces_a])
+    flat_a, total_b = lax.optimization_barrier((flat_a, total_b))
+    blocks_a = rep_gather(flat_a, groups)
+    blocks_b = rep_gather(spread_b.reshape(-1, lanes), groups)
+
+    def assemble(blocks, p, start):
+        n = p.size // lanes
+        g = jnp.stack([b[start : start + n] for b in blocks]).reshape((groups,) + p.shape)
+        return g.transpose(1, 0, 2).reshape(p.shape[0], groups * p.shape[1])
+
     outs = []
     start = 0
-    for p in pieces:
-        n = p.size // lanes
-        g = jnp.stack([b[start : start + n] for b in blocks]).reshape((groups,) + p.shape)
-        start += n
-        if p.ndim == 3:
-            g = g.transpose(1, 0, 2, 3).reshape(p.shape[0], groups * p.shape[1], p.shape[2])
+    for p in pieces_a:
+        if p is spread_a:
+            g = jnp.stack([b[: p.size // lanes] for b in blocks_a]).reshape((groups * p.shape[0], p.shape[1]))
         else:
-            g = g.transpose(1, 0, 2).reshape(p.shape[0], groups * p.shape[1])
+            g = assemble(blocks_a, p, start)
+        start += p.size // lanes
         outs.append(g)
-
+    copy_b = jnp.stack(blocks_b).reshape((groups * spread_b.shape[0], spread_b.shape[1]))
+    copy_experts = jnp.stack([outs[0], copy_b])
+
+    expert_outer = jnp.stack([ea_outer, eb_outer])
+    expert_moment = jnp.stack([ea_moment, eb_moment])
     return (
         expert_outer[None],
         expert_moment[None],
-        outs[0][None],
+        copy_experts[None],
         dense_outer,
         dense_moment,
         outs[1],

time: 158 us -> 194 us (1.23)
  the two profiles are of different devices: /device:TPU:1 before, /device:TPU:42 now
where the time goes in v5:
time: 194 us; the launch traced here: 193 us
  starting transfers between devices  113 us (58%)
  waiting for transfers between devices  56.2 us (29%)
  local copies, waits for them, and re-layouts  10.6 us (5%)
  other arithmetic  7.95 us (4%)
  matrix products  3.24 us (2%)
    ppermute x8, starting transfers between devices, to_next(): lax.ppermute(x, 'rep', [(i, (i + 1) % groups) for i in range(groups)])  48.3 us
    ppermute x8, starting transfers between devices, to_prev(): lax.ppermute(x, 'rep', [(i, (i - 1) % groups) for i in range(groups)])  34.4 us
    ppermute x8, waiting for transfers between devices, to_prev(): lax.ppermute(x, 'rep', [(i, (i - 1) % groups) for i in range(groups)])  25.3 us
    ppermute x8, waiting for transfers between devices, to_next(): lax.ppermute(x, 'rep', [(i, (i + 1) % groups) for i in range(groups)])  21.9 us
    all_to_all x2, starting transfers between devices, expert_half(): lax.all_to_all(ex_sum, 'mdl', split_axis=0, concat_axis=1, tiled=True)  21.3 us
    all_to_all x2, starting transfers between devices, expert_half(): lax.all_to_all(e_outer.astype(bf), 'mdl', split_axis=1, concat_axis=0, ti...  9.35 us
    all_to_all x2, waiting for transfers between devices, expert_half(): lax.all_to_all(ex_sum, 'mdl', split_axis=0, concat_axis=1, tiled=True)  4.73 us
    all_to_all x2, waiting for transfers between devices, expert_half(): lax.all_to_all(e_outer.astype(bf), 'mdl', split_axis=1, concat_axis=0, ti...  4.23 us
  transfers between devices with their start and end apart: 20, of which 12 were waited for; matrix products, arithmetic and copies ran while one was open for 6% of the time, Pallas kernels for 0%

profile of v5, /device:TPU:42, one launch (start us, length us, event | category | flops | bytes accessed | tf_op | source)
XLA Modules:
  0.0 192.9 jit_solution(7598991500471829979)
XLA Ops:
  2.7 1.2 subtract_convert_fusion
  6.1 11.8 %collective-permute-start.2 = (bf16[292,128]{1,0:T(8,128)(2,1)S(1)}, bf16[292,128]{1,0:T(8,128)(2,1)S(1)}, u32[]{:S(2)}, u32[]{:S(2)}) collective-permute-start(bf16[292,128]{1,0:T(8,128)(2,1)S(1)} %pad_maximum_fusion.12), channel_id=1, source_target_pairs={{0,384},{128,0},{256,128},{384,256},{1,385},{129,1},{257,129},{385... | collective-permute-start | bytes 224264 | tf_op jit(solution)/shard_map/ppermute | solution.py:26
  18.1 1.9 collective-permute-start
  20.1 11.4 %collective-permute-done = bf16[291,128]{1,0:T(8,128)(2,1)S(1)} collective-permute-done((bf16[291,128]{1,0:T(8,128)(2,1)S(1)}, bf16[291,128]{1,0:T(8,128)(2,1)S(1)}, u32[]{:S(2)}, u32[]{:S(2)}) %collective-permute-start) | collective-permute-done | bytes 74528 | tf_op jit(solution)/shard_map/ppermute | solution.py:22
  32.2 1.9 collective-permute-start.1
  34.9 7.8 %collective-permute-start.3 = (bf16[615,128]{1,0:T(8,128)(2,1)}, bf16[615,128]{1,0:T(8,128)(2,1)}, u32[]{:S(2)}, u32[]{:S(2)}) collective-permute-start(bf16[615,128]{1,0:T(8,128)(2,1)} %pad_maximum_fusion.7), channel_id=1, source_target_pairs={{0,384},{128,0},{256,128},{384,256},{1,385},{129,1},{257,129},{385... | collective-permute-start | bytes 472328 | tf_op jit(solution)/shard_map/ppermute | solution.py:26
  43.3 2.3 %collective-permute-done.1 = bf16[615,128]{1,0:T(8,128)(2,1)S(1)} collective-permute-done((bf16[615,128]{1,0:T(8,128)(2,1)}, bf16[615,128]{1,0:T(8,128)(2,1)S(1)}, u32[]{:S(2)}, u32[]{:S(2)}) %collective-permute-start.1) | collective-permute-done | bytes 157472 | tf_op jit(solution)/shard_map/ppermute | solution.py:22
  45.6 1.5 collective-permute-done.3
  49.8 12.9 %all-to-all-start = ((f32[8,24,256]{2,1,0:T(8,128)}), f32[8,24,256]{2,1,0:T(8,128)S(1)}, u32[]{:S(2)}, u32[]{:S(2)}) async-start(f32[8,24,256]{2,1,0:T(8,128)} %all_to_all.40), calls=%async_computation | async-start | bytes 393216 | tf_op jit(solution)/shard_map/all_to_all | solution.py:134
  62.8 7.8 %collective-permute-start.4 = (bf16[192,128]{1,0:T(8,128)(2,1)S(1)}, bf16[192,128]{1,0:T(8,128)(2,1)S(1)}, u32[]{:S(2)}, u32[]{:S(2)}) collective-permute-start(bf16[192,128]{1,0:T(8,128)(2,1)S(1)} %get-tuple-element.67), channel_id=1, source_target_pairs={{0,128},{128,256},{256,384},{384,0},{1,129},{129,257},{257,385},{3... | collective-permute-start | bytes 147464 | tf_op jit(solution)/shard_map/ppermute | solution.py:22
  70.6 2.0 %collective-permute-start.6 = (bf16[192,128]{1,0:T(8,128)(2,1)S(1)}, bf16[192,128]{1,0:T(8,128)(2,1)S(1)}, u32[]{:S(2)}, u32[]{:S(2)}) collective-permute-start(bf16[192,128]{1,0:T(8,128)(2,1)S(1)} %get-tuple-element.69), channel_id=1, source_target_pairs={{0,384},{128,0},{256,128},{384,256},{1,385},{129,1},{257,129},{385... | collective-permute-start | bytes 147464 | tf_op jit(solution)/shard_map/ppermute | solution.py:26
  73.9 7.7 %collective-permute-done.6 = bf16[192,128]{1,0:T(8,128)(2,1)S(1)} collective-permute-done((bf16[192,128]{1,0:T(8,128)(2,1)S(1)}, bf16[192,128]{1,0:T(8,128)(2,1)S(1)}, u32[]{:S(2)}, u32[]{:S(2)}) %collective-permute-start.6) | collective-permute-done | bytes 49184 | tf_op jit(solution)/shard_map/ppermute | solution.py:26
  81.7 2.9 %collective-permute-start.7 = (bf16[384,128]{1,0:T(8,128)(2,1)S(1)}, bf16[384,128]{1,0:T(8,128)(2,1)S(1)}, u32[]{:S(2)}, u32[]{:S(2)}) collective-permute-start(bf16[384,128]{1,0:T(8,128)(2,1)S(1)} %pad_maximum_fusion.10), channel_id=1, source_target_pairs={{0,384},{128,0},{256,128},{384,256},{1,385},{129,1},{257,129},{385... | collective-permute-start | bytes 294920 | tf_op jit(solution)/shard_map/ppermute | solution.py:26
  84.7 7.0 %collective-permute-start.5 = (bf16[384,128]{1,0:T(8,128)(2,1)S(1)}, bf16[384,128]{1,0:T(8,128)(2,1)S(1)}, u32[]{:S(2)}, u32[]{:S(2)}) collective-permute-start(bf16[384,128]{1,0:T(8,128)(2,1)S(1)} %pad_maximum_fusion.9), channel_id=1, source_target_pairs={{0,128},{128,256},{256,384},{384,0},{1,129},{129,257},{257,385},{3... | collective-permute-start | bytes 294920 | tf_op jit(solution)/shard_map/ppermute | solution.py:22
  91.9 3.1 %collective-permute-done.7 = bf16[384,128]{1,0:T(8,128)(2,1)S(1)} collective-permute-done((bf16[384,128]{1,0:T(8,128)(2,1)S(1)}, bf16[384,128]{1,0:T(8,128)(2,1)S(1)}, u32[]{:S(2)}, u32[]{:S(2)}) %collective-permute-start.7) | collective-permute-done | bytes 98336 | tf_op jit(solution)/shard_map/ppermute | solution.py:26
  96.5 8.3 %all-to-all-start.1 = ((f32[8,24,256]{2,1,0:T(8,128)}), f32[8,24,256]{2,1,0:T(8,128)S(1)}, u32[]{:S(2)}, u32[]{:S(2)}) async-start(f32[8,24,256]{2,1,0:T(8,128)} %all_to_all.42), calls=%async_computation.1 | async-start | bytes 393216 | tf_op jit(solution)/shard_map/all_to_all | solution.py:134
  106.8 4.7 %all-to-all-done.1 = f32[8,24,256]{2,1,0:T(8,128)S(1)} async-done(((f32[8,24,256]{2,1,0:T(8,128)}), f32[8,24,256]{2,1,0:T(8,128)S(1)}, u32[]{:S(2)}, u32[]{:S(2)}) %all-to-all-start.1) | async-done | bytes 196640 | tf_op jit(solution)/shard_map/all_to_all | solution.py:134
  111.5 4.9 %all-to-all-start.2 = ((bf16[24,8,256]{2,0,1:T(8,128)(2,1)}), bf16[24,8,256]{2,0,1:T(8,128)(2,1)S(1)}, u32[]{:S(2)}, u32[]{:S(2)}) async-start(bf16[24,8,256]{2,0,1:T(8,128)(2,1)} %fusion.12), calls=%async_computation.2 | async-start | bytes 196608 | tf_op jit(solution)/shard_map/all_to_all | solution.py:137
  117.3 4.2 %all-to-all-done.2 = bf16[24,8,256]{2,0,1:T(8,128)(2,1)S(1)} async-done(((bf16[24,8,256]{2,0,1:T(8,128)(2,1)}), bf16[24,8,256]{2,0,1:T(8,128)(2,1)S(1)}, u32[]{:S(2)}, u32[]{:S(2)}) %all-to-all-start.2) | async-done | bytes 98336 | tf_op jit(solution)/shard_map/all_to_all | solution.py:137
  121.6 4.5 %all-to-all-start.3 = ((bf16[24,8,256]{2,0,1:T(8,128)(2,1)}), bf16[24,8,256]{2,0,1:T(8,128)(2,1)S(1)}, u32[]{:S(2)}, u32[]{:S(2)}) async-start(bf16[24,8,256]{2,0,1:T(8,128)(2,1)} %fusion.7), calls=%async_computation.3 | async-start | bytes 196608 | tf_op jit(solution)/shard_map/all_to_all | solution.py:137
  126.1 7.2 %collective-permute-start.9 = (bf16[615,128]{1,0:T(8,128)(2,1)S(1)}, bf16[615,128]{1,0:T(8,128)(2,1)S(1)}, u32[]{:S(2)}, u32[]{:S(2)}) collective-permute-start(bf16[615,128]{1,0:T(8,128)(2,1)S(1)} %pad_maximum_fusion.8), channel_id=1, source_target_pairs={{0,128},{128,256},{256,384},{384,0},{1,129},{129,257},{257,385},{3... | collective-permute-start | bytes 472328 | tf_op jit(solution)/shard_map/ppermute | solution.py:22
  133.3 2.5 %collective-permute-start.8 = (bf16[615,128]{1,0:T(8,128)(2,1)S(1)}, bf16[615,128]{1,0:T(8,128)(2,1)S(1)}, u32[]{:S(2)}, u32[]{:S(2)}) collective-permute-start(bf16[615,128]{1,0:T(8,128)(2,1)S(1)} %pad_maximum_fusion.8), channel_id=1, source_target_pairs={{0,384},{128,0},{256,128},{384,256},{1,385},{129,1},{257,129},{385... | collective-permute-start | bytes 472328 | tf_op jit(solution)/shard_map/ppermute | solution.py:26
  136.0 5.6 %collective-permute-done.9 = bf16[615,128]{1,0:T(8,128)(2,1)S(1)} collective-permute-done((bf16[615,128]{1,0:T(8,128)(2,1)S(1)}, bf16[615,128]{1,0:T(8,128)(2,1)S(1)}, u32[]{:S(2)}, u32[]{:S(2)}) %collective-permute-start.9) | collective-permute-done | bytes 157472 | tf_op jit(solution)/shard_map/ppermute | solution.py:22
  141.5 7.2 %collective-permute-start.10 = (bf16[307,128]{1,0:T(8,128)(2,1)S(1)}, bf16[307,128]{1,0:T(8,128)(2,1)S(1)}, u32[]{:S(2)}, u32[]{:S(2)}) collective-permute-start(bf16[307,128]{1,0:T(8,128)(2,1)S(1)} %slice.305), channel_id=1, source_target_pairs={{0,128},{128,256},{256,384},{384,0},{1,129},{129,257},{257,385},{3... | collective-permute-start | bytes 235784 | tf_op jit(solution)/shard_map/ppermute | solution.py:22
  148.7 6.4 %collective-permute-done.8 = bf16[615,128]{1,0:T(8,128)(2,1)S(1)} collective-permute-done((bf16[615,128]{1,0:T(8,128)(2,1)S(1)}, bf16[615,128]{1,0:T(8,128)(2,1)S(1)}, u32[]{:S(2)}, u32[]{:S(2)}) %collective-permute-start.8) | collective-permute-done | bytes 157472 | tf_op jit(solution)/shard_map/ppermute | solution.py:26
  155.2 2.7 %collective-permute-start.11 = (bf16[308,128]{1,0:T(8,128)(2,1)S(1)}, bf16[308,128]{1,0:T(8,128)(2,1)S(1)}, u32[]{:S(2)}, u32[]{:S(2)}) collective-permute-start(bf16[308,128]{1,0:T(8,128)(2,1)S(1)} %slice.306), channel_id=1, source_target_pairs={{0,384},{128,0},{256,128},{384,256},{1,385},{129,1},{257,129},{385... | collective-permute-start | bytes 236552 | tf_op jit(solution)/shard_map/ppermute | solution.py:26
  158.9 7.0 %collective-permute-start.13 = (bf16[384,128]{1,0:T(8,128)(2,1)S(1)}, bf16[384,128]{1,0:T(8,128)(2,1)S(1)}, u32[]{:S(2)}, u32[]{:S(2)}) collective-permute-start(bf16[384,128]{1,0:T(8,128)(2,1)S(1)} %reshape.310), channel_id=1, source_target_pairs={{0,128},{128,256},{256,384},{384,0},{1,129},{129,257},{257,385},{3... | collective-permute-start | bytes 294920 | tf_op jit(solution)/shard_map/ppermute | solution.py:22
  165.9 2.7 %collective-permute-start.12 = (bf16[384,128]{1,0:T(8,128)(2,1)S(1)}, bf16[384,128]{1,0:T(8,128)(2,1)S(1)}, u32[]{:S(2)}, u32[]{:S(2)}) collective-permute-start(bf16[384,128]{1,0:T(8,128)(2,1)S(1)} %reshape.310), channel_id=1, source_target_pairs={{0,384},{128,0},{256,128},{384,256},{1,385},{129,1},{257,129},{385... | collective-permute-start | bytes 294920 | tf_op jit(solution)/shard_map/ppermute | solution.py:26
  170.1 1.9 %collective-permute-done.13 = bf16[384,128]{1,0:T(8,128)(2,1)S(1)} collective-permute-done((bf16[384,128]{1,0:T(8,128)(2,1)S(1)}, bf16[384,128]{1,0:T(8,128)(2,1)S(1)}, u32[]{:S(2)}, u32[]{:S(2)}) %collective-permute-start.13) | collective-permute-done | bytes 98336 | tf_op jit(solution)/shard_map/ppermute | solution.py:22
  172.1 8.3 %collective-permute-start.14 = (bf16[192,128]{1,0:T(8,128)(2,1)S(1)}, bf16[192,128]{1,0:T(8,128)(2,1)S(1)}, u32[]{:S(2)}, u32[]{:S(2)}) collective-permute-start(bf16[192,128]{1,0:T(8,128)(2,1)S(1)} %slice.307), channel_id=1, source_target_pairs={{0,128},{128,256},{256,384},{384,0},{1,129},{129,257},{257,385},{3... | collective-permute-start | bytes 147464 | tf_op jit(solution)/shard_map/ppermute | solution.py:22
  180.4 1.9 collective-permute-start.15
  184.8 6.6 %collective-permute-done.15 = bf16[192,128]{1,0:T(8,128)(2,1)S(1)} collective-permute-done((bf16[192,128]{1,0:T(8,128)(2,1)S(1)}, bf16[192,128]{1,0:T(8,128)(2,1)S(1)}, u32[]{:S(2)}, u32[]{:S(2)}) %collective-permute-start.15) | collective-permute-done | bytes 49184 | tf_op jit(solution)/shard_map/ppermute | solution.py:26
  (145 shorter events, 21.4 us)
Async XLA Ops:
  0.6 0.9 copy-start
  0.7 4.6 %copy-start.5 = (bf16[1,72,768]{2,1,0:T(8,128)(2,1)S(1)}, bf16[1,72,768]{2,1,0:T(8,128)(2,1)}, u32[]{:S(2)}) copy-start(bf16[1,72,768]{2,1,0:T(8,128)(2,1)} %param.14) | copy-start | bytes 331780
  2.7 3.0 %copy-start.3 = (bf16[1,1,2,768,256]{4,3,2,1,0:T(8,128)(2,1)S(1)}, bf16[1,1,2,768,256]{4,3,2,1,0:T(8,128)(2,1)}, u32[]{:S(2)}) copy-start(bf16[1,1,2,768,256]{4,3,2,1,0:T(8,128)(2,1)} %param.13) | copy-start | bytes 2359300
  6.0 14.0 %copy-start.1 = (f32[1,2,24,2048]{3,2,1,0:T(8,128)S(1)}, f32[1,2,24,2048]{3,2,1,0:T(8,128)}, u32[]{:S(2)}) copy-start(f32[1,2,24,2048]{3,2,1,0:T(8,128)} %param.17) | copy-start | bytes 1179652
  6.1 28.0 %collective-permute-start.2 = (bf16[292,128]{1,0:T(8,128)(2,1)S(1)}, bf16[292,128]{1,0:T(8,128)(2,1)S(1)}, u32[]{:S(2)}, u32[]{:S(2)}) collective-permute-start(bf16[292,128]{1,0:T(8,128)(2,1)S(1)} %pad_maximum_fusion.12), channel_id=1, source_target_pairs={{0,384},{128,0},{256,128},{384,256},{1,385},{129,1},{257,129},{385... | collective-permute-start | bytes 224264 | tf_op jit(solution)/shard_map/ppermute | solution.py:26
  18.1 13.5 %collective-permute-start = (bf16[291,128]{1,0:T(8,128)(2,1)S(1)}, bf16[291,128]{1,0:T(8,128)(2,1)S(1)}, u32[]{:S(2)}, u32[]{:S(2)}) collective-permute-start(bf16[291,128]{1,0:T(8,128)(2,1)S(1)} %pad_maximum_fusion.11), channel_id=1, source_target_pairs={{0,128},{128,256},{256,384},{384,0},{1,129},{129,257},{257,385},{3... | collective-permute-start | bytes 223496 | tf_op jit(solution)/shard_map/ppermute | solution.py:22
  20.0 22.7 %copy-start.2 = (f32[1,2,24,2048]{3,2,1,0:T(8,128)S(1)}, f32[1,2,24,2048]{3,2,1,0:T(8,128)}, u32[]{:S(2)}) copy-start(f32[1,2,24,2048]{3,2,1,0:T(8,128)} %param.21) | copy-start | bytes 1179652
  32.2 13.4 %collective-permute-start.1 = (bf16[615,128]{1,0:T(8,128)(2,1)}, bf16[615,128]{1,0:T(8,128)(2,1)S(1)}, u32[]{:S(2)}, u32[]{:S(2)}) collective-permute-start(bf16[615,128]{1,0:T(8,128)(2,1)} %pad_maximum_fusion.6), channel_id=1, source_target_pairs={{0,128},{128,256},{256,384},{384,0},{1,129},{129,257},{257,385},{3... | collective-permute-start | bytes 472328 | tf_op jit(solution)/shard_map/ppermute | solution.py:22
  34.9 12.2 %collective-permute-start.3 = (bf16[615,128]{1,0:T(8,128)(2,1)}, bf16[615,128]{1,0:T(8,128)(2,1)}, u32[]{:S(2)}, u32[]{:S(2)}) collective-permute-start(bf16[615,128]{1,0:T(8,128)(2,1)} %pad_maximum_fusion.7), channel_id=1, source_target_pairs={{0,384},{128,0},{256,128},{384,256},{1,385},{129,1},{257,129},{385... | collective-permute-start | bytes 472328 | tf_op jit(solution)/shard_map/ppermute | solution.py:26
  48.9 23.7 %copy-start.6 = (f32[72,192]{1,0:T(8,128)S(1)}, f32[72,192]{1,0:T(8,128)}, u32[]{:S(2)}) copy-start(f32[72,192]{1,0:T(8,128)} %param.18) | copy-start | bytes 165892
  48.9 23.7 %copy-start.7 = (f32[72,192]{1,0:T(8,128)S(1)}, f32[72,192]{1,0:T(8,128)}, u32[]{:S(2)}) copy-start(f32[72,192]{1,0:T(8,128)} %param.22) | copy-start | bytes 165892
  49.0 24.2 %copy-start.9 = (f32[18,192]{1,0:T(8,128)S(1)}, f32[18,192]{1,0:T(8,128)}, u32[]{:S(2)}) copy-start(f32[18,192]{1,0:T(8,128)} %param.19) | copy-start | bytes 41476
  49.0 24.2 %copy-start.10 = (f32[18,192]{1,0:T(8,128)S(1)}, f32[18,192]{1,0:T(8,128)}, u32[]{:S(2)}) copy-start(f32[18,192]{1,0:T(8,128)} %param.23) | copy-start | bytes 41476
  49.8 46.7 %all-to-all-start = ((f32[8,24,256]{2,1,0:T(8,128)}), f32[8,24,256]{2,1,0:T(8,128)S(1)}, u32[]{:S(2)}, u32[]{:S(2)}) async-start(f32[8,24,256]{2,1,0:T(8,128)} %all_to_all.40), calls=%async_computation | async-start | bytes 393216 | tf_op jit(solution)/shard_map/all_to_all | solution.py:134
  62.8 11.1 %collective-permute-start.4 = (bf16[192,128]{1,0:T(8,128)(2,1)S(1)}, bf16[192,128]{1,0:T(8,128)(2,1)S(1)}, u32[]{:S(2)}, u32[]{:S(2)}) collective-permute-start(bf16[192,128]{1,0:T(8,128)(2,1)S(1)} %get-tuple-element.67), channel_id=1, source_target_pairs={{0,128},{128,256},{256,384},{384,0},{1,129},{129,257},{257,385},{3... | collective-permute-start | bytes 147464 | tf_op jit(solution)/shard_map/ppermute | solution.py:22
  70.6 11.1 %collective-permute-start.6 = (bf16[192,128]{1,0:T(8,128)(2,1)S(1)}, bf16[192,128]{1,0:T(8,128)(2,1)S(1)}, u32[]{:S(2)}, u32[]{:S(2)}) collective-permute-start(bf16[192,128]{1,0:T(8,128)(2,1)S(1)} %get-tuple-element.69), channel_id=1, source_target_pairs={{0,384},{128,0},{256,128},{384,256},{1,385},{129,1},{257,129},{385... | collective-permute-start | bytes 147464 | tf_op jit(solution)/shard_map/ppermute | solution.py:26
  81.7 13.3 %collective-permute-start.7 = (bf16[384,128]{1,0:T(8,128)(2,1)S(1)}, bf16[384,128]{1,0:T(8,128)(2,1)S(1)}, u32[]{:S(2)}, u32[]{:S(2)}) collective-permute-start(bf16[384,128]{1,0:T(8,128)(2,1)S(1)} %pad_maximum_fusion.10), channel_id=1, source_target_pairs={{0,384},{128,0},{256,128},{384,256},{1,385},{129,1},{257,129},{385... | collective-permute-start | bytes 294920 | tf_op jit(solution)/shard_map/ppermute | solution.py:26
  84.6 20.2 %copy-start.4 = (f32[64,192]{1,0:T(8,128)S(1)}, f32[64,192]{1,0:T(8,128)}, u32[]{:S(2)}) copy-start(f32[64,192]{1,0:T(8,128)} %param.20) | copy-start | bytes 147460
  84.6 20.2 %copy-start.8 = (f32[64,192]{1,0:T(8,128)S(1)}, f32[64,192]{1,0:T(8,128)}, u32[]{:S(2)}) copy-start(f32[64,192]{1,0:T(8,128)} %param.24) | copy-start | bytes 147460
  84.7 11.1 %collective-permute-start.5 = (bf16[384,128]{1,0:T(8,128)(2,1)S(1)}, bf16[384,128]{1,0:T(8,128)(2,1)S(1)}, u32[]{:S(2)}, u32[]{:S(2)}) collective-permute-start(bf16[384,128]{1,0:T(8,128)(2,1)S(1)} %pad_maximum_fusion.9), channel_id=1, source_target_pairs={{0,128},{128,256},{256,384},{384,0},{1,129},{129,257},{257,385},{3... | collective-permute-start | bytes 294920 | tf_op jit(solution)/shard_map/ppermute | solution.py:22
  96.5 15.0 %all-to-all-start.1 = ((f32[8,24,256]{2,1,0:T(8,128)}), f32[8,24,256]{2,1,0:T(8,128)S(1)}, u32[]{:S(2)}, u32[]{:S(2)}) async-start(f32[8,24,256]{2,1,0:T(8,128)} %all_to_all.42), calls=%async_computation.1 | async-start | bytes 393216 | tf_op jit(solution)/shard_map/all_to_all | solution.py:134
  111.5 10.0 %all-to-all-start.2 = ((bf16[24,8,256]{2,0,1:T(8,128)(2,1)}), bf16[24,8,256]{2,0,1:T(8,128)(2,1)S(1)}, u32[]{:S(2)}, u32[]{:S(2)}) async-start(bf16[24,8,256]{2,0,1:T(8,128)(2,1)} %fusion.12), calls=%async_computation.2 | async-start | bytes 196608 | tf_op jit(solution)/shard_map/all_to_all | solution.py:137
  121.6 37.2 %all-to-all-start.3 = ((bf16[24,8,256]{2,0,1:T(8,128)(2,1)}), bf16[24,8,256]{2,0,1:T(8,128)(2,1)S(1)}, u32[]{:S(2)}, u32[]{:S(2)}) async-start(bf16[24,8,256]{2,0,1:T(8,128)(2,1)} %fusion.7), calls=%async_computation.3 | async-start | bytes 196608 | tf_op jit(solution)/shard_map/all_to_all | solution.py:137
  126.1 15.4 %collective-permute-start.9 = (bf16[615,128]{1,0:T(8,128)(2,1)S(1)}, bf16[615,128]{1,0:T(8,128)(2,1)S(1)}, u32[]{:S(2)}, u32[]{:S(2)}) collective-permute-start(bf16[615,128]{1,0:T(8,128)(2,1)S(1)} %pad_maximum_fusion.8), channel_id=1, source_target_pairs={{0,128},{128,256},{256,384},{384,0},{1,129},{129,257},{257,385},{3... | collective-permute-start | bytes 472328 | tf_op jit(solution)/shard_map/ppermute | solution.py:22
  133.3 21.8 %collective-permute-start.8 = (bf16[615,128]{1,0:T(8,128)(2,1)S(1)}, bf16[615,128]{1,0:T(8,128)(2,1)S(1)}, u32[]{:S(2)}, u32[]{:S(2)}) collective-permute-start(bf16[615,128]{1,0:T(8,128)(2,1)S(1)} %pad_maximum_fusion.8), channel_id=1, source_target_pairs={{0,384},{128,0},{256,128},{384,256},{1,385},{129,1},{257,129},{385... | collective-permute-start | bytes 472328 | tf_op jit(solution)/shard_map/ppermute | solution.py:26
  141.5 27.1 %collective-permute-start.10 = (bf16[307,128]{1,0:T(8,128)(2,1)S(1)}, bf16[307,128]{1,0:T(8,128)(2,1)S(1)}, u32[]{:S(2)}, u32[]{:S(2)}) collective-permute-start(bf16[307,128]{1,0:T(8,128)(2,1)S(1)} %slice.305), channel_id=1, source_target_pairs={{0,128},{128,256},{256,384},{384,0},{1,129},{129,257},{257,385},{3... | collective-permute-start | bytes 235784 | tf_op jit(solution)/shard_map/ppermute | solution.py:22
  155.2 13.5 %collective-permute-start.11 = (bf16[308,128]{1,0:T(8,128)(2,1)S(1)}, bf16[308,128]{1,0:T(8,128)(2,1)S(1)}, u32[]{:S(2)}, u32[]{:S(2)}) collective-permute-start(bf16[308,128]{1,0:T(8,128)(2,1)S(1)} %slice.306), channel_id=1, source_target_pairs={{0,384},{128,0},{256,128},{384,256},{1,385},{129,1},{257,129},{385... | collective-permute-start | bytes 236552 | tf_op jit(solution)/shard_map/ppermute | solution.py:26
  158.9 13.2 %collective-permute-start.13 = (bf16[384,128]{1,0:T(8,128)(2,1)S(1)}, bf16[384,128]{1,0:T(8,128)(2,1)S(1)}, u32[]{:S(2)}, u32[]{:S(2)}) collective-permute-start(bf16[384,128]{1,0:T(8,128)(2,1)S(1)} %reshape.310), channel_id=1, source_target_pairs={{0,128},{128,256},{256,384},{384,0},{1,129},{129,257},{257,385},{3... | collective-permute-start | bytes 294920 | tf_op jit(solution)/shard_map/ppermute | solution.py:22
  165.9 14.4 %collective-permute-start.12 = (bf16[384,128]{1,0:T(8,128)(2,1)S(1)}, bf16[384,128]{1,0:T(8,128)(2,1)S(1)}, u32[]{:S(2)}, u32[]{:S(2)}) collective-permute-start(bf16[384,128]{1,0:T(8,128)(2,1)S(1)} %reshape.310), channel_id=1, source_target_pairs={{0,384},{128,0},{256,128},{384,256},{1,385},{129,1},{257,129},{385... | collective-permute-start | bytes 294920 | tf_op jit(solution)/shard_map/ppermute | solution.py:26
  172.1 12.7 %collective-permute-start.14 = (bf16[192,128]{1,0:T(8,128)(2,1)S(1)}, bf16[192,128]{1,0:T(8,128)(2,1)S(1)}, u32[]{:S(2)}, u32[]{:S(2)}) collective-permute-start(bf16[192,128]{1,0:T(8,128)(2,1)S(1)} %slice.307), channel_id=1, source_target_pairs={{0,128},{128,256},{256,384},{384,0},{1,129},{129,257},{257,385},{3... | collective-permute-start | bytes 147464 | tf_op jit(solution)/shard_map/ppermute | solution.py:22
  180.4 11.1 %collective-permute-start.15 = (bf16[192,128]{1,0:T(8,128)(2,1)S(1)}, bf16[192,128]{1,0:T(8,128)(2,1)S(1)}, u32[]{:S(2)}, u32[]{:S(2)}) collective-permute-start(bf16[192,128]{1,0:T(8,128)(2,1)S(1)} %slice.308), channel_id=1, source_target_pairs={{0,384},{128,0},{256,128},{384,256},{1,385},{129,1},{257,129},{385... | collective-permute-start | bytes 147464 | tf_op jit(solution)/shard_map/ppermute | solution.py:26

commit v6 on v4

--- a/solution.py
+++ b/solution.py
@@ -129,7 +129,9 @@
     nhalf = parts[3].shape[0] // 2
     coefficient = (parts[3][:nhalf] + parts[3][nhalf:]).reshape(partial_value.shape)
 
-    expert_sum = lax.all_to_all(ex_sum, "mdl", split_axis=1, concat_axis=2, tiled=True)
+    expert_sum = lax.all_to_all(
+        ex_sum.astype(jnp.bfloat16), "mdl", split_axis=1, concat_axis=2, tiled=True
+    ).astype(jnp.float32)
     grad_experts = outer_experts[0] - expert_sum / groups
     grad_dense = outer_dense - dense_sum / groups
     grad_small = outer_small - small_sum / groups

time: 158 us -> 153 us (0.968)
  waiting for transfers between devices: 71.9 us -> 66.4 us
    all_to_all x1, waiting for transfers between devices: 10.2 us -> 5.46 us  [on_device(): lax.all_to_all(ex_sum.astype(jnp.bfloat16), 'mdl', split_axis=1, concat_a...]
where the time goes in v6:
time: 153 us; the launch traced here: 152 us
  waiting for transfers between devices  66.4 us (43%)
  starting transfers between devices  61.7 us (40%)
  local copies, waits for them, and re-layouts  15.8 us (10%)
  other arithmetic  3.28 us (2%)
  matrix products  3.16 us (2%)
    ppermute x4, starting transfers between devices, to_next(): lax.ppermute(x, 'rep', [(i, (i + 1) % groups) for i in range(groups)])  35.5 us
    ppermute x4, waiting for transfers between devices, to_next(): lax.ppermute(x, 'rep', [(i, (i + 1) % groups) for i in range(groups)])  30 us
    ppermute x4, waiting for transfers between devices, to_prev(): lax.ppermute(x, 'rep', [(i, (i - 1) % groups) for i in range(groups)])  26.2 us
    ppermute x4, starting transfers between devices, to_prev(): lax.ppermute(x, 'rep', [(i, (i - 1) % groups) for i in range(groups)])  15.4 us
    all_to_all x1, starting transfers between devices, on_device(): lax.all_to_all(ex_sum.astype(jnp.bfloat16), 'mdl', split_axis=1, concat_a...  5.65 us
    all_to_all x1, waiting for transfers between devices, on_device(): lax.all_to_all(ex_sum.astype(jnp.bfloat16), 'mdl', split_axis=1, concat_a...  5.46 us
    all_to_all x1, starting transfers between devices, on_device(): lax.all_to_all(expert_outer.astype(jnp.bfloat16), 'mdl', split_axis=2, co...  5.08 us
    unnamed x24, local copies, waits for them, and re-layouts  5.04 us
  transfers between devices with their start and end apart: 10, of which 10 were waited for; matrix products, arithmetic and copies ran while one was open for 3% of the time, Pallas kernels for 0%

profile of v6, /device:TPU:1, one launch (start us, length us, event | category | flops | bytes accessed | tf_op | source)
XLA Modules:
  0.0 151.8 jit_solution(17911756644763333592)
XLA Ops:
  0.7 0.9 copy-done
  1.6 1.1 convolution_bitcast_fusion
  2.7 1.1 subtract_convert_fusion
  4.2 1.2 copy.65
  7.2 9.6 %collective-permute-start = (bf16[483,128]{1,0:T(8,128)(2,1)S(1)}, bf16[483,128]{1,0:T(8,128)(2,1)S(1)}, u32[]{:S(2)}, u32[]{:S(2)}) collective-permute-start(bf16[483,128]{1,0:T(8,128)(2,1)S(1)} %pad_maximum_fusion.5), channel_id=1, source_target_pairs={{0,128},{128,256},{256,384},{384,0},{1,129},{129,257},{257,385},{3... | collective-permute-start | bytes 370952 | tf_op jit(solution)/shard_map/ppermute | solution.py:22
  16.9 5.6 %collective-permute-start.2 = (bf16[484,128]{1,0:T(8,128)(2,1)S(1)}, bf16[484,128]{1,0:T(8,128)(2,1)S(1)}, u32[]{:S(2)}, u32[]{:S(2)}) collective-permute-start(bf16[484,128]{1,0:T(8,128)(2,1)S(1)} %pad_maximum_fusion.6), channel_id=1, source_target_pairs={{0,384},{128,0},{256,128},{384,256},{1,385},{129,1},{257,129},{385... | collective-permute-start | bytes 371720 | tf_op jit(solution)/shard_map/ppermute | solution.py:26
  23.3 12.8 %collective-permute-start.1 = (bf16[999,128]{1,0:T(8,128)(2,1)S(1)}, bf16[999,128]{1,0:T(8,128)(2,1)S(1)}, u32[]{:S(2)}, u32[]{:S(2)}) collective-permute-start(bf16[999,128]{1,0:T(8,128)(2,1)S(1)} %pad_maximum_fusion.2), channel_id=1, source_target_pairs={{0,128},{128,256},{256,384},{384,0},{1,129},{129,257},{257,385},{3... | collective-permute-start | bytes 767240 | tf_op jit(solution)/shard_map/ppermute | solution.py:22
  36.1 1.1 collective-permute-done.2
  37.3 4.0 %collective-permute-start.3 = (bf16[999,128]{1,0:T(8,128)(2,1)S(1)}, bf16[999,128]{1,0:T(8,128)(2,1)S(1)}, u32[]{:S(2)}, u32[]{:S(2)}) collective-permute-start(bf16[999,128]{1,0:T(8,128)(2,1)S(1)} %pad_maximum_fusion.3), channel_id=1, source_target_pairs={{0,384},{128,0},{256,128},{384,256},{1,385},{129,1},{257,129},{385... | collective-permute-start | bytes 767240 | tf_op jit(solution)/shard_map/ppermute | solution.py:26
  41.4 15.7 %collective-permute-done.1 = bf16[999,128]{1,0:T(8,128)(2,1)S(1)} collective-permute-done((bf16[999,128]{1,0:T(8,128)(2,1)S(1)}, bf16[999,128]{1,0:T(8,128)(2,1)S(1)}, u32[]{:S(2)}, u32[]{:S(2)}) %collective-permute-start.1) | collective-permute-done | bytes 255776 | tf_op jit(solution)/shard_map/ppermute | solution.py:22
  57.0 8.1 %collective-permute-done.3 = bf16[999,128]{1,0:T(8,128)(2,1)S(1)} collective-permute-done((bf16[999,128]{1,0:T(8,128)(2,1)S(1)}, bf16[999,128]{1,0:T(8,128)(2,1)S(1)}, u32[]{:S(2)}, u32[]{:S(2)}) %collective-permute-start.3) | collective-permute-done | bytes 255776 | tf_op jit(solution)/shard_map/ppermute | solution.py:26
  65.4 0.9 copy.71
  66.2 5.6 %all-to-all-start = ((bf16[2,192,256]{2,0,1:T(2,128)(2,1)}), bf16[2,192,256]{2,0,1:T(2,128)(2,1)S(1)}, u32[]{:S(2)}, u32[]{:S(2)}) async-start(bf16[2,192,256]{2,0,1:T(2,128)(2,1)} %copy.71), calls=%async_computation | async-start | bytes 393216 | tf_op jit(solution)/shard_map/all_to_all | solution.py:132
  72.0 0.9 fusion.17
  73.0 5.5 %all-to-all-done = bf16[2,192,256]{2,0,1:T(2,128)(2,1)S(1)} async-done(((bf16[2,192,256]{2,0,1:T(2,128)(2,1)}), bf16[2,192,256]{2,0,1:T(2,128)(2,1)S(1)}, u32[]{:S(2)}, u32[]{:S(2)}) %all-to-all-start) | async-done | bytes 196640 | tf_op jit(solution)/shard_map/all_to_all | solution.py:132
  78.6 0.7 copy.75
  79.4 2.0 %reshape.176 = bf16[8,2,6144]{2,1,0:T(2,128)(2,1)} reshape(bf16[2048,2,24]{2,1,0:T(2,128)(2,1)S(1)} %bitcast.93) | data formatting | bytes 393216
  81.4 5.1 %all-to-all-start.1 = ((bf16[8,2,6144]{2,1,0:T(2,128)(2,1)}), bf16[8,2,6144]{2,1,0:T(2,128)(2,1)S(1)}, u32[]{:S(2)}, u32[]{:S(2)}) async-start(bf16[8,2,6144]{2,1,0:T(2,128)(2,1)} %reshape.176), calls=%async_computation.1 | async-start | bytes 393216 | tf_op jit(solution)/shard_map/all_to_all | solution.py:145
  88.3 4.7 %all-to-all-done.1 = bf16[8,2,6144]{2,1,0:T(2,128)(2,1)S(1)} async-done(((bf16[8,2,6144]{2,1,0:T(2,128)(2,1)}), bf16[8,2,6144]{2,1,0:T(2,128)(2,1)S(1)}, u32[]{:S(2)}, u32[]{:S(2)}) %all-to-all-start.1) | async-done | bytes 196640 | tf_op jit(solution)/shard_map/all_to_all | solution.py:145
  93.0 1.5 reshape.177
  95.3 6.2 %collective-permute-start.5 = (bf16[999,128]{1,0:T(8,128)(2,1)S(1)}, bf16[999,128]{1,0:T(8,128)(2,1)S(1)}, u32[]{:S(2)}, u32[]{:S(2)}) collective-permute-start(bf16[999,128]{1,0:T(8,128)(2,1)S(1)} %pad_maximum_fusion.4), channel_id=1, source_target_pairs={{0,128},{128,256},{256,384},{384,0},{1,129},{129,257},{257,385},{3... | collective-permute-start | bytes 767240 | tf_op jit(solution)/shard_map/ppermute | solution.py:22
  101.5 3.0 %collective-permute-start.4 = (bf16[999,128]{1,0:T(8,128)(2,1)S(1)}, bf16[999,128]{1,0:T(8,128)(2,1)S(1)}, u32[]{:S(2)}, u32[]{:S(2)}) collective-permute-start(bf16[999,128]{1,0:T(8,128)(2,1)S(1)} %pad_maximum_fusion.4), channel_id=1, source_target_pairs={{0,384},{128,0},{256,128},{384,256},{1,385},{129,1},{257,129},{385... | collective-permute-start | bytes 767240 | tf_op jit(solution)/shard_map/ppermute | solution.py:26
  104.8 12.9 %collective-permute-done.5 = bf16[999,128]{1,0:T(8,128)(2,1)S(1)} collective-permute-done((bf16[999,128]{1,0:T(8,128)(2,1)S(1)}, bf16[999,128]{1,0:T(8,128)(2,1)S(1)}, u32[]{:S(2)}, u32[]{:S(2)}) %collective-permute-start.5) | collective-permute-done | bytes 255776 | tf_op jit(solution)/shard_map/ppermute | solution.py:22
  117.6 6.9 %collective-permute-start.6 = (bf16[499,128]{1,0:T(8,128)(2,1)S(1)}, bf16[499,128]{1,0:T(8,128)(2,1)S(1)}, u32[]{:S(2)}, u32[]{:S(2)}) collective-permute-start(bf16[499,128]{1,0:T(8,128)(2,1)S(1)} %slice.229), channel_id=1, source_target_pairs={{0,128},{128,256},{256,384},{384,0},{1,129},{129,257},{257,385},{3... | collective-permute-start | bytes 383240 | tf_op jit(solution)/shard_map/ppermute | solution.py:22
  124.6 7.0 %collective-permute-done.4 = bf16[999,128]{1,0:T(8,128)(2,1)S(1)} collective-permute-done((bf16[999,128]{1,0:T(8,128)(2,1)S(1)}, bf16[999,128]{1,0:T(8,128)(2,1)S(1)}, u32[]{:S(2)}, u32[]{:S(2)}) %collective-permute-start.4) | collective-permute-done | bytes 255776 | tf_op jit(solution)/shard_map/ppermute | solution.py:26
  131.6 2.9 %collective-permute-start.7 = (bf16[500,128]{1,0:T(8,128)(2,1)S(1)}, bf16[500,128]{1,0:T(8,128)(2,1)S(1)}, u32[]{:S(2)}, u32[]{:S(2)}) collective-permute-start(bf16[500,128]{1,0:T(8,128)(2,1)S(1)} %slice.230), channel_id=1, source_target_pairs={{0,384},{128,0},{256,128},{384,256},{1,385},{129,1},{257,129},{385... | collective-permute-start | bytes 384008 | tf_op jit(solution)/shard_map/ppermute | solution.py:26
  134.5 1.0 multiply_subtract_fusion
  135.5 0.9 collective-permute-done.6
  136.3 10.0 %collective-permute-done.7 = bf16[500,128]{1,0:T(8,128)(2,1)S(1)} collective-permute-done((bf16[500,128]{1,0:T(8,128)(2,1)S(1)}, bf16[500,128]{1,0:T(8,128)(2,1)S(1)}, u32[]{:S(2)}, u32[]{:S(2)}) %collective-permute-start.7) | collective-permute-done | bytes 128032 | tf_op jit(solution)/shard_map/ppermute | solution.py:26
  147.2 0.8 reshape.172
  149.6 0.8 reshape.170
  150.8 0.9 copy.77
  (107 shorter events, 9.1 us)
Async XLA Ops:
  0.6 0.9 copy-start
  5.4 0.9 copy-start.4
  5.4 1.3 copy-start.8
  7.2 16.0 %collective-permute-start = (bf16[483,128]{1,0:T(8,128)(2,1)S(1)}, bf16[483,128]{1,0:T(8,128)(2,1)S(1)}, u32[]{:S(2)}, u32[]{:S(2)}) collective-permute-start(bf16[483,128]{1,0:T(8,128)(2,1)S(1)} %pad_maximum_fusion.5), channel_id=1, source_target_pairs={{0,128},{128,256},{256,384},{384,0},{1,129},{129,257},{257,385},{3... | collective-permute-start | bytes 370952 | tf_op jit(solution)/shard_map/ppermute | solution.py:22
  16.9 20.3 %collective-permute-start.2 = (bf16[484,128]{1,0:T(8,128)(2,1)S(1)}, bf16[484,128]{1,0:T(8,128)(2,1)S(1)}, u32[]{:S(2)}, u32[]{:S(2)}) collective-permute-start(bf16[484,128]{1,0:T(8,128)(2,1)S(1)} %pad_maximum_fusion.6), channel_id=1, source_target_pairs={{0,384},{128,0},{256,128},{384,256},{1,385},{129,1},{257,129},{385... | collective-permute-start | bytes 371720 | tf_op jit(solution)/shard_map/ppermute | solution.py:26
  23.3 33.7 %collective-permute-start.1 = (bf16[999,128]{1,0:T(8,128)(2,1)S(1)}, bf16[999,128]{1,0:T(8,128)(2,1)S(1)}, u32[]{:S(2)}, u32[]{:S(2)}) collective-permute-start(bf16[999,128]{1,0:T(8,128)(2,1)S(1)} %pad_maximum_fusion.2), channel_id=1, source_target_pairs={{0,128},{128,256},{256,384},{384,0},{1,129},{129,257},{257,385},{3... | collective-permute-start | bytes 767240 | tf_op jit(solution)/shard_map/ppermute | solution.py:22
  37.3 27.8 %collective-permute-start.3 = (bf16[999,128]{1,0:T(8,128)(2,1)S(1)}, bf16[999,128]{1,0:T(8,128)(2,1)S(1)}, u32[]{:S(2)}, u32[]{:S(2)}) collective-permute-start(bf16[999,128]{1,0:T(8,128)(2,1)S(1)} %pad_maximum_fusion.3), channel_id=1, source_target_pairs={{0,384},{128,0},{256,128},{384,256},{1,385},{129,1},{257,129},{385... | collective-permute-start | bytes 767240 | tf_op jit(solution)/shard_map/ppermute | solution.py:26
  65.2 6.8 %copy-start.3 = (f32[64,192]{1,0:T(8,128)S(1)}, f32[64,192]{1,0:T(8,128)}, u32[]{:S(2)}) copy-start(f32[64,192]{1,0:T(8,128)} %param.20) | copy-start | bytes 147460
  65.2 6.8 %copy-start.7 = (f32[64,192]{1,0:T(8,128)S(1)}, f32[64,192]{1,0:T(8,128)}, u32[]{:S(2)}) copy-start(f32[64,192]{1,0:T(8,128)} %param.24) | copy-start | bytes 147460
  66.2 12.2 %all-to-all-start = ((bf16[2,192,256]{2,0,1:T(2,128)(2,1)}), bf16[2,192,256]{2,0,1:T(2,128)(2,1)S(1)}, u32[]{:S(2)}, u32[]{:S(2)}) async-start(bf16[2,192,256]{2,0,1:T(2,128)(2,1)} %copy.71), calls=%async_computation | async-start | bytes 393216 | tf_op jit(solution)/shard_map/all_to_all | solution.py:132
  71.9 6.6 %copy-start.1 = (f32[1,2,24,2048]{3,2,1,0:T(8,128)S(1)}, f32[1,2,24,2048]{3,2,1,0:T(8,128)}, u32[]{:S(2)}) copy-start(f32[1,2,24,2048]{3,2,1,0:T(8,128)} %param.17) | copy-start | bytes 1179652
  71.9 6.6 %copy-start.2 = (f32[1,2,24,2048]{3,2,1,0:T(8,128)S(1)}, f32[1,2,24,2048]{3,2,1,0:T(8,128)}, u32[]{:S(2)}) copy-start(f32[1,2,24,2048]{3,2,1,0:T(8,128)} %param.21) | copy-start | bytes 1179652
  79.4 7.3 %copy-start.5 = (f32[72,192]{1,0:T(8,128)S(1)}, f32[72,192]{1,0:T(8,128)}, u32[]{:S(2)}) copy-start(f32[72,192]{1,0:T(8,128)} %param.18) | copy-start | bytes 165892
  79.4 7.3 %copy-start.6 = (f32[72,192]{1,0:T(8,128)S(1)}, f32[72,192]{1,0:T(8,128)}, u32[]{:S(2)}) copy-start(f32[72,192]{1,0:T(8,128)} %param.22) | copy-start | bytes 165892
  79.4 8.2 %copy-start.9 = (f32[18,192]{1,0:T(8,128)S(1)}, f32[18,192]{1,0:T(8,128)}, u32[]{:S(2)}) copy-start(f32[18,192]{1,0:T(8,128)} %param.19) | copy-start | bytes 41476
  79.4 8.2 %copy-start.10 = (f32[18,192]{1,0:T(8,128)S(1)}, f32[18,192]{1,0:T(8,128)}, u32[]{:S(2)}) copy-start(f32[18,192]{1,0:T(8,128)} %param.23) | copy-start | bytes 41476
  81.4 11.6 %all-to-all-start.1 = ((bf16[8,2,6144]{2,1,0:T(2,128)(2,1)}), bf16[8,2,6144]{2,1,0:T(2,128)(2,1)S(1)}, u32[]{:S(2)}, u32[]{:S(2)}) async-start(bf16[8,2,6144]{2,1,0:T(2,128)(2,1)} %reshape.176), calls=%async_computation.1 | async-start | bytes 393216 | tf_op jit(solution)/shard_map/all_to_all | solution.py:145
  95.3 22.3 %collective-permute-start.5 = (bf16[999,128]{1,0:T(8,128)(2,1)S(1)}, bf16[999,128]{1,0:T(8,128)(2,1)S(1)}, u32[]{:S(2)}, u32[]{:S(2)}) collective-permute-start(bf16[999,128]{1,0:T(8,128)(2,1)S(1)} %pad_maximum_fusion.4), channel_id=1, source_target_pairs={{0,128},{128,256},{256,384},{384,0},{1,129},{129,257},{257,385},{3... | collective-permute-start | bytes 767240 | tf_op jit(solution)/shard_map/ppermute | solution.py:22
  101.5 30.0 %collective-permute-start.4 = (bf16[999,128]{1,0:T(8,128)(2,1)S(1)}, bf16[999,128]{1,0:T(8,128)(2,1)S(1)}, u32[]{:S(2)}, u32[]{:S(2)}) collective-permute-start(bf16[999,128]{1,0:T(8,128)(2,1)S(1)} %pad_maximum_fusion.4), channel_id=1, source_target_pairs={{0,384},{128,0},{256,128},{384,256},{1,385},{129,1},{257,129},{385... | collective-permute-start | bytes 767240 | tf_op jit(solution)/shard_map/ppermute | solution.py:26
  117.6 18.7 %collective-permute-start.6 = (bf16[499,128]{1,0:T(8,128)(2,1)S(1)}, bf16[499,128]{1,0:T(8,128)(2,1)S(1)}, u32[]{:S(2)}, u32[]{:S(2)}) collective-permute-start(bf16[499,128]{1,0:T(8,128)(2,1)S(1)} %slice.229), channel_id=1, source_target_pairs={{0,128},{128,256},{256,384},{384,0},{1,129},{129,257},{257,385},{3... | collective-permute-start | bytes 383240 | tf_op jit(solution)/shard_map/ppermute | solution.py:22
  131.6 14.7 %collective-permute-start.7 = (bf16[500,128]{1,0:T(8,128)(2,1)S(1)}, bf16[500,128]{1,0:T(8,128)(2,1)S(1)}, u32[]{:S(2)}, u32[]{:S(2)}) collective-permute-start(bf16[500,128]{1,0:T(8,128)(2,1)S(1)} %slice.230), channel_id=1, source_target_pairs={{0,384},{128,0},{256,128},{384,256},{1,385},{129,1},{257,129},{385... | collective-permute-start | bytes 384008 | tf_op jit(solution)/shard_map/ppermute | solution.py:26

commit v7 on v6

--- a/solution.py
+++ b/solution.py
@@ -36,23 +36,29 @@
     rh = raw_rows // 2
     f32 = jnp.float32
     bf = send.dtype
-    a = to_next(jnp.concatenate([rel[2][:h], rel[2][m : m + rh]]), groups)
-    b = to_prev(jnp.concatenate([rel[2][h:m], rel[2][m + rh :]]), groups)
-    x = to_next(
-        jnp.concatenate(
-            [(rel[1][:h].astype(f32) + a[:h].astype(f32)).astype(bf), rel[1][h:], a[h:]]
-        ),
+    a = to_next(jnp.concatenate([rel[2][:h], rel[2][m : m + rh], rel[1][h:m], rel[1][m:]]), groups)
+    b = to_prev(jnp.concatenate([rel[2][h:m], rel[2][m + rh :], rel[3][:h], rel[3][m:]]), groups)
+    a_relay, a_pp_relay = a[:h], a[h : h + rh]
+    a_near, a_pp = a[h + rh : h + rh + m - h], a[h + rh + m - h :]
+    b_relay, b_pp_relay = b[: m - h], b[m - h : m - h + raw_rows - rh]
+    b_near, b_pp = b[m - h + raw_rows - rh : m - h + raw_rows - rh + h], b[m - h + raw_rows - rh + h :]
+    c = to_next(
+        jnp.concatenate([(rel[1][:h].astype(f32) + a_relay.astype(f32)).astype(bf), a_pp_relay]),
         groups,
     )
-    y = to_prev(
-        jnp.concatenate(
-            [rel[3][:h], (rel[3][h:m].astype(f32) + b[: m - h].astype(f32)).astype(bf), rel[3][m:], b[m - h :]]
-        ),
+    d = to_prev(
+        jnp.concatenate([(rel[3][h:m].astype(f32) + b_relay.astype(f32)).astype(bf), b_pp_relay]),
         groups,
     )
-    near = rel[0].astype(f32) + x[:k].astype(f32) + y[:k].astype(f32)
-    far_raw = jnp.concatenate([x[k:], y[k:]]).astype(f32)
-    return jnp.concatenate([near[:m], near[m:] + far_raw])
+    first = rel[0][:h].astype(f32) + c[:h].astype(f32) + b_near.astype(f32)
+    second = rel[0][h:m].astype(f32) + a_near.astype(f32) + d[: m - h].astype(f32)
+    raw = (
+        rel[0][m:].astype(f32)
+        + a_pp.astype(f32)
+        + b_pp.astype(f32)
+        + jnp.concatenate([c[h:], d[m - h :]]).astype(f32)
+    )
+    return jnp.concatenate([first, second, raw])
 
 
 def rep_gather(flat, groups):

time: 153 us -> 147 us (0.961)
  waiting for transfers between devices: 66.4 us -> 51.9 us
  starting transfers between devices: 61.7 us -> 71.1 us
    ppermute x4, waiting for transfers between devices: 30 us -> 9.29 us  [to_next(): lax.ppermute(x, 'rep', [(i, (i + 1) % groups) for i in range(groups)])]
    ppermute x4, waiting for transfers between devices: 26.2 us -> 32.5 us  [to_prev(): lax.ppermute(x, 'rep', [(i, (i - 1) % groups) for i in range(groups)])]
    ppermute x4, starting transfers between devices: 35.5 us -> 41.5 us  [to_next(): lax.ppermute(x, 'rep', [(i, (i + 1) % groups) for i in range(groups)])]
    all_to_all x1, starting transfers between devices: 5.65 us -> 8.84 us  [on_device(): lax.all_to_all(ex_sum.astype(jnp.bfloat16), 'mdl', split_axis=1, concat_a...]
  transfers between devices with their start and end apart: 10 -> 10, of which waited for: 10 -> 7; matrix products, arithmetic and copies ran while one was open for 3% -> 3% of each run, Pallas kernels for 0% -> 0%
where the time goes in v7:
time: 147 us; the launch traced here: 146 us
  starting transfers between devices  71.1 us (48%)
  waiting for transfers between devices  51.9 us (35%)
  local copies, waits for them, and re-layouts  14.8 us (10%)
  other arithmetic  3.4 us (2%)
  matrix products  3.17 us (2%)
    ppermute x4, starting transfers between devices, to_next(): lax.ppermute(x, 'rep', [(i, (i + 1) % groups) for i in range(groups)])  41.5 us
    ppermute x4, waiting for transfers between devices, to_prev(): lax.ppermute(x, 'rep', [(i, (i - 1) % groups) for i in range(groups)])  32.5 us
    ppermute x4, starting transfers between devices, to_prev(): lax.ppermute(x, 'rep', [(i, (i - 1) % groups) for i in range(groups)])  15.7 us
    ppermute x4, waiting for transfers between devices, to_next(): lax.ppermute(x, 'rep', [(i, (i + 1) % groups) for i in range(groups)])  9.29 us
    all_to_all x1, starting transfers between devices, on_device(): lax.all_to_all(ex_sum.astype(jnp.bfloat16), 'mdl', split_axis=1, concat_a...  8.84 us
    all_to_all x1, waiting for transfers between devices, on_device(): lax.all_to_all(ex_sum.astype(jnp.bfloat16), 'mdl', split_axis=1, concat_a...  6.22 us
    all_to_all x1, starting transfers between devices, on_device(): lax.all_to_all(expert_outer.astype(jnp.bfloat16), 'mdl', split_axis=2, co...  5.08 us
    unnamed x24, local copies, waits for them, and re-layouts  4.4 us
  transfers between devices with their start and end apart: 10, of which 7 were waited for; matrix products, arithmetic and copies ran while one was open for 3% of the time, Pallas kernels for 0%

profile of v7, /device:TPU:1, one launch (start us, length us, event | category | flops | bytes accessed | tf_op | source)
XLA Modules:
  0.0 145.8 jit_solution(17785608880701081259)
XLA Ops:
  0.7 0.9 copy-done
  1.6 1.1 convolution_bitcast_fusion
  2.7 1.1 subtract_convert_fusion
  4.2 0.9 reshape_squeeze.11
  6.4 9.6 %collective-permute-start = (bf16[999,128]{1,0:T(8,128)(2,1)S(1)}, bf16[999,128]{1,0:T(8,128)(2,1)S(1)}, u32[]{:S(2)}, u32[]{:S(2)}) collective-permute-start(bf16[999,128]{1,0:T(8,128)(2,1)S(1)} %pad_maximum_fusion.2), channel_id=1, source_target_pairs={{0,128},{128,256},{256,384},{384,0},{1,129},{129,257},{257,385},{3... | collective-permute-start | bytes 767240 | tf_op jit(solution)/shard_map/ppermute | solution.py:22
  16.1 5.6 %collective-permute-start.2 = (bf16[999,128]{1,0:T(8,128)(2,1)S(1)}, bf16[999,128]{1,0:T(8,128)(2,1)S(1)}, u32[]{:S(2)}, u32[]{:S(2)}) collective-permute-start(bf16[999,128]{1,0:T(8,128)(2,1)S(1)} %pad_maximum_fusion.3), channel_id=1, source_target_pairs={{0,384},{128,0},{256,128},{384,256},{1,385},{129,1},{257,129},{385... | collective-permute-start | bytes 767240 | tf_op jit(solution)/shard_map/ppermute | solution.py:26
  21.6 5.3 %collective-permute-done = bf16[999,128]{1,0:T(8,128)(2,1)S(1)} collective-permute-done((bf16[999,128]{1,0:T(8,128)(2,1)S(1)}, bf16[999,128]{1,0:T(8,128)(2,1)S(1)}, u32[]{:S(2)}, u32[]{:S(2)}) %collective-permute-start) | collective-permute-done | bytes 255776 | tf_op jit(solution)/shard_map/ppermute | solution.py:22
  27.0 19.5 %collective-permute-start.1 = (bf16[483,128]{1,0:T(8,128)(2,1)S(1)}, bf16[483,128]{1,0:T(8,128)(2,1)S(1)}, u32[]{:S(2)}, u32[]{:S(2)}) collective-permute-start(bf16[483,128]{1,0:T(8,128)(2,1)S(1)} %pad_maximum_fusion.6), channel_id=1, source_target_pairs={{0,128},{128,256},{256,384},{384,0},{1,129},{129,257},{257,385},{3... | collective-permute-start | bytes 370952 | tf_op jit(solution)/shard_map/ppermute | solution.py:22
  46.5 1.1 collective-permute-done.2
  47.7 4.1 %collective-permute-start.3 = (bf16[484,128]{1,0:T(8,128)(2,1)S(1)}, bf16[484,128]{1,0:T(8,128)(2,1)S(1)}, u32[]{:S(2)}, u32[]{:S(2)}) collective-permute-start(bf16[484,128]{1,0:T(8,128)(2,1)S(1)} %pad_maximum_fusion.7), channel_id=1, source_target_pairs={{0,384},{128,0},{256,128},{384,256},{1,385},{129,1},{257,129},{385... | collective-permute-start | bytes 371720 | tf_op jit(solution)/shard_map/ppermute | solution.py:26
  51.9 9.6 %collective-permute-done.3 = bf16[484,128]{1,0:T(8,128)(2,1)S(1)} collective-permute-done((bf16[484,128]{1,0:T(8,128)(2,1)S(1)}, bf16[484,128]{1,0:T(8,128)(2,1)S(1)}, u32[]{:S(2)}, u32[]{:S(2)}) %collective-permute-start.3) | collective-permute-done | bytes 123936 | tf_op jit(solution)/shard_map/ppermute | solution.py:26
  61.7 0.9 copy.71
  62.6 8.8 %all-to-all-start = ((bf16[2,192,256]{2,0,1:T(2,128)(2,1)}), bf16[2,192,256]{2,0,1:T(2,128)(2,1)S(1)}, u32[]{:S(2)}, u32[]{:S(2)}) async-start(bf16[2,192,256]{2,0,1:T(2,128)(2,1)} %copy.71), calls=%async_computation | async-start | bytes 393216 | tf_op jit(solution)/shard_map/all_to_all | solution.py:138
  71.7 6.2 %all-to-all-done = bf16[2,192,256]{2,0,1:T(2,128)(2,1)S(1)} async-done(((bf16[2,192,256]{2,0,1:T(2,128)(2,1)}), bf16[2,192,256]{2,0,1:T(2,128)(2,1)S(1)}, u32[]{:S(2)}, u32[]{:S(2)}) %all-to-all-start) | async-done | bytes 196640 | tf_op jit(solution)/shard_map/all_to_all | solution.py:138
  78.1 0.7 copy.75
  79.0 2.0 %reshape.186 = bf16[8,2,6144]{2,1,0:T(2,128)(2,1)} reshape(bf16[2048,2,24]{2,1,0:T(2,128)(2,1)S(1)} %bitcast.108) | data formatting | bytes 393216
  81.0 5.1 %all-to-all-start.1 = ((bf16[8,2,6144]{2,1,0:T(2,128)(2,1)}), bf16[8,2,6144]{2,1,0:T(2,128)(2,1)S(1)}, u32[]{:S(2)}, u32[]{:S(2)}) async-start(bf16[8,2,6144]{2,1,0:T(2,128)(2,1)} %reshape.186), calls=%async_computation.1 | async-start | bytes 393216 | tf_op jit(solution)/shard_map/all_to_all | solution.py:151
  86.8 0.7 fusion.19
  87.6 0.9 fusion.21
  88.6 3.9 %all-to-all-done.1 = bf16[8,2,6144]{2,1,0:T(2,128)(2,1)S(1)} async-done(((bf16[8,2,6144]{2,1,0:T(2,128)(2,1)}), bf16[8,2,6144]{2,1,0:T(2,128)(2,1)S(1)}, u32[]{:S(2)}, u32[]{:S(2)}) %all-to-all-start.1) | async-done | bytes 196640 | tf_op jit(solution)/shard_map/all_to_all | solution.py:151
  92.6 1.5 %reshape.187 = bf16[2048,2,24]{2,1,0:T(2,128)(2,1)S(1)} reshape(bf16[8,2,6144]{2,1,0:T(2,128)(2,1)S(1)} %all-to-all-done.1) | data formatting | bytes 393216
  94.8 3.0 %collective-permute-start.4 = (bf16[999,128]{1,0:T(8,128)(2,1)S(1)}, bf16[999,128]{1,0:T(8,128)(2,1)S(1)}, u32[]{:S(2)}, u32[]{:S(2)}) collective-permute-start(bf16[999,128]{1,0:T(8,128)(2,1)S(1)} %pad_maximum_fusion.4), channel_id=1, source_target_pairs={{0,384},{128,0},{256,128},{384,256},{1,385},{129,1},{257,129},{385... | collective-permute-start | bytes 767240 | tf_op jit(solution)/shard_map/ppermute | solution.py:26
  97.9 6.2 %collective-permute-start.5 = (bf16[999,128]{1,0:T(8,128)(2,1)S(1)}, bf16[999,128]{1,0:T(8,128)(2,1)S(1)}, u32[]{:S(2)}, u32[]{:S(2)}) collective-permute-start(bf16[999,128]{1,0:T(8,128)(2,1)S(1)} %pad_maximum_fusion.4), channel_id=1, source_target_pairs={{0,128},{128,256},{256,384},{384,0},{1,129},{129,257},{257,385},{3... | collective-permute-start | bytes 767240 | tf_op jit(solution)/shard_map/ppermute | solution.py:22
  104.3 21.8 %collective-permute-done.4 = bf16[999,128]{1,0:T(8,128)(2,1)S(1)} collective-permute-done((bf16[999,128]{1,0:T(8,128)(2,1)S(1)}, bf16[999,128]{1,0:T(8,128)(2,1)S(1)}, u32[]{:S(2)}, u32[]{:S(2)}) %collective-permute-start.4) | collective-permute-done | bytes 255776 | tf_op jit(solution)/shard_map/ppermute | solution.py:26
  126.1 3.0 %collective-permute-start.7 = (bf16[500,128]{1,0:T(8,128)(2,1)S(1)}, bf16[500,128]{1,0:T(8,128)(2,1)S(1)}, u32[]{:S(2)}, u32[]{:S(2)}) collective-permute-start(bf16[500,128]{1,0:T(8,128)(2,1)S(1)} %slice.263), channel_id=1, source_target_pairs={{0,384},{128,0},{256,128},{384,256},{1,385},{129,1},{257,129},{385... | collective-permute-start | bytes 384008 | tf_op jit(solution)/shard_map/ppermute | solution.py:26
  129.2 6.2 %collective-permute-start.6 = (bf16[499,128]{1,0:T(8,128)(2,1)S(1)}, bf16[499,128]{1,0:T(8,128)(2,1)S(1)}, u32[]{:S(2)}, u32[]{:S(2)}) collective-permute-start(bf16[499,128]{1,0:T(8,128)(2,1)S(1)} %slice.262), channel_id=1, source_target_pairs={{0,128},{128,256},{256,384},{384,0},{1,129},{129,257},{257,385},{3... | collective-permute-start | bytes 383240 | tf_op jit(solution)/shard_map/ppermute | solution.py:22
  135.3 1.0 multiply_subtract_fusion
  136.3 4.0 %collective-permute-done.6 = bf16[499,128]{1,0:T(8,128)(2,1)S(1)} collective-permute-done((bf16[499,128]{1,0:T(8,128)(2,1)S(1)}, bf16[499,128]{1,0:T(8,128)(2,1)S(1)}, u32[]{:S(2)}, u32[]{:S(2)}) %collective-permute-start.6) | collective-permute-done | bytes 127776 | tf_op jit(solution)/shard_map/ppermute | solution.py:22
  141.1 0.7 reshape.179
  142.4 0.8 reshape.180
  143.8 0.8 reshape.178
  144.9 0.9 copy.77
  (107 shorter events, 6.5 us)
Async XLA Ops:
  0.6 0.9 copy-start
  0.7 4.6 %copy-start.5 = (bf16[1,72,768]{2,1,0:T(8,128)(2,1)S(1)}, bf16[1,72,768]{2,1,0:T(8,128)(2,1)}, u32[]{:S(2)}) copy-start(bf16[1,72,768]{2,1,0:T(8,128)(2,1)} %param.14) | copy-start | bytes 331780
  0.7 5.0 %copy-start.3 = (bf16[1,1,2,768,256]{4,3,2,1,0:T(8,128)(2,1)S(1)}, bf16[1,1,2,768,256]{4,3,2,1,0:T(8,128)(2,1)}, u32[]{:S(2)}) copy-start(bf16[1,1,2,768,256]{4,3,2,1,0:T(8,128)(2,1)} %param.13) | copy-start | bytes 2359300
  6.4 20.5 %collective-permute-start = (bf16[999,128]{1,0:T(8,128)(2,1)S(1)}, bf16[999,128]{1,0:T(8,128)(2,1)S(1)}, u32[]{:S(2)}, u32[]{:S(2)}) collective-permute-start(bf16[999,128]{1,0:T(8,128)(2,1)S(1)} %pad_maximum_fusion.2), channel_id=1, source_target_pairs={{0,128},{128,256},{256,384},{384,0},{1,129},{129,257},{257,385},{3... | collective-permute-start | bytes 767240 | tf_op jit(solution)/shard_map/ppermute | solution.py:22
  16.1 31.5 %collective-permute-start.2 = (bf16[999,128]{1,0:T(8,128)(2,1)S(1)}, bf16[999,128]{1,0:T(8,128)(2,1)S(1)}, u32[]{:S(2)}, u32[]{:S(2)}) collective-permute-start(bf16[999,128]{1,0:T(8,128)(2,1)S(1)} %pad_maximum_fusion.3), channel_id=1, source_target_pairs={{0,384},{128,0},{256,128},{384,256},{1,385},{129,1},{257,129},{385... | collective-permute-start | bytes 767240 | tf_op jit(solution)/shard_map/ppermute | solution.py:26
  27.0 24.8 %collective-permute-start.1 = (bf16[483,128]{1,0:T(8,128)(2,1)S(1)}, bf16[483,128]{1,0:T(8,128)(2,1)S(1)}, u32[]{:S(2)}, u32[]{:S(2)}) collective-permute-start(bf16[483,128]{1,0:T(8,128)(2,1)S(1)} %pad_maximum_fusion.6), channel_id=1, source_target_pairs={{0,128},{128,256},{256,384},{384,0},{1,129},{129,257},{257,385},{3... | collective-permute-start | bytes 370952 | tf_op jit(solution)/shard_map/ppermute | solution.py:22
  47.7 13.8 %collective-permute-start.3 = (bf16[484,128]{1,0:T(8,128)(2,1)S(1)}, bf16[484,128]{1,0:T(8,128)(2,1)S(1)}, u32[]{:S(2)}, u32[]{:S(2)}) collective-permute-start(bf16[484,128]{1,0:T(8,128)(2,1)S(1)} %pad_maximum_fusion.7), channel_id=1, source_target_pairs={{0,384},{128,0},{256,128},{384,256},{1,385},{129,1},{257,129},{385... | collective-permute-start | bytes 371720 | tf_op jit(solution)/shard_map/ppermute | solution.py:26
  62.6 15.4 %all-to-all-start = ((bf16[2,192,256]{2,0,1:T(2,128)(2,1)}), bf16[2,192,256]{2,0,1:T(2,128)(2,1)S(1)}, u32[]{:S(2)}, u32[]{:S(2)}) async-start(bf16[2,192,256]{2,0,1:T(2,128)(2,1)} %copy.71), calls=%async_computation | async-start | bytes 393216 | tf_op jit(solution)/shard_map/all_to_all | solution.py:138
  71.4 6.6 %copy-start.1 = (f32[1,2,24,2048]{3,2,1,0:T(8,128)S(1)}, f32[1,2,24,2048]{3,2,1,0:T(8,128)}, u32[]{:S(2)}) copy-start(f32[1,2,24,2048]{3,2,1,0:T(8,128)} %param.17) | copy-start | bytes 1179652
  71.4 6.6 %copy-start.2 = (f32[1,2,24,2048]{3,2,1,0:T(8,128)S(1)}, f32[1,2,24,2048]{3,2,1,0:T(8,128)}, u32[]{:S(2)}) copy-start(f32[1,2,24,2048]{3,2,1,0:T(8,128)} %param.21) | copy-start | bytes 1179652
  78.9 7.2 %copy-start.9 = (f32[18,192]{1,0:T(8,128)S(1)}, f32[18,192]{1,0:T(8,128)}, u32[]{:S(2)}) copy-start(f32[18,192]{1,0:T(8,128)} %param.19) | copy-start | bytes 41476
  78.9 7.2 %copy-start.10 = (f32[18,192]{1,0:T(8,128)S(1)}, f32[18,192]{1,0:T(8,128)}, u32[]{:S(2)}) copy-start(f32[18,192]{1,0:T(8,128)} %param.23) | copy-start | bytes 41476
  78.9 7.9 %copy-start.6 = (f32[72,192]{1,0:T(8,128)S(1)}, f32[72,192]{1,0:T(8,128)}, u32[]{:S(2)}) copy-start(f32[72,192]{1,0:T(8,128)} %param.18) | copy-start | bytes 165892
  78.9 7.9 %copy-start.7 = (f32[72,192]{1,0:T(8,128)S(1)}, f32[72,192]{1,0:T(8,128)}, u32[]{:S(2)}) copy-start(f32[72,192]{1,0:T(8,128)} %param.22) | copy-start | bytes 165892
  78.9 8.6 %copy-start.4 = (f32[64,192]{1,0:T(8,128)S(1)}, f32[64,192]{1,0:T(8,128)}, u32[]{:S(2)}) copy-start(f32[64,192]{1,0:T(8,128)} %param.20) | copy-start | bytes 147460
  78.9 8.6 %copy-start.8 = (f32[64,192]{1,0:T(8,128)S(1)}, f32[64,192]{1,0:T(8,128)}, u32[]{:S(2)}) copy-start(f32[64,192]{1,0:T(8,128)} %param.24) | copy-start | bytes 147460
  81.0 11.6 %all-to-all-start.1 = ((bf16[8,2,6144]{2,1,0:T(2,128)(2,1)}), bf16[8,2,6144]{2,1,0:T(2,128)(2,1)S(1)}, u32[]{:S(2)}, u32[]{:S(2)}) async-start(bf16[8,2,6144]{2,1,0:T(2,128)(2,1)} %reshape.186), calls=%async_computation.1 | async-start | bytes 393216 | tf_op jit(solution)/shard_map/all_to_all | solution.py:151
  94.8 31.3 %collective-permute-start.4 = (bf16[999,128]{1,0:T(8,128)(2,1)S(1)}, bf16[999,128]{1,0:T(8,128)(2,1)S(1)}, u32[]{:S(2)}, u32[]{:S(2)}) collective-permute-start(bf16[999,128]{1,0:T(8,128)(2,1)S(1)} %pad_maximum_fusion.4), channel_id=1, source_target_pairs={{0,384},{128,0},{256,128},{384,256},{1,385},{129,1},{257,129},{385... | collective-permute-start | bytes 767240 | tf_op jit(solution)/shard_map/ppermute | solution.py:26
  97.9 31.3 %collective-permute-start.5 = (bf16[999,128]{1,0:T(8,128)(2,1)S(1)}, bf16[999,128]{1,0:T(8,128)(2,1)S(1)}, u32[]{:S(2)}, u32[]{:S(2)}) collective-permute-start(bf16[999,128]{1,0:T(8,128)(2,1)S(1)} %pad_maximum_fusion.4), channel_id=1, source_target_pairs={{0,128},{128,256},{256,384},{384,0},{1,129},{129,257},{257,385},{3... | collective-permute-start | bytes 767240 | tf_op jit(solution)/shard_map/ppermute | solution.py:22
  126.1 14.3 %collective-permute-start.7 = (bf16[500,128]{1,0:T(8,128)(2,1)S(1)}, bf16[500,128]{1,0:T(8,128)(2,1)S(1)}, u32[]{:S(2)}, u32[]{:S(2)}) collective-permute-start(bf16[500,128]{1,0:T(8,128)(2,1)S(1)} %slice.263), channel_id=1, source_target_pairs={{0,384},{128,0},{256,128},{384,256},{1,385},{129,1},{257,129},{385... | collective-permute-start | bytes 384008 | tf_op jit(solution)/shard_map/ppermute | solution.py:26
  129.2 11.2 %collective-permute-start.6 = (bf16[499,128]{1,0:T(8,128)(2,1)S(1)}, bf16[499,128]{1,0:T(8,128)(2,1)S(1)}, u32[]{:S(2)}, u32[]{:S(2)}) collective-permute-start(bf16[499,128]{1,0:T(8,128)(2,1)S(1)} %slice.262), channel_id=1, source_target_pairs={{0,128},{128,256},{256,384},{384,0},{1,129},{129,257},{257,385},{3... | collective-permute-start | bytes 383240 | tf_op jit(solution)/shard_map/ppermute | solution.py:22

commit v8 on v7

--- a/solution.py
+++ b/solution.py
@@ -97,9 +97,11 @@
     own_shard = inner_experts[0, 0]
     halves, all_rows, my_cols = own_shard.shape
     rep_rows = all_rows // groups
+    mdl_size = lax.axis_size("mdl")
+    own_rows = rep_rows // mdl_size
     ex_send = (
-        own_shard.reshape(halves, groups, rep_rows, my_cols)
-        .transpose(1, 0, 2, 3)
+        own_shard.reshape(halves, groups, mdl_size, own_rows, my_cols)
+        .transpose(1, 2, 0, 3, 4)
         .reshape(groups, -1, lanes)
     )
     de_send = split_rows(inner_dense[0], groups).reshape(groups, -1, lanes)
@@ -129,15 +131,16 @@
         bounds.append(bounds[-1] + s)
     parts = [total[bounds[i] : bounds[i + 1]] for i in range(4)]
 
-    ex_sum = parts[0].reshape(halves, rep_rows, my_cols)
+    ex_sum = parts[0].reshape(mdl_size, halves, own_rows, my_cols)
     dense_sum = parts[1].reshape(outer_dense.shape)
     small_sum = parts[2].reshape(outer_small.shape)
     nhalf = parts[3].shape[0] // 2
     coefficient = (parts[3][:nhalf] + parts[3][nhalf:]).reshape(partial_value.shape)
 
     expert_sum = lax.all_to_all(
-        ex_sum.astype(jnp.bfloat16), "mdl", split_axis=1, concat_axis=2, tiled=True
+        ex_sum.astype(jnp.bfloat16), "mdl", split_axis=0, concat_axis=0, tiled=True
     ).astype(jnp.float32)
+    expert_sum = expert_sum.transpose(1, 2, 0, 3).reshape(outer_experts.shape[1:])
     grad_experts = outer_experts[0] - expert_sum / groups
     grad_dense = outer_dense - dense_sum / groups
     grad_small = outer_small - small_sum / groups
@@ -149,7 +152,13 @@
     small_outer, small_moment = nesterov(outer_small, moment_small, grad_small)
     embed_outer, embed_moment = nesterov(outer_embed, moment_embed, grad_embed)
     spread = lax.all_to_all(
-        expert_outer.astype(jnp.bfloat16), "mdl", split_axis=2, concat_axis=1, tiled=True
+        expert_outer.astype(jnp.bfloat16)
+        .reshape(halves, own_rows, mdl_size, my_cols)
+        .transpose(2, 0, 1, 3),
+        "mdl",
+        split_axis=0,
+        concat_axis=0,
+        tiled=True,
     )
 
     pieces = [
@@ -166,8 +175,8 @@
         n = p.size // lanes
         g = jnp.stack([b[start : start + n] for b in blocks]).reshape((groups,) + p.shape)
         start += n
-        if p.ndim == 3:
-            g = g.transpose(1, 0, 2, 3).reshape(p.shape[0], groups * p.shape[1], p.shape[2])
+        if p.ndim == 4:
+            g = g.transpose(2, 0, 1, 3, 4).reshape(halves, all_rows, my_cols)
         else:
             g = g.transpose(1, 0, 2).reshape(p.shape[0], groups * p.shape[1])
         outs.append(g)

time: 147 us -> 145 us (0.986)
  local copies, waits for them, and re-layouts: 14.8 us -> 10.1 us
    unnamed x24, local copies, waits for them, and re-layouts: 4.4 us -> 1.17 us
  transfers between devices with their start and end apart: 10 -> 10, of which waited for: 7 -> 7; matrix products, arithmetic and copies ran while one was open for 3% -> 2% of each run, Pallas kernels for 0% -> 0%
where the time goes in v8:
time: 145 us; the launch traced here: 143 us
  starting transfers between devices  71.1 us (49%)
  waiting for transfers between devices  52.9 us (36%)
  local copies, waits for them, and re-layouts  10.1 us (7%)
  other arithmetic  4.26 us (3%)
  matrix products  3.17 us (2%)
    ppermute x4, starting transfers between devices, to_next(): lax.ppermute(x, 'rep', [(i, (i + 1) % groups) for i in range(groups)])  41.5 us
    ppermute x4, waiting for transfers between devices, to_prev(): lax.ppermute(x, 'rep', [(i, (i - 1) % groups) for i in range(groups)])  32.7 us
    ppermute x4, starting transfers between devices, to_prev(): lax.ppermute(x, 'rep', [(i, (i - 1) % groups) for i in range(groups)])  15.7 us
    ppermute x4, waiting for transfers between devices, to_next(): lax.ppermute(x, 'rep', [(i, (i + 1) % groups) for i in range(groups)])  10 us
    all_to_all x1, starting transfers between devices, on_device(): lax.all_to_all(ex_sum.astype(jnp.bfloat16), 'mdl', split_axis=0, concat_a...  8.84 us
    all_to_all x1, waiting for transfers between devices, on_device(): lax.all_to_all(ex_sum.astype(jnp.bfloat16), 'mdl', split_axis=0, concat_a...  6.23 us
    all_to_all x1, starting transfers between devices, on_device(): lax.all_to_all(expert_outer.astype(jnp.bfloat16).reshape(halves, own_rows...  5.08 us
    all_to_all x1, waiting for transfers between devices, on_device(): lax.all_to_all(expert_outer.astype(jnp.bfloat16).reshape(halves, own_rows...  3.94 us
  transfers between devices with their start and end apart: 10, of which 7 were waited for; matrix products, arithmetic and copies ran while one was open for 2% of the time, Pallas kernels for 0%

profile of v8, /device:TPU:1, one launch (start us, length us, event | category | flops | bytes accessed | tf_op | source)
XLA Modules:
  0.0 142.9 jit_solution(11045393226840670256)
XLA Ops:
  0.7 0.9 copy-done
  1.6 1.1 convolution_bitcast_fusion
  2.7 1.1 subtract_convert_fusion
  4.2 0.9 reshape_squeeze.11
  5.7 0.3 reshape.160
  6.4 9.6 %collective-permute-start = (bf16[999,128]{1,0:T(8,128)(2,1)S(1)}, bf16[999,128]{1,0:T(8,128)(2,1)S(1)}, u32[]{:S(2)}, u32[]{:S(2)}) collective-permute-start(bf16[999,128]{1,0:T(8,128)(2,1)S(1)} %pad_maximum_fusion.2), channel_id=1, source_target_pairs={{0,128},{128,256},{256,384},{384,0},{1,129},{129,257},{257,385},{3... | collective-permute-start | bytes 767240 | tf_op jit(solution)/shard_map/ppermute | solution.py:22
  16.1 5.6 %collective-permute-start.2 = (bf16[999,128]{1,0:T(8,128)(2,1)S(1)}, bf16[999,128]{1,0:T(8,128)(2,1)S(1)}, u32[]{:S(2)}, u32[]{:S(2)}) collective-permute-start(bf16[999,128]{1,0:T(8,128)(2,1)S(1)} %pad_maximum_fusion.3), channel_id=1, source_target_pairs={{0,384},{128,0},{256,128},{384,256},{1,385},{129,1},{257,129},{385... | collective-permute-start | bytes 767240 | tf_op jit(solution)/shard_map/ppermute | solution.py:26
  21.8 5.1 %collective-permute-done = bf16[999,128]{1,0:T(8,128)(2,1)S(1)} collective-permute-done((bf16[999,128]{1,0:T(8,128)(2,1)S(1)}, bf16[999,128]{1,0:T(8,128)(2,1)S(1)}, u32[]{:S(2)}, u32[]{:S(2)}) %collective-permute-start) | collective-permute-done | bytes 255776 | tf_op jit(solution)/shard_map/ppermute | solution.py:22
  27.0 19.5 %collective-permute-start.1 = (bf16[483,128]{1,0:T(8,128)(2,1)S(1)}, bf16[483,128]{1,0:T(8,128)(2,1)S(1)}, u32[]{:S(2)}, u32[]{:S(2)}) collective-permute-start(bf16[483,128]{1,0:T(8,128)(2,1)S(1)} %pad_maximum_fusion.6), channel_id=1, source_target_pairs={{0,128},{128,256},{256,384},{384,0},{1,129},{129,257},{257,385},{3... | collective-permute-start | bytes 370952 | tf_op jit(solution)/shard_map/ppermute | solution.py:22
  46.5 1.1 collective-permute-done.2
  47.7 4.1 %collective-permute-start.3 = (bf16[484,128]{1,0:T(8,128)(2,1)S(1)}, bf16[484,128]{1,0:T(8,128)(2,1)S(1)}, u32[]{:S(2)}, u32[]{:S(2)}) collective-permute-start(bf16[484,128]{1,0:T(8,128)(2,1)S(1)} %pad_maximum_fusion.7), channel_id=1, source_target_pairs={{0,384},{128,0},{256,128},{384,256},{1,385},{129,1},{257,129},{385... | collective-permute-start | bytes 371720 | tf_op jit(solution)/shard_map/ppermute | solution.py:26
  51.9 9.6 %collective-permute-done.3 = bf16[484,128]{1,0:T(8,128)(2,1)S(1)} collective-permute-done((bf16[484,128]{1,0:T(8,128)(2,1)S(1)}, bf16[484,128]{1,0:T(8,128)(2,1)S(1)}, u32[]{:S(2)}, u32[]{:S(2)}) %collective-permute-start.3) | collective-permute-done | bytes 123936 | tf_op jit(solution)/shard_map/ppermute | solution.py:26
  61.6 0.7 convert_element_type.112
  62.4 8.8 %all-to-all-start = ((bf16[8,2,24,256]{3,2,1,0:T(8,128)(2,1)}), bf16[8,2,24,256]{3,2,1,0:T(8,128)(2,1)S(1)}, u32[]{:S(2)}, u32[]{:S(2)}) async-start(bf16[8,2,24,256]{3,2,1,0:T(8,128)(2,1)} %convert_element_type.112), calls=%async_computation | async-start | bytes 393216 | tf_op jit(solution)/shard_map/all_to_all | solution.py:140
  71.5 6.2 %all-to-all-done = bf16[8,2,24,256]{3,2,1,0:T(8,128)(2,1)S(1)} async-done(((bf16[8,2,24,256]{3,2,1,0:T(8,128)(2,1)}), bf16[8,2,24,256]{3,2,1,0:T(8,128)(2,1)S(1)}, u32[]{:S(2)}, u32[]{:S(2)}) %all-to-all-start) | async-done | bytes 196640 | tf_op jit(solution)/shard_map/all_to_all | solution.py:140
  78.1 1.0 multiply_subtract_fusion
  79.3 1.0 fusion.11
  80.2 5.1 %all-to-all-start.1 = ((bf16[8,2,24,256]{3,2,1,0:T(8,128)(2,1)}), bf16[8,2,24,256]{3,2,1,0:T(8,128)(2,1)S(1)}, u32[]{:S(2)}, u32[]{:S(2)}) async-start(bf16[8,2,24,256]{3,2,1,0:T(8,128)(2,1)} %fusion.11), calls=%async_computation.1 | async-start | bytes 393216 | tf_op jit(solution)/shard_map/all_to_all | solution.py:154
  85.3 0.6 fusion.22
  86.0 0.7 fusion.21
  86.8 0.9 fusion.23
  87.9 3.9 %all-to-all-done.1 = bf16[8,2,24,256]{3,2,1,0:T(8,128)(2,1)S(1)} async-done(((bf16[8,2,24,256]{3,2,1,0:T(8,128)(2,1)}), bf16[8,2,24,256]{3,2,1,0:T(8,128)(2,1)S(1)}, u32[]{:S(2)}, u32[]{:S(2)}) %all-to-all-start.1) | async-done | bytes 196640 | tf_op jit(solution)/shard_map/all_to_all | solution.py:154
  91.9 3.0 %collective-permute-start.4 = (bf16[999,128]{1,0:T(8,128)(2,1)S(1)}, bf16[999,128]{1,0:T(8,128)(2,1)S(1)}, u32[]{:S(2)}, u32[]{:S(2)}) collective-permute-start(bf16[999,128]{1,0:T(8,128)(2,1)S(1)} %pad_maximum_fusion.4), channel_id=1, source_target_pairs={{0,384},{128,0},{256,128},{384,256},{1,385},{129,1},{257,129},{385... | collective-permute-start | bytes 767240 | tf_op jit(solution)/shard_map/ppermute | solution.py:26
  95.0 6.2 %collective-permute-start.5 = (bf16[999,128]{1,0:T(8,128)(2,1)S(1)}, bf16[999,128]{1,0:T(8,128)(2,1)S(1)}, u32[]{:S(2)}, u32[]{:S(2)}) collective-permute-start(bf16[999,128]{1,0:T(8,128)(2,1)S(1)} %pad_maximum_fusion.4), channel_id=1, source_target_pairs={{0,128},{128,256},{256,384},{384,0},{1,129},{129,257},{257,385},{3... | collective-permute-start | bytes 767240 | tf_op jit(solution)/shard_map/ppermute | solution.py:22
  101.1 22.0 %collective-permute-done.4 = bf16[999,128]{1,0:T(8,128)(2,1)S(1)} collective-permute-done((bf16[999,128]{1,0:T(8,128)(2,1)S(1)}, bf16[999,128]{1,0:T(8,128)(2,1)S(1)}, u32[]{:S(2)}, u32[]{:S(2)}) %collective-permute-start.4) | collective-permute-done | bytes 255776 | tf_op jit(solution)/shard_map/ppermute | solution.py:26
  123.2 3.0 %collective-permute-start.7 = (bf16[500,128]{1,0:T(8,128)(2,1)S(1)}, bf16[500,128]{1,0:T(8,128)(2,1)S(1)}, u32[]{:S(2)}, u32[]{:S(2)}) collective-permute-start(bf16[500,128]{1,0:T(8,128)(2,1)S(1)} %slice.263), channel_id=1, source_target_pairs={{0,384},{128,0},{256,128},{384,256},{1,385},{129,1},{257,129},{385... | collective-permute-start | bytes 384008 | tf_op jit(solution)/shard_map/ppermute | solution.py:26
  126.3 6.2 %collective-permute-start.6 = (bf16[499,128]{1,0:T(8,128)(2,1)S(1)}, bf16[499,128]{1,0:T(8,128)(2,1)S(1)}, u32[]{:S(2)}, u32[]{:S(2)}) collective-permute-start(bf16[499,128]{1,0:T(8,128)(2,1)S(1)} %slice.262), channel_id=1, source_target_pairs={{0,128},{128,256},{256,384},{384,0},{1,129},{129,257},{257,385},{3... | collective-permute-start | bytes 383240 | tf_op jit(solution)/shard_map/ppermute | solution.py:22
  132.6 4.9 %collective-permute-done.6 = bf16[499,128]{1,0:T(8,128)(2,1)S(1)} collective-permute-done((bf16[499,128]{1,0:T(8,128)(2,1)S(1)}, bf16[499,128]{1,0:T(8,128)(2,1)S(1)}, u32[]{:S(2)}, u32[]{:S(2)}) %collective-permute-start.6) | collective-permute-done | bytes 127776 | tf_op jit(solution)/shard_map/ppermute | solution.py:22
  138.3 0.7 reshape.169
  139.5 0.8 reshape.170
  140.9 0.8 reshape.168
  142.0 0.9 copy.50
  (103 shorter events, 5.1 us)
Async XLA Ops:
  0.6 0.9 copy-start
  0.7 4.6 %copy-start.5 = (bf16[1,72,768]{2,1,0:T(8,128)(2,1)S(1)}, bf16[1,72,768]{2,1,0:T(8,128)(2,1)}, u32[]{:S(2)}) copy-start(bf16[1,72,768]{2,1,0:T(8,128)(2,1)} %param.14) | copy-start | bytes 331780
  0.7 5.0 %copy-start.2 = (bf16[1,1,2,768,256]{4,3,2,1,0:T(8,128)(2,1)S(1)}, bf16[1,1,2,768,256]{4,3,2,1,0:T(8,128)(2,1)}, u32[]{:S(2)}) copy-start(bf16[1,1,2,768,256]{4,3,2,1,0:T(8,128)(2,1)} %param.13) | copy-start | bytes 2359300
  6.1 15.5 %copy-start.1 = (f32[1,2,24,2048]{3,2,1,0:T(8,128)S(1)}, f32[1,2,24,2048]{3,2,1,0:T(8,128)}, u32[]{:S(2)}) copy-start(f32[1,2,24,2048]{3,2,1,0:T(8,128)} %param.17) | copy-start | bytes 1179652
  6.4 20.5 %collective-permute-start = (bf16[999,128]{1,0:T(8,128)(2,1)S(1)}, bf16[999,128]{1,0:T(8,128)(2,1)S(1)}, u32[]{:S(2)}, u32[]{:S(2)}) collective-permute-start(bf16[999,128]{1,0:T(8,128)(2,1)S(1)} %pad_maximum_fusion.2), channel_id=1, source_target_pairs={{0,128},{128,256},{256,384},{384,0},{1,129},{129,257},{257,385},{3... | collective-permute-start | bytes 767240 | tf_op jit(solution)/shard_map/ppermute | solution.py:22
  16.1 31.5 %collective-permute-start.2 = (bf16[999,128]{1,0:T(8,128)(2,1)S(1)}, bf16[999,128]{1,0:T(8,128)(2,1)S(1)}, u32[]{:S(2)}, u32[]{:S(2)}) collective-permute-start(bf16[999,128]{1,0:T(8,128)(2,1)S(1)} %pad_maximum_fusion.3), channel_id=1, source_target_pairs={{0,384},{128,0},{256,128},{384,256},{1,385},{129,1},{257,129},{385... | collective-permute-start | bytes 767240 | tf_op jit(solution)/shard_map/ppermute | solution.py:26
  27.0 24.8 %collective-permute-start.1 = (bf16[483,128]{1,0:T(8,128)(2,1)S(1)}, bf16[483,128]{1,0:T(8,128)(2,1)S(1)}, u32[]{:S(2)}, u32[]{:S(2)}) collective-permute-start(bf16[483,128]{1,0:T(8,128)(2,1)S(1)} %pad_maximum_fusion.6), channel_id=1, source_target_pairs={{0,128},{128,256},{256,384},{384,0},{1,129},{129,257},{257,385},{3... | collective-permute-start | bytes 370952 | tf_op jit(solution)/shard_map/ppermute | solution.py:22
  47.7 13.8 %collective-permute-start.3 = (bf16[484,128]{1,0:T(8,128)(2,1)S(1)}, bf16[484,128]{1,0:T(8,128)(2,1)S(1)}, u32[]{:S(2)}, u32[]{:S(2)}) collective-permute-start(bf16[484,128]{1,0:T(8,128)(2,1)S(1)} %pad_maximum_fusion.7), channel_id=1, source_target_pairs={{0,384},{128,0},{256,128},{384,256},{1,385},{129,1},{257,129},{385... | collective-permute-start | bytes 371720 | tf_op jit(solution)/shard_map/ppermute | solution.py:26
  62.4 15.4 %all-to-all-start = ((bf16[8,2,24,256]{3,2,1,0:T(8,128)(2,1)}), bf16[8,2,24,256]{3,2,1,0:T(8,128)(2,1)S(1)}, u32[]{:S(2)}, u32[]{:S(2)}) async-start(bf16[8,2,24,256]{3,2,1,0:T(8,128)(2,1)} %convert_element_type.112), calls=%async_computation | async-start | bytes 393216 | tf_op jit(solution)/shard_map/all_to_all | solution.py:140
  71.5 6.6 %copy-start.3 = (f32[1,2,24,2048]{3,2,1,0:T(8,128)S(1)}, f32[1,2,24,2048]{3,2,1,0:T(8,128)}, u32[]{:S(2)}) copy-start(f32[1,2,24,2048]{3,2,1,0:T(8,128)} %param.21) | copy-start | bytes 1179652
  79.1 6.2 %copy-start.9 = (f32[18,192]{1,0:T(8,128)S(1)}, f32[18,192]{1,0:T(8,128)}, u32[]{:S(2)}) copy-start(f32[18,192]{1,0:T(8,128)} %param.19) | copy-start | bytes 41476
  79.1 6.2 %copy-start.10 = (f32[18,192]{1,0:T(8,128)S(1)}, f32[18,192]{1,0:T(8,128)}, u32[]{:S(2)}) copy-start(f32[18,192]{1,0:T(8,128)} %param.23) | copy-start | bytes 41476
  79.2 6.8 %copy-start.6 = (f32[72,192]{1,0:T(8,128)S(1)}, f32[72,192]{1,0:T(8,128)}, u32[]{:S(2)}) copy-start(f32[72,192]{1,0:T(8,128)} %param.18) | copy-start | bytes 165892
  79.2 6.8 %copy-start.7 = (f32[72,192]{1,0:T(8,128)S(1)}, f32[72,192]{1,0:T(8,128)}, u32[]{:S(2)}) copy-start(f32[72,192]{1,0:T(8,128)} %param.22) | copy-start | bytes 165892
  79.2 7.6 %copy-start.4 = (f32[64,192]{1,0:T(8,128)S(1)}, f32[64,192]{1,0:T(8,128)}, u32[]{:S(2)}) copy-start(f32[64,192]{1,0:T(8,128)} %param.20) | copy-start | bytes 147460
  79.3 7.6 %copy-start.8 = (f32[64,192]{1,0:T(8,128)S(1)}, f32[64,192]{1,0:T(8,128)}, u32[]{:S(2)}) copy-start(f32[64,192]{1,0:T(8,128)} %param.24) | copy-start | bytes 147460
  80.2 11.6 %all-to-all-start.1 = ((bf16[8,2,24,256]{3,2,1,0:T(8,128)(2,1)}), bf16[8,2,24,256]{3,2,1,0:T(8,128)(2,1)S(1)}, u32[]{:S(2)}, u32[]{:S(2)}) async-start(bf16[8,2,24,256]{3,2,1,0:T(8,128)(2,1)} %fusion.11), calls=%async_computation.1 | async-start | bytes 393216 | tf_op jit(solution)/shard_map/all_to_all | solution.py:154
  91.9 31.3 %collective-permute-start.4 = (bf16[999,128]{1,0:T(8,128)(2,1)S(1)}, bf16[999,128]{1,0:T(8,128)(2,1)S(1)}, u32[]{:S(2)}, u32[]{:S(2)}) collective-permute-start(bf16[999,128]{1,0:T(8,128)(2,1)S(1)} %pad_maximum_fusion.4), channel_id=1, source_target_pairs={{0,384},{128,0},{256,128},{384,256},{1,385},{129,1},{257,129},{385... | collective-permute-start | bytes 767240 | tf_op jit(solution)/shard_map/ppermute | solution.py:26
  95.0 31.3 %collective-permute-start.5 = (bf16[999,128]{1,0:T(8,128)(2,1)S(1)}, bf16[999,128]{1,0:T(8,128)(2,1)S(1)}, u32[]{:S(2)}, u32[]{:S(2)}) collective-permute-start(bf16[999,128]{1,0:T(8,128)(2,1)S(1)} %pad_maximum_fusion.4), channel_id=1, source_target_pairs={{0,128},{128,256},{256,384},{384,0},{1,129},{129,257},{257,385},{3... | collective-permute-start | bytes 767240 | tf_op jit(solution)/shard_map/ppermute | solution.py:22
  123.2 14.3 %collective-permute-start.7 = (bf16[500,128]{1,0:T(8,128)(2,1)S(1)}, bf16[500,128]{1,0:T(8,128)(2,1)S(1)}, u32[]{:S(2)}, u32[]{:S(2)}) collective-permute-start(bf16[500,128]{1,0:T(8,128)(2,1)S(1)} %slice.263), channel_id=1, source_target_pairs={{0,384},{128,0},{256,128},{384,256},{1,385},{129,1},{257,129},{385... | collective-permute-start | bytes 384008 | tf_op jit(solution)/shard_map/ppermute | solution.py:26
  126.3 11.2 %collective-permute-start.6 = (bf16[499,128]{1,0:T(8,128)(2,1)S(1)}, bf16[499,128]{1,0:T(8,128)(2,1)S(1)}, u32[]{:S(2)}, u32[]{:S(2)}) collective-permute-start(bf16[499,128]{1,0:T(8,128)(2,1)S(1)} %slice.262), channel_id=1, source_target_pairs={{0,128},{128,256},{256,384},{384,0},{1,129},{129,257},{257,385},{3... | collective-permute-start | bytes 383240 | tf_op jit(solution)/shard_map/ppermute | solution.py:22

commit v9 on v8

--- a/solution.py
+++ b/solution.py
@@ -111,13 +111,11 @@
     offset = lax.axis_index("rep") * col_count
     basis_part = lax.dynamic_slice_in_dim(embed_basis, offset, col_count, 0)
     partial_value = jnp.dot(
-        outer_embed, basis_part, precision=hi_prec, preferred_element_type=jnp.float32
-    ) - jnp.dot(
-        inner_embed[0].astype(jnp.float32),
-        embed_basis,
+        jnp.concatenate([outer_embed, inner_embed[0].astype(jnp.float32) / groups], axis=1),
+        jnp.concatenate([basis_part, -embed_basis], axis=0),
         precision=hi_prec,
         preferred_element_type=jnp.float32,
-    ) / groups
+    )
     part_hi = partial_value.astype(jnp.bfloat16)
     part_lo = (partial_value - part_hi.astype(jnp.float32)).astype(jnp.bfloat16)
     pp = jnp.concatenate([part_hi.reshape(-1, lanes), part_lo.reshape(-1, lanes)])
@@ -173,12 +171,14 @@
     start = 0
     for p in pieces:
         n = p.size // lanes
-        g = jnp.stack([b[start : start + n] for b in blocks]).reshape((groups,) + p.shape)
+        g = [b[start : start + n].reshape(p.shape) for b in blocks]
         start += n
         if p.ndim == 4:
-            g = g.transpose(2, 0, 1, 3, 4).reshape(halves, all_rows, my_cols)
+            g = jnp.concatenate(
+                [x.transpose(1, 0, 2, 3).reshape(halves, rep_rows, my_cols) for x in g], axis=1
+            )
         else:
-            g = g.transpose(1, 0, 2).reshape(p.shape[0], groups * p.shape[1])
+            g = jnp.concatenate(g, axis=1)
         outs.append(g)
 
     return (

time: 145 us -> 144 us (level)
  other arithmetic: 4.26 us -> 7.37 us
  local copies, waits for them, and re-layouts: 10.1 us -> 8.14 us
  matrix products: 3.17 us -> 1.31 us
    concatenate x0 -> x3, other arithmetic: none -> 2.18 us  [on_device(): g = jnp.concatenate(g, axis=1)]
    dot_general x2 -> x1, matrix products: 2.23 us -> 0.46 us  [on_device(): jnp.dot(jnp.concatenate([outer_embed, inner_embed[0].astype(jnp.float32)...]
where the time goes in v9:
time: 144 us; the launch traced here: 142 us
  starting transfers between devices  71.1 us (49%)
  waiting for transfers between devices  53.1 us (37%)
  local copies, waits for them, and re-layouts  8.14 us (6%)
  other arithmetic  7.37 us (5%)
    ppermute x4, starting transfers between devices, to_next(): lax.ppermute(x, 'rep', [(i, (i + 1) % groups) for i in range(groups)])  41.7 us
    ppermute x4, waiting for transfers between devices, to_prev(): lax.ppermute(x, 'rep', [(i, (i - 1) % groups) for i in range(groups)])  32.8 us
    ppermute x4, starting transfers between devices, to_prev(): lax.ppermute(x, 'rep', [(i, (i - 1) % groups) for i in range(groups)])  15.6 us
    ppermute x4, waiting for transfers between devices, to_next(): lax.ppermute(x, 'rep', [(i, (i + 1) % groups) for i in range(groups)])  10 us
    all_to_all x1, starting transfers between devices, on_device(): lax.all_to_all(ex_sum.astype(jnp.bfloat16), 'mdl', split_axis=0, concat_a...  8.82 us
    all_to_all x1, waiting for transfers between devices, on_device(): lax.all_to_all(ex_sum.astype(jnp.bfloat16), 'mdl', split_axis=0, concat_a...  6.23 us
    all_to_all x1, starting transfers between devices, on_device(): lax.all_to_all(expert_outer.astype(jnp.bfloat16).reshape(halves, own_rows...  5.08 us
    all_to_all x1, waiting for transfers between devices, on_device(): lax.all_to_all(expert_outer.astype(jnp.bfloat16).reshape(halves, own_rows...  4.03 us
  transfers between devices with their start and end apart: 10, of which 7 were waited for; matrix products, arithmetic and copies ran while one was open for 2% of the time, Pallas kernels for 0%

profile of v9, /device:TPU:1, one launch (start us, length us, event | category | flops | bytes accessed | tf_op | source)
XLA Modules:
  0.0 142.4 jit_solution(7710875387455700453)
XLA Ops:
  0.7 0.9 reshape_squeeze.11
  1.7 0.9 neg.3
  2.7 1.1 constant_dynamic-slice_fusion.16
  3.7 1.1 reshape_squeeze.10
  5.1 0.5 subtract_convert_fusion
  6.5 9.6 %collective-permute-start = (bf16[999,128]{1,0:T(8,128)(2,1)S(1)}, bf16[999,128]{1,0:T(8,128)(2,1)S(1)}, u32[]{:S(2)}, u32[]{:S(2)}) collective-permute-start(bf16[999,128]{1,0:T(8,128)(2,1)S(1)} %pad_maximum_fusion.2), channel_id=1, source_target_pairs={{0,128},{128,256},{256,384},{384,0},{1,129},{129,257},{257,385},{3... | collective-permute-start | bytes 767240 | tf_op jit(solution)/shard_map/ppermute | solution.py:22
  16.2 5.5 %collective-permute-start.2 = (bf16[999,128]{1,0:T(8,128)(2,1)S(1)}, bf16[999,128]{1,0:T(8,128)(2,1)S(1)}, u32[]{:S(2)}, u32[]{:S(2)}) collective-permute-start(bf16[999,128]{1,0:T(8,128)(2,1)S(1)} %pad_maximum_fusion.3), channel_id=1, source_target_pairs={{0,384},{128,0},{256,128},{384,256},{1,385},{129,1},{257,129},{385... | collective-permute-start | bytes 767240 | tf_op jit(solution)/shard_map/ppermute | solution.py:26
  21.9 5.0 %collective-permute-done = bf16[999,128]{1,0:T(8,128)(2,1)S(1)} collective-permute-done((bf16[999,128]{1,0:T(8,128)(2,1)S(1)}, bf16[999,128]{1,0:T(8,128)(2,1)S(1)}, u32[]{:S(2)}, u32[]{:S(2)}) %collective-permute-start) | collective-permute-done | bytes 255776 | tf_op jit(solution)/shard_map/ppermute | solution.py:22
  27.0 19.7 %collective-permute-start.1 = (bf16[483,128]{1,0:T(8,128)(2,1)S(1)}, bf16[483,128]{1,0:T(8,128)(2,1)S(1)}, u32[]{:S(2)}, u32[]{:S(2)}) collective-permute-start(bf16[483,128]{1,0:T(8,128)(2,1)S(1)} %pad_maximum_fusion.6), channel_id=1, source_target_pairs={{0,128},{128,256},{256,384},{384,0},{1,129},{129,257},{257,385},{3... | collective-permute-start | bytes 370952 | tf_op jit(solution)/shard_map/ppermute | solution.py:22
  46.7 1.0 collective-permute-done.2
  47.8 4.0 %collective-permute-start.3 = (bf16[484,128]{1,0:T(8,128)(2,1)S(1)}, bf16[484,128]{1,0:T(8,128)(2,1)S(1)}, u32[]{:S(2)}, u32[]{:S(2)}) collective-permute-start(bf16[484,128]{1,0:T(8,128)(2,1)S(1)} %pad_maximum_fusion.7), channel_id=1, source_target_pairs={{0,384},{128,0},{256,128},{384,256},{1,385},{129,1},{257,129},{385... | collective-permute-start | bytes 371720 | tf_op jit(solution)/shard_map/ppermute | solution.py:26
  51.9 9.7 %collective-permute-done.3 = bf16[484,128]{1,0:T(8,128)(2,1)S(1)} collective-permute-done((bf16[484,128]{1,0:T(8,128)(2,1)S(1)}, bf16[484,128]{1,0:T(8,128)(2,1)S(1)}, u32[]{:S(2)}, u32[]{:S(2)}) %collective-permute-start.3) | collective-permute-done | bytes 123936 | tf_op jit(solution)/shard_map/ppermute | solution.py:26
  61.7 0.7 convert_element_type.116
  62.5 8.8 %all-to-all-start = ((bf16[8,2,24,256]{3,2,1,0:T(8,128)(2,1)}), bf16[8,2,24,256]{3,2,1,0:T(8,128)(2,1)S(1)}, u32[]{:S(2)}, u32[]{:S(2)}) async-start(bf16[8,2,24,256]{3,2,1,0:T(8,128)(2,1)} %convert_element_type.116), calls=%async_computation | async-start | bytes 393216 | tf_op jit(solution)/shard_map/all_to_all | solution.py:138
  71.6 6.2 %all-to-all-done = bf16[8,2,24,256]{3,2,1,0:T(8,128)(2,1)S(1)} async-done(((bf16[8,2,24,256]{3,2,1,0:T(8,128)(2,1)}), bf16[8,2,24,256]{3,2,1,0:T(8,128)(2,1)S(1)}, u32[]{:S(2)}, u32[]{:S(2)}) %all-to-all-start) | async-done | bytes 196640 | tf_op jit(solution)/shard_map/all_to_all | solution.py:138
  78.0 1.0 multiply_subtract_fusion
  79.3 0.7 copy.54
  80.0 5.1 %all-to-all-start.1 = ((bf16[8,2,24,256]{3,2,1,0:T(8,128)(2,1)}), bf16[8,2,24,256]{3,2,1,0:T(8,128)(2,1)S(1)}, u32[]{:S(2)}, u32[]{:S(2)}) async-start(bf16[8,2,24,256]{3,2,1,0:T(8,128)(2,1)} %copy.54), calls=%async_computation.1 | async-start | bytes 393216 | tf_op jit(solution)/shard_map/all_to_all | solution.py:152
  85.1 0.6 fusion.23
  85.8 0.9 fusion.24
  86.8 0.7 fusion.22
  87.6 4.0 %all-to-all-done.1 = bf16[8,2,24,256]{3,2,1,0:T(8,128)(2,1)S(1)} async-done(((bf16[8,2,24,256]{3,2,1,0:T(8,128)(2,1)}), bf16[8,2,24,256]{3,2,1,0:T(8,128)(2,1)S(1)}, u32[]{:S(2)}, u32[]{:S(2)}) %all-to-all-start.1) | async-done | bytes 196640 | tf_op jit(solution)/shard_map/all_to_all | solution.py:152
  91.7 3.0 %collective-permute-start.4 = (bf16[999,128]{1,0:T(8,128)(2,1)S(1)}, bf16[999,128]{1,0:T(8,128)(2,1)S(1)}, u32[]{:S(2)}, u32[]{:S(2)}) collective-permute-start(bf16[999,128]{1,0:T(8,128)(2,1)S(1)} %pad_maximum_fusion.4), channel_id=1, source_target_pairs={{0,384},{128,0},{256,128},{384,256},{1,385},{129,1},{257,129},{385... | collective-permute-start | bytes 767240 | tf_op jit(solution)/shard_map/ppermute | solution.py:26
  94.8 6.1 %collective-permute-start.5 = (bf16[999,128]{1,0:T(8,128)(2,1)S(1)}, bf16[999,128]{1,0:T(8,128)(2,1)S(1)}, u32[]{:S(2)}, u32[]{:S(2)}) collective-permute-start(bf16[999,128]{1,0:T(8,128)(2,1)S(1)} %pad_maximum_fusion.4), channel_id=1, source_target_pairs={{0,128},{128,256},{256,384},{384,0},{1,129},{129,257},{257,385},{3... | collective-permute-start | bytes 767240 | tf_op jit(solution)/shard_map/ppermute | solution.py:22
  101.0 22.1 %collective-permute-done.4 = bf16[999,128]{1,0:T(8,128)(2,1)S(1)} collective-permute-done((bf16[999,128]{1,0:T(8,128)(2,1)S(1)}, bf16[999,128]{1,0:T(8,128)(2,1)S(1)}, u32[]{:S(2)}, u32[]{:S(2)}) %collective-permute-start.4) | collective-permute-done | bytes 255776 | tf_op jit(solution)/shard_map/ppermute | solution.py:26
  123.1 3.0 %collective-permute-start.7 = (bf16[500,128]{1,0:T(8,128)(2,1)S(1)}, bf16[500,128]{1,0:T(8,128)(2,1)S(1)}, u32[]{:S(2)}, u32[]{:S(2)}) collective-permute-start(bf16[500,128]{1,0:T(8,128)(2,1)S(1)} %slice.263), channel_id=1, source_target_pairs={{0,384},{128,0},{256,128},{384,256},{1,385},{129,1},{257,129},{385... | collective-permute-start | bytes 384008 | tf_op jit(solution)/shard_map/ppermute | solution.py:26
  126.1 6.2 %collective-permute-start.6 = (bf16[499,128]{1,0:T(8,128)(2,1)S(1)}, bf16[499,128]{1,0:T(8,128)(2,1)S(1)}, u32[]{:S(2)}, u32[]{:S(2)}) collective-permute-start(bf16[499,128]{1,0:T(8,128)(2,1)S(1)} %slice.262), channel_id=1, source_target_pairs={{0,128},{128,256},{256,384},{384,0},{1,129},{129,257},{257,385},{3... | collective-permute-start | bytes 383240 | tf_op jit(solution)/shard_map/ppermute | solution.py:22
  132.4 5.0 %collective-permute-done.6 = bf16[499,128]{1,0:T(8,128)(2,1)S(1)} collective-permute-done((bf16[499,128]{1,0:T(8,128)(2,1)S(1)}, bf16[499,128]{1,0:T(8,128)(2,1)S(1)}, u32[]{:S(2)}, u32[]{:S(2)}) %collective-permute-start.6) | collective-permute-done | bytes 127776 | tf_op jit(solution)/shard_map/ppermute | solution.py:22
  139.3 0.7 pad_maximum_fusion.10
  140.0 0.7 pad_maximum_fusion.9
  140.7 0.7 pad_maximum_fusion.8
  141.5 0.9 maximum_bitcast_fusion
  (98 shorter events, 4.7 us)
Async XLA Ops:
  0.6 4.4 %copy-start.4 = (bf16[1,64,768]{2,1,0:T(8,128)(2,1)S(1)}, bf16[1,64,768]{2,1,0:T(8,128)(2,1)}, u32[]{:S(2)}) copy-start(bf16[1,64,768]{2,1,0:T(8,128)(2,1)} %param.16) | copy-start | bytes 294916
  0.7 4.4 %copy-start.3 = (f32[64,192]{1,0:T(8,128)S(1)}, f32[64,192]{1,0:T(8,128)}, u32[]{:S(2)}) copy-start(f32[64,192]{1,0:T(8,128)} %param.20) | copy-start | bytes 147460
  2.7 3.1 %copy-start.1 = (bf16[1,1,2,768,256]{4,3,2,1,0:T(8,128)(2,1)S(1)}, bf16[1,1,2,768,256]{4,3,2,1,0:T(8,128)(2,1)}, u32[]{:S(2)}) copy-start(bf16[1,1,2,768,256]{4,3,2,1,0:T(8,128)(2,1)} %param.13) | copy-start | bytes 2359300
  6.2 15.5 %copy-start = (f32[1,2,24,2048]{3,2,1,0:T(8,128)S(1)}, f32[1,2,24,2048]{3,2,1,0:T(8,128)}, u32[]{:S(2)}) copy-start(f32[1,2,24,2048]{3,2,1,0:T(8,128)} %param.17) | copy-start | bytes 1179652
  6.5 20.4 %collective-permute-start = (bf16[999,128]{1,0:T(8,128)(2,1)S(1)}, bf16[999,128]{1,0:T(8,128)(2,1)S(1)}, u32[]{:S(2)}, u32[]{:S(2)}) collective-permute-start(bf16[999,128]{1,0:T(8,128)(2,1)S(1)} %pad_maximum_fusion.2), channel_id=1, source_target_pairs={{0,128},{128,256},{256,384},{384,0},{1,129},{129,257},{257,385},{3... | collective-permute-start | bytes 767240 | tf_op jit(solution)/shard_map/ppermute | solution.py:22
  16.2 31.5 %collective-permute-start.2 = (bf16[999,128]{1,0:T(8,128)(2,1)S(1)}, bf16[999,128]{1,0:T(8,128)(2,1)S(1)}, u32[]{:S(2)}, u32[]{:S(2)}) collective-permute-start(bf16[999,128]{1,0:T(8,128)(2,1)S(1)} %pad_maximum_fusion.3), channel_id=1, source_target_pairs={{0,384},{128,0},{256,128},{384,256},{1,385},{129,1},{257,129},{385... | collective-permute-start | bytes 767240 | tf_op jit(solution)/shard_map/ppermute | solution.py:26
  27.0 24.9 %collective-permute-start.1 = (bf16[483,128]{1,0:T(8,128)(2,1)S(1)}, bf16[483,128]{1,0:T(8,128)(2,1)S(1)}, u32[]{:S(2)}, u32[]{:S(2)}) collective-permute-start(bf16[483,128]{1,0:T(8,128)(2,1)S(1)} %pad_maximum_fusion.6), channel_id=1, source_target_pairs={{0,128},{128,256},{256,384},{384,0},{1,129},{129,257},{257,385},{3... | collective-permute-start | bytes 370952 | tf_op jit(solution)/shard_map/ppermute | solution.py:22
  47.8 13.8 %collective-permute-start.3 = (bf16[484,128]{1,0:T(8,128)(2,1)S(1)}, bf16[484,128]{1,0:T(8,128)(2,1)S(1)}, u32[]{:S(2)}, u32[]{:S(2)}) collective-permute-start(bf16[484,128]{1,0:T(8,128)(2,1)S(1)} %pad_maximum_fusion.7), channel_id=1, source_target_pairs={{0,384},{128,0},{256,128},{384,256},{1,385},{129,1},{257,129},{385... | collective-permute-start | bytes 371720 | tf_op jit(solution)/shard_map/ppermute | solution.py:26
  62.5 15.3 %all-to-all-start = ((bf16[8,2,24,256]{3,2,1,0:T(8,128)(2,1)}), bf16[8,2,24,256]{3,2,1,0:T(8,128)(2,1)S(1)}, u32[]{:S(2)}, u32[]{:S(2)}) async-start(bf16[8,2,24,256]{3,2,1,0:T(8,128)(2,1)} %convert_element_type.116), calls=%async_computation | async-start | bytes 393216 | tf_op jit(solution)/shard_map/all_to_all | solution.py:138
  71.3 6.7 %copy-start.2 = (f32[1,2,24,2048]{3,2,1,0:T(8,128)S(1)}, f32[1,2,24,2048]{3,2,1,0:T(8,128)}, u32[]{:S(2)}) copy-start(f32[1,2,24,2048]{3,2,1,0:T(8,128)} %param.21) | copy-start | bytes 1179652
  79.1 6.0 %copy-start.8 = (f32[18,192]{1,0:T(8,128)S(1)}, f32[18,192]{1,0:T(8,128)}, u32[]{:S(2)}) copy-start(f32[18,192]{1,0:T(8,128)} %param.19) | copy-start | bytes 41476
  79.1 6.0 %copy-start.9 = (f32[18,192]{1,0:T(8,128)S(1)}, f32[18,192]{1,0:T(8,128)}, u32[]{:S(2)}) copy-start(f32[18,192]{1,0:T(8,128)} %param.23) | copy-start | bytes 41476
  79.1 6.7 %copy-start.7 = (f32[64,192]{1,0:T(8,128)S(1)}, f32[64,192]{1,0:T(8,128)}, u32[]{:S(2)}) copy-start(f32[64,192]{1,0:T(8,128)} %param.24) | copy-start | bytes 147460
  79.1 7.6 %copy-start.5 = (f32[72,192]{1,0:T(8,128)S(1)}, f32[72,192]{1,0:T(8,128)}, u32[]{:S(2)}) copy-start(f32[72,192]{1,0:T(8,128)} %param.18) | copy-start | bytes 165892
  79.2 7.6 %copy-start.6 = (f32[72,192]{1,0:T(8,128)S(1)}, f32[72,192]{1,0:T(8,128)}, u32[]{:S(2)}) copy-start(f32[72,192]{1,0:T(8,128)} %param.22) | copy-start | bytes 165892
  80.0 11.6 %all-to-all-start.1 = ((bf16[8,2,24,256]{3,2,1,0:T(8,128)(2,1)}), bf16[8,2,24,256]{3,2,1,0:T(8,128)(2,1)S(1)}, u32[]{:S(2)}, u32[]{:S(2)}) async-start(bf16[8,2,24,256]{3,2,1,0:T(8,128)(2,1)} %copy.54), calls=%async_computation.1 | async-start | bytes 393216 | tf_op jit(solution)/shard_map/all_to_all | solution.py:152
  91.7 31.3 %collective-permute-start.4 = (bf16[999,128]{1,0:T(8,128)(2,1)S(1)}, bf16[999,128]{1,0:T(8,128)(2,1)S(1)}, u32[]{:S(2)}, u32[]{:S(2)}) collective-permute-start(bf16[999,128]{1,0:T(8,128)(2,1)S(1)} %pad_maximum_fusion.4), channel_id=1, source_target_pairs={{0,384},{128,0},{256,128},{384,256},{1,385},{129,1},{257,129},{385... | collective-permute-start | bytes 767240 | tf_op jit(solution)/shard_map/ppermute | solution.py:26
  94.8 31.3 %collective-permute-start.5 = (bf16[999,128]{1,0:T(8,128)(2,1)S(1)}, bf16[999,128]{1,0:T(8,128)(2,1)S(1)}, u32[]{:S(2)}, u32[]{:S(2)}) collective-permute-start(bf16[999,128]{1,0:T(8,128)(2,1)S(1)} %pad_maximum_fusion.4), channel_id=1, source_target_pairs={{0,128},{128,256},{256,384},{384,0},{1,129},{129,257},{257,385},{3... | collective-permute-start | bytes 767240 | tf_op jit(solution)/shard_map/ppermute | solution.py:22
  123.1 14.4 %collective-permute-start.7 = (bf16[500,128]{1,0:T(8,128)(2,1)S(1)}, bf16[500,128]{1,0:T(8,128)(2,1)S(1)}, u32[]{:S(2)}, u32[]{:S(2)}) collective-permute-start(bf16[500,128]{1,0:T(8,128)(2,1)S(1)} %slice.263), channel_id=1, source_target_pairs={{0,384},{128,0},{256,128},{384,256},{1,385},{129,1},{257,129},{385... | collective-permute-start | bytes 384008 | tf_op jit(solution)/shard_map/ppermute | solution.py:26
  126.1 11.3 %collective-permute-start.6 = (bf16[499,128]{1,0:T(8,128)(2,1)S(1)}, bf16[499,128]{1,0:T(8,128)(2,1)S(1)}, u32[]{:S(2)}, u32[]{:S(2)}) collective-permute-start(bf16[499,128]{1,0:T(8,128)(2,1)S(1)} %slice.262), channel_id=1, source_target_pairs={{0,128},{128,256},{256,384},{384,0},{1,129},{129,257},{257,385},{3... | collective-permute-start | bytes 383240 | tf_op jit(solution)/shard_map/ppermute | solution.py:22

commit v10 on v9

--- a/solution.py
+++ b/solution.py
@@ -111,8 +111,8 @@
     offset = lax.axis_index("rep") * col_count
     basis_part = lax.dynamic_slice_in_dim(embed_basis, offset, col_count, 0)
     partial_value = jnp.dot(
-        jnp.concatenate([outer_embed, inner_embed[0].astype(jnp.float32) / groups], axis=1),
-        jnp.concatenate([basis_part, -embed_basis], axis=0),
+        jnp.concatenate([outer_embed, inner_embed[0].astype(jnp.float32) * (-1.0 / groups)], axis=1),
+        jnp.concatenate([basis_part, embed_basis], axis=0),
         precision=hi_prec,
         preferred_element_type=jnp.float32,
     )

time: 144 us -> 142 us (0.986)
  no operation moved by 1% of the time
where the time goes in v10:
time: 142 us; the launch traced here: 141 us
  starting transfers between devices  71.1 us (50%)
  waiting for transfers between devices  53 us (37%)
  local copies, waits for them, and re-layouts  7.31 us (5%)
  other arithmetic  6.43 us (5%)
  between operations  1.42 us (1%)
    ppermute x4, starting transfers between devices, to_next(): lax.ppermute(x, 'rep', [(i, (i + 1) % groups) for i in range(groups)])  41.6 us
    ppermute x4, waiting for transfers between devices, to_prev(): lax.ppermute(x, 'rep', [(i, (i - 1) % groups) for i in range(groups)])  32.8 us
    ppermute x4, starting transfers between devices, to_prev(): lax.ppermute(x, 'rep', [(i, (i - 1) % groups) for i in range(groups)])  15.6 us
    ppermute x4, waiting for transfers between devices, to_next(): lax.ppermute(x, 'rep', [(i, (i + 1) % groups) for i in range(groups)])  9.97 us
    all_to_all x1, starting transfers between devices, on_device(): lax.all_to_all(ex_sum.astype(jnp.bfloat16), 'mdl', split_axis=0, concat_a...  8.85 us
    all_to_all x1, waiting for transfers between devices, on_device(): lax.all_to_all(ex_sum.astype(jnp.bfloat16), 'mdl', split_axis=0, concat_a...  6.23 us
    all_to_all x1, starting transfers between devices, on_device(): lax.all_to_all(expert_outer.astype(jnp.bfloat16).reshape(halves, own_rows...  5.08 us
    all_to_all x1, waiting for transfers between devices, on_device(): lax.all_to_all(expert_outer.astype(jnp.bfloat16).reshape(halves, own_rows...  4.03 us
  transfers between devices with their start and end apart: 10, of which 7 were waited for; matrix products, arithmetic and copies ran while one was open for 2% of the time, Pallas kernels for 0%

profile of v10, /device:TPU:1, one launch (start us, length us, event | category | flops | bytes accessed | tf_op | source)
XLA Modules:
  0.0 140.6 jit_solution(16514944806515902730)
XLA Ops:
  0.7 1.0 reshape_squeeze.11
  1.8 1.1 reshape_squeeze.10
  3.0 0.2 reshape_reshape.6
  3.4 0.5 subtract_convert_fusion
  4.1 0.3 reshape.194
  4.7 9.6 %collective-permute-start = (bf16[999,128]{1,0:T(8,128)(2,1)S(1)}, bf16[999,128]{1,0:T(8,128)(2,1)S(1)}, u32[]{:S(2)}, u32[]{:S(2)}) collective-permute-start(bf16[999,128]{1,0:T(8,128)(2,1)S(1)} %pad_maximum_fusion.2), channel_id=1, source_target_pairs={{0,128},{128,256},{256,384},{384,0},{1,129},{129,257},{257,385},{3... | collective-permute-start | bytes 767240 | tf_op jit(solution)/shard_map/ppermute | solution.py:22
  14.4 5.6 %collective-permute-start.2 = (bf16[999,128]{1,0:T(8,128)(2,1)S(1)}, bf16[999,128]{1,0:T(8,128)(2,1)S(1)}, u32[]{:S(2)}, u32[]{:S(2)}) collective-permute-start(bf16[999,128]{1,0:T(8,128)(2,1)S(1)} %pad_maximum_fusion.3), channel_id=1, source_target_pairs={{0,384},{128,0},{256,128},{384,256},{1,385},{129,1},{257,129},{385... | collective-permute-start | bytes 767240 | tf_op jit(solution)/shard_map/ppermute | solution.py:26
  20.2 5.1 %collective-permute-done = bf16[999,128]{1,0:T(8,128)(2,1)S(1)} collective-permute-done((bf16[999,128]{1,0:T(8,128)(2,1)S(1)}, bf16[999,128]{1,0:T(8,128)(2,1)S(1)}, u32[]{:S(2)}, u32[]{:S(2)}) %collective-permute-start) | collective-permute-done | bytes 255776 | tf_op jit(solution)/shard_map/ppermute | solution.py:22
  25.3 19.6 %collective-permute-start.1 = (bf16[483,128]{1,0:T(8,128)(2,1)S(1)}, bf16[483,128]{1,0:T(8,128)(2,1)S(1)}, u32[]{:S(2)}, u32[]{:S(2)}) collective-permute-start(bf16[483,128]{1,0:T(8,128)(2,1)S(1)} %pad_maximum_fusion.6), channel_id=1, source_target_pairs={{0,128},{128,256},{256,384},{384,0},{1,129},{129,257},{257,385},{3... | collective-permute-start | bytes 370952 | tf_op jit(solution)/shard_map/ppermute | solution.py:22
  44.9 1.1 collective-permute-done.2
  46.1 4.0 %collective-permute-start.3 = (bf16[484,128]{1,0:T(8,128)(2,1)S(1)}, bf16[484,128]{1,0:T(8,128)(2,1)S(1)}, u32[]{:S(2)}, u32[]{:S(2)}) collective-permute-start(bf16[484,128]{1,0:T(8,128)(2,1)S(1)} %pad_maximum_fusion.7), channel_id=1, source_target_pairs={{0,384},{128,0},{256,128},{384,256},{1,385},{129,1},{257,129},{385... | collective-permute-start | bytes 371720 | tf_op jit(solution)/shard_map/ppermute | solution.py:26
  50.2 9.6 %collective-permute-done.3 = bf16[484,128]{1,0:T(8,128)(2,1)S(1)} collective-permute-done((bf16[484,128]{1,0:T(8,128)(2,1)S(1)}, bf16[484,128]{1,0:T(8,128)(2,1)S(1)}, u32[]{:S(2)}, u32[]{:S(2)}) %collective-permute-start.3) | collective-permute-done | bytes 123936 | tf_op jit(solution)/shard_map/ppermute | solution.py:26
  60.0 0.7 convert_element_type.116
  60.7 8.8 %all-to-all-start = ((bf16[8,2,24,256]{3,2,1,0:T(8,128)(2,1)}), bf16[8,2,24,256]{3,2,1,0:T(8,128)(2,1)S(1)}, u32[]{:S(2)}, u32[]{:S(2)}) async-start(bf16[8,2,24,256]{3,2,1,0:T(8,128)(2,1)} %convert_element_type.116), calls=%async_computation | async-start | bytes 393216 | tf_op jit(solution)/shard_map/all_to_all | solution.py:138
  69.9 6.2 %all-to-all-done = bf16[8,2,24,256]{3,2,1,0:T(8,128)(2,1)S(1)} async-done(((bf16[8,2,24,256]{3,2,1,0:T(8,128)(2,1)}), bf16[8,2,24,256]{3,2,1,0:T(8,128)(2,1)S(1)}, u32[]{:S(2)}, u32[]{:S(2)}) %all-to-all-start) | async-done | bytes 196640 | tf_op jit(solution)/shard_map/all_to_all | solution.py:138
  76.3 1.0 multiply_subtract_fusion
  77.6 0.7 copy.54
  78.3 5.1 %all-to-all-start.1 = ((bf16[8,2,24,256]{3,2,1,0:T(8,128)(2,1)}), bf16[8,2,24,256]{3,2,1,0:T(8,128)(2,1)S(1)}, u32[]{:S(2)}, u32[]{:S(2)}) async-start(bf16[8,2,24,256]{3,2,1,0:T(8,128)(2,1)} %copy.54), calls=%async_computation.1 | async-start | bytes 393216 | tf_op jit(solution)/shard_map/all_to_all | solution.py:152
  83.4 0.6 fusion.23
  84.1 0.9 fusion.24
  85.1 0.7 fusion.22
  85.9 4.0 %all-to-all-done.1 = bf16[8,2,24,256]{3,2,1,0:T(8,128)(2,1)S(1)} async-done(((bf16[8,2,24,256]{3,2,1,0:T(8,128)(2,1)}), bf16[8,2,24,256]{3,2,1,0:T(8,128)(2,1)S(1)}, u32[]{:S(2)}, u32[]{:S(2)}) %all-to-all-start.1) | async-done | bytes 196640 | tf_op jit(solution)/shard_map/all_to_all | solution.py:152
  90.0 3.0 %collective-permute-start.4 = (bf16[999,128]{1,0:T(8,128)(2,1)S(1)}, bf16[999,128]{1,0:T(8,128)(2,1)S(1)}, u32[]{:S(2)}, u32[]{:S(2)}) collective-permute-start(bf16[999,128]{1,0:T(8,128)(2,1)S(1)} %pad_maximum_fusion.4), channel_id=1, source_target_pairs={{0,384},{128,0},{256,128},{384,256},{1,385},{129,1},{257,129},{385... | collective-permute-start | bytes 767240 | tf_op jit(solution)/shard_map/ppermute | solution.py:26
  93.0 6.2 %collective-permute-start.5 = (bf16[999,128]{1,0:T(8,128)(2,1)S(1)}, bf16[999,128]{1,0:T(8,128)(2,1)S(1)}, u32[]{:S(2)}, u32[]{:S(2)}) collective-permute-start(bf16[999,128]{1,0:T(8,128)(2,1)S(1)} %pad_maximum_fusion.4), channel_id=1, source_target_pairs={{0,128},{128,256},{256,384},{384,0},{1,129},{129,257},{257,385},{3... | collective-permute-start | bytes 767240 | tf_op jit(solution)/shard_map/ppermute | solution.py:22
  99.2 22.1 %collective-permute-done.4 = bf16[999,128]{1,0:T(8,128)(2,1)S(1)} collective-permute-done((bf16[999,128]{1,0:T(8,128)(2,1)S(1)}, bf16[999,128]{1,0:T(8,128)(2,1)S(1)}, u32[]{:S(2)}, u32[]{:S(2)}) %collective-permute-start.4) | collective-permute-done | bytes 255776 | tf_op jit(solution)/shard_map/ppermute | solution.py:26
  121.3 3.0 %collective-permute-start.7 = (bf16[500,128]{1,0:T(8,128)(2,1)S(1)}, bf16[500,128]{1,0:T(8,128)(2,1)S(1)}, u32[]{:S(2)}, u32[]{:S(2)}) collective-permute-start(bf16[500,128]{1,0:T(8,128)(2,1)S(1)} %slice.263), channel_id=1, source_target_pairs={{0,384},{128,0},{256,128},{384,256},{1,385},{129,1},{257,129},{385... | collective-permute-start | bytes 384008 | tf_op jit(solution)/shard_map/ppermute | solution.py:26
  124.4 6.2 %collective-permute-start.6 = (bf16[499,128]{1,0:T(8,128)(2,1)S(1)}, bf16[499,128]{1,0:T(8,128)(2,1)S(1)}, u32[]{:S(2)}, u32[]{:S(2)}) collective-permute-start(bf16[499,128]{1,0:T(8,128)(2,1)S(1)} %slice.262), channel_id=1, source_target_pairs={{0,128},{128,256},{256,384},{384,0},{1,129},{129,257},{257,385},{3... | collective-permute-start | bytes 383240 | tf_op jit(solution)/shard_map/ppermute | solution.py:22
  130.7 4.9 %collective-permute-done.6 = bf16[499,128]{1,0:T(8,128)(2,1)S(1)} collective-permute-done((bf16[499,128]{1,0:T(8,128)(2,1)S(1)}, bf16[499,128]{1,0:T(8,128)(2,1)S(1)}, u32[]{:S(2)}, u32[]{:S(2)}) %collective-permute-start.6) | collective-permute-done | bytes 127776 | tf_op jit(solution)/shard_map/ppermute | solution.py:22
  137.5 0.7 pad_maximum_fusion.10
  138.2 0.7 pad_maximum_fusion.9
  138.9 0.7 pad_maximum_fusion.8
  139.7 0.9 maximum_bitcast_fusion
  (99 shorter events, 4.3 us)
Async XLA Ops:
  0.6 2.6 %copy-start.5 = (bf16[1,64,768]{2,1,0:T(8,128)(2,1)S(1)}, bf16[1,64,768]{2,1,0:T(8,128)(2,1)}, u32[]{:S(2)}) copy-start(bf16[1,64,768]{2,1,0:T(8,128)(2,1)} %param.16) | copy-start | bytes 294916
  0.7 2.6 %copy-start.3 = (f32[768,64]{0,1:T(8,128)S(1)}, f32[768,64]{0,1:T(8,128)}, u32[]{:S(2)}) copy-start(f32[768,64]{0,1:T(8,128)} %param.25) | copy-start | bytes 589828
  0.7 2.7 %copy-start.4 = (f32[64,192]{1,0:T(8,128)S(1)}, f32[64,192]{1,0:T(8,128)}, u32[]{:S(2)}) copy-start(f32[64,192]{1,0:T(8,128)} %param.20) | copy-start | bytes 147460
  1.7 2.3 %copy-start.1 = (bf16[1,1,2,768,256]{4,3,2,1,0:T(8,128)(2,1)S(1)}, bf16[1,1,2,768,256]{4,3,2,1,0:T(8,128)(2,1)}, u32[]{:S(2)}) copy-start(bf16[1,1,2,768,256]{4,3,2,1,0:T(8,128)(2,1)} %param.13) | copy-start | bytes 2359300
  4.5 15.5 %copy-start = (f32[1,2,24,2048]{3,2,1,0:T(8,128)S(1)}, f32[1,2,24,2048]{3,2,1,0:T(8,128)}, u32[]{:S(2)}) copy-start(f32[1,2,24,2048]{3,2,1,0:T(8,128)} %param.17) | copy-start | bytes 1179652
  4.7 20.5 %collective-permute-start = (bf16[999,128]{1,0:T(8,128)(2,1)S(1)}, bf16[999,128]{1,0:T(8,128)(2,1)S(1)}, u32[]{:S(2)}, u32[]{:S(2)}) collective-permute-start(bf16[999,128]{1,0:T(8,128)(2,1)S(1)} %pad_maximum_fusion.2), channel_id=1, source_target_pairs={{0,128},{128,256},{256,384},{384,0},{1,129},{129,257},{257,385},{3... | collective-permute-start | bytes 767240 | tf_op jit(solution)/shard_map/ppermute | solution.py:22
  14.4 31.5 %collective-permute-start.2 = (bf16[999,128]{1,0:T(8,128)(2,1)S(1)}, bf16[999,128]{1,0:T(8,128)(2,1)S(1)}, u32[]{:S(2)}, u32[]{:S(2)}) collective-permute-start(bf16[999,128]{1,0:T(8,128)(2,1)S(1)} %pad_maximum_fusion.3), channel_id=1, source_target_pairs={{0,384},{128,0},{256,128},{384,256},{1,385},{129,1},{257,129},{385... | collective-permute-start | bytes 767240 | tf_op jit(solution)/shard_map/ppermute | solution.py:26
  25.3 24.8 %collective-permute-start.1 = (bf16[483,128]{1,0:T(8,128)(2,1)S(1)}, bf16[483,128]{1,0:T(8,128)(2,1)S(1)}, u32[]{:S(2)}, u32[]{:S(2)}) collective-permute-start(bf16[483,128]{1,0:T(8,128)(2,1)S(1)} %pad_maximum_fusion.6), channel_id=1, source_target_pairs={{0,128},{128,256},{256,384},{384,0},{1,129},{129,257},{257,385},{3... | collective-permute-start | bytes 370952 | tf_op jit(solution)/shard_map/ppermute | solution.py:22
  46.1 13.8 %collective-permute-start.3 = (bf16[484,128]{1,0:T(8,128)(2,1)S(1)}, bf16[484,128]{1,0:T(8,128)(2,1)S(1)}, u32[]{:S(2)}, u32[]{:S(2)}) collective-permute-start(bf16[484,128]{1,0:T(8,128)(2,1)S(1)} %pad_maximum_fusion.7), channel_id=1, source_target_pairs={{0,384},{128,0},{256,128},{384,256},{1,385},{129,1},{257,129},{385... | collective-permute-start | bytes 371720 | tf_op jit(solution)/shard_map/ppermute | solution.py:26
  60.7 15.4 %all-to-all-start = ((bf16[8,2,24,256]{3,2,1,0:T(8,128)(2,1)}), bf16[8,2,24,256]{3,2,1,0:T(8,128)(2,1)S(1)}, u32[]{:S(2)}, u32[]{:S(2)}) async-start(bf16[8,2,24,256]{3,2,1,0:T(8,128)(2,1)} %convert_element_type.116), calls=%async_computation | async-start | bytes 393216 | tf_op jit(solution)/shard_map/all_to_all | solution.py:138
  69.6 6.7 %copy-start.2 = (f32[1,2,24,2048]{3,2,1,0:T(8,128)S(1)}, f32[1,2,24,2048]{3,2,1,0:T(8,128)}, u32[]{:S(2)}) copy-start(f32[1,2,24,2048]{3,2,1,0:T(8,128)} %param.21) | copy-start | bytes 1179652
  77.4 6.0 %copy-start.9 = (f32[18,192]{1,0:T(8,128)S(1)}, f32[18,192]{1,0:T(8,128)}, u32[]{:S(2)}) copy-start(f32[18,192]{1,0:T(8,128)} %param.19) | copy-start | bytes 41476
  77.4 6.0 %copy-start.10 = (f32[18,192]{1,0:T(8,128)S(1)}, f32[18,192]{1,0:T(8,128)}, u32[]{:S(2)}) copy-start(f32[18,192]{1,0:T(8,128)} %param.23) | copy-start | bytes 41476
  77.4 6.7 %copy-start.8 = (f32[64,192]{1,0:T(8,128)S(1)}, f32[64,192]{1,0:T(8,128)}, u32[]{:S(2)}) copy-start(f32[64,192]{1,0:T(8,128)} %param.24) | copy-start | bytes 147460
  77.4 7.6 %copy-start.6 = (f32[72,192]{1,0:T(8,128)S(1)}, f32[72,192]{1,0:T(8,128)}, u32[]{:S(2)}) copy-start(f32[72,192]{1,0:T(8,128)} %param.18) | copy-start | bytes 165892
  77.4 7.6 %copy-start.7 = (f32[72,192]{1,0:T(8,128)S(1)}, f32[72,192]{1,0:T(8,128)}, u32[]{:S(2)}) copy-start(f32[72,192]{1,0:T(8,128)} %param.22) | copy-start | bytes 165892
  78.3 11.6 %all-to-all-start.1 = ((bf16[8,2,24,256]{3,2,1,0:T(8,128)(2,1)}), bf16[8,2,24,256]{3,2,1,0:T(8,128)(2,1)S(1)}, u32[]{:S(2)}, u32[]{:S(2)}) async-start(bf16[8,2,24,256]{3,2,1,0:T(8,128)(2,1)} %copy.54), calls=%async_computation.1 | async-start | bytes 393216 | tf_op jit(solution)/shard_map/all_to_all | solution.py:152
  90.0 31.3 %collective-permute-start.4 = (bf16[999,128]{1,0:T(8,128)(2,1)S(1)}, bf16[999,128]{1,0:T(8,128)(2,1)S(1)}, u32[]{:S(2)}, u32[]{:S(2)}) collective-permute-start(bf16[999,128]{1,0:T(8,128)(2,1)S(1)} %pad_maximum_fusion.4), channel_id=1, source_target_pairs={{0,384},{128,0},{256,128},{384,256},{1,385},{129,1},{257,129},{385... | collective-permute-start | bytes 767240 | tf_op jit(solution)/shard_map/ppermute | solution.py:26
  93.0 31.3 %collective-permute-start.5 = (bf16[999,128]{1,0:T(8,128)(2,1)S(1)}, bf16[999,128]{1,0:T(8,128)(2,1)S(1)}, u32[]{:S(2)}, u32[]{:S(2)}) collective-permute-start(bf16[999,128]{1,0:T(8,128)(2,1)S(1)} %pad_maximum_fusion.4), channel_id=1, source_target_pairs={{0,128},{128,256},{256,384},{384,0},{1,129},{129,257},{257,385},{3... | collective-permute-start | bytes 767240 | tf_op jit(solution)/shard_map/ppermute | solution.py:22
  121.3 14.2 %collective-permute-start.7 = (bf16[500,128]{1,0:T(8,128)(2,1)S(1)}, bf16[500,128]{1,0:T(8,128)(2,1)S(1)}, u32[]{:S(2)}, u32[]{:S(2)}) collective-permute-start(bf16[500,128]{1,0:T(8,128)(2,1)S(1)} %slice.263), channel_id=1, source_target_pairs={{0,384},{128,0},{256,128},{384,256},{1,385},{129,1},{257,129},{385... | collective-permute-start | bytes 384008 | tf_op jit(solution)/shard_map/ppermute | solution.py:26
  124.4 11.2 %collective-permute-start.6 = (bf16[499,128]{1,0:T(8,128)(2,1)S(1)}, bf16[499,128]{1,0:T(8,128)(2,1)S(1)}, u32[]{:S(2)}, u32[]{:S(2)}) collective-permute-start(bf16[499,128]{1,0:T(8,128)(2,1)S(1)} %slice.262), channel_id=1, source_target_pairs={{0,128},{128,256},{256,384},{384,0},{1,129},{129,257},{257,385},{3... | collective-permute-start | bytes 383240 | tf_op jit(solution)/shard_map/ppermute | solution.py:22

commit v11 on v10

--- a/solution.py
+++ b/solution.py
@@ -58,7 +58,7 @@
         + b_pp.astype(f32)
         + jnp.concatenate([c[h:], d[m - h :]]).astype(f32)
     )
-    return jnp.concatenate([first, second, raw])
+    return first, second, raw
 
 
 def rep_gather(flat, groups):
@@ -123,17 +123,26 @@
 
     sizes = [ex_send.shape[1], de_send.shape[1], sm_send.shape[1], pp.shape[0]]
     send = jnp.concatenate([ex_send, de_send, sm_send, pp_send], axis=1)
-    total = rep_exchange(send, pp.shape[0], groups)
+    first, second, raw = rep_exchange(send, pp.shape[0], groups)
+    h = first.shape[0]
+
+    def main_rows(lo, hi):
+        pieces = []
+        if lo < h:
+            pieces.append(first[lo : min(hi, h)])
+        if hi > h:
+            pieces.append(second[max(lo, h) - h : hi - h])
+        return pieces[0] if len(pieces) == 1 else jnp.concatenate(pieces)
+
     bounds = [0]
-    for s in sizes:
-        bounds.append(bounds[-1] + s)
-    parts = [total[bounds[i] : bounds[i + 1]] for i in range(4)]
-
-    ex_sum = parts[0].reshape(mdl_size, halves, own_rows, my_cols)
-    dense_sum = parts[1].reshape(outer_dense.shape)
-    small_sum = parts[2].reshape(outer_small.shape)
-    nhalf = parts[3].shape[0] // 2
-    coefficient = (parts[3][:nhalf] + parts[3][nhalf:]).reshape(partial_value.shape)
+    for n in sizes[:3]:
+        bounds.append(bounds[-1] + n)
+
+    ex_sum = main_rows(bounds[0], bounds[1]).reshape(mdl_size, halves, own_rows, my_cols)
+    dense_sum = main_rows(bounds[1], bounds[2]).reshape(outer_dense.shape)
+    small_sum = main_rows(bounds[2], bounds[3]).reshape(outer_small.shape)
+    nhalf = raw.shape[0] // 2
+    coefficient = (raw[:nhalf] + raw[nhalf:]).reshape(partial_value.shape)
 
     expert_sum = lax.all_to_all(
         ex_sum.astype(jnp.bfloat16), "mdl", split_axis=0, concat_axis=0, tiled=True

time: 142 us -> 143 us (level)
  waiting for transfers between devices: 53 us -> 51 us
  local copies, waits for them, and re-layouts: 7.31 us -> 9.29 us
  transfers between devices with their start and end apart: 10 -> 10, of which waited for: 7 -> 7; matrix products, arithmetic and copies ran while one was open for 2% -> 4% of each run, Pallas kernels for 0% -> 0%
where the time goes in v11:
time: 143 us; the launch traced here: 141 us
  starting transfers between devices  71.1 us (50%)
  waiting for transfers between devices  51 us (36%)
  local copies, waits for them, and re-layouts  9.29 us (6%)
  other arithmetic  7.16 us (5%)
  between operations  1.45 us (1%)
    ppermute x4, starting transfers between devices, to_next(): lax.ppermute(x, 'rep', [(i, (i + 1) % groups) for i in range(groups)])  41.5 us
    ppermute x4, waiting for transfers between devices, to_prev(): lax.ppermute(x, 'rep', [(i, (i - 1) % groups) for i in range(groups)])  32.7 us
    ppermute x4, starting transfers between devices, to_prev(): lax.ppermute(x, 'rep', [(i, (i - 1) % groups) for i in range(groups)])  15.7 us
    ppermute x4, waiting for transfers between devices, to_next(): lax.ppermute(x, 'rep', [(i, (i + 1) % groups) for i in range(groups)])  10.2 us
    all_to_all x1, starting transfers between devices, on_device(): lax.all_to_all(ex_sum.astype(jnp.bfloat16), 'mdl', split_axis=0, concat_a...  8.82 us
    all_to_all x1, starting transfers between devices, on_device(): lax.all_to_all(expert_outer.astype(jnp.bfloat16).reshape(halves, own_rows...  5.07 us
    all_to_all x1, waiting for transfers between devices, on_device(): lax.all_to_all(ex_sum.astype(jnp.bfloat16), 'mdl', split_axis=0, concat_a...  4.88 us
    all_to_all x1, waiting for transfers between devices, on_device(): lax.all_to_all(expert_outer.astype(jnp.bfloat16).reshape(halves, own_rows...  3.19 us
  transfers between devices with their start and end apart: 10, of which 7 were waited for; matrix products, arithmetic and copies ran while one was open for 4% of the time, Pallas kernels for 0%

profile of v11, /device:TPU:1, one launch (start us, length us, event | category | flops | bytes accessed | tf_op | source)
XLA Modules:
  0.0 141.3 jit_solution(17090473262689474330)
XLA Ops:
  0.7 1.0 reshape_squeeze.11
  1.8 1.1 reshape_squeeze.10
  4.7 9.6 %collective-permute-start = (bf16[999,128]{1,0:T(8,128)(2,1)S(1)}, bf16[999,128]{1,0:T(8,128)(2,1)S(1)}, u32[]{:S(2)}, u32[]{:S(2)}) collective-permute-start(bf16[999,128]{1,0:T(8,128)(2,1)S(1)} %pad_maximum_fusion.2), channel_id=1, source_target_pairs={{0,128},{128,256},{256,384},{384,0},{1,129},{129,257},{257,385},{3... | collective-permute-start | bytes 767240 | tf_op jit(solution)/shard_map/ppermute | solution.py:22
  14.4 5.6 %collective-permute-start.2 = (bf16[999,128]{1,0:T(8,128)(2,1)S(1)}, bf16[999,128]{1,0:T(8,128)(2,1)S(1)}, u32[]{:S(2)}, u32[]{:S(2)}) collective-permute-start(bf16[999,128]{1,0:T(8,128)(2,1)S(1)} %pad_maximum_fusion.3), channel_id=1, source_target_pairs={{0,384},{128,0},{256,128},{384,256},{1,385},{129,1},{257,129},{385... | collective-permute-start | bytes 767240 | tf_op jit(solution)/shard_map/ppermute | solution.py:26
  20.0 5.2 %collective-permute-done = bf16[999,128]{1,0:T(8,128)(2,1)S(1)} collective-permute-done((bf16[999,128]{1,0:T(8,128)(2,1)S(1)}, bf16[999,128]{1,0:T(8,128)(2,1)S(1)}, u32[]{:S(2)}, u32[]{:S(2)}) %collective-permute-start) | collective-permute-done | bytes 255776 | tf_op jit(solution)/shard_map/ppermute | solution.py:22
  25.3 19.5 %collective-permute-start.1 = (bf16[483,128]{1,0:T(8,128)(2,1)S(1)}, bf16[483,128]{1,0:T(8,128)(2,1)S(1)}, u32[]{:S(2)}, u32[]{:S(2)}) collective-permute-start(bf16[483,128]{1,0:T(8,128)(2,1)S(1)} %pad_maximum_fusion.6), channel_id=1, source_target_pairs={{0,128},{128,256},{256,384},{384,0},{1,129},{129,257},{257,385},{3... | collective-permute-start | bytes 370952 | tf_op jit(solution)/shard_map/ppermute | solution.py:22
  44.9 1.1 collective-permute-done.2
  46.1 4.1 %collective-permute-start.3 = (bf16[484,128]{1,0:T(8,128)(2,1)S(1)}, bf16[484,128]{1,0:T(8,128)(2,1)S(1)}, u32[]{:S(2)}, u32[]{:S(2)}) collective-permute-start(bf16[484,128]{1,0:T(8,128)(2,1)S(1)} %pad_maximum_fusion.7), channel_id=1, source_target_pairs={{0,384},{128,0},{256,128},{384,256},{1,385},{129,1},{257,129},{385... | collective-permute-start | bytes 371720 | tf_op jit(solution)/shard_map/ppermute | solution.py:26
  50.2 9.6 %collective-permute-done.3 = bf16[484,128]{1,0:T(8,128)(2,1)S(1)} collective-permute-done((bf16[484,128]{1,0:T(8,128)(2,1)S(1)}, bf16[484,128]{1,0:T(8,128)(2,1)S(1)}, u32[]{:S(2)}, u32[]{:S(2)}) %collective-permute-start.3) | collective-permute-done | bytes 123936 | tf_op jit(solution)/shard_map/ppermute | solution.py:26
  59.8 0.6 copy-done.7
  60.6 0.7 convert_element_type.116
  61.4 8.8 %all-to-all-start = ((bf16[8,2,24,256]{3,2,1,0:T(8,128)(2,1)}), bf16[8,2,24,256]{3,2,1,0:T(8,128)(2,1)S(1)}, u32[]{:S(2)}, u32[]{:S(2)}) async-start(bf16[8,2,24,256]{3,2,1,0:T(8,128)(2,1)} %convert_element_type.116), calls=%async_computation | async-start | bytes 393216 | tf_op jit(solution)/shard_map/all_to_all | solution.py:147
  70.4 0.7 div.35
  71.2 0.7 fusion.22
  71.9 4.9 %all-to-all-done = bf16[8,2,24,256]{3,2,1,0:T(8,128)(2,1)S(1)} async-done(((bf16[8,2,24,256]{3,2,1,0:T(8,128)(2,1)}), bf16[8,2,24,256]{3,2,1,0:T(8,128)(2,1)S(1)}, u32[]{:S(2)}, u32[]{:S(2)}) %all-to-all-start) | async-done | bytes 196640 | tf_op jit(solution)/shard_map/all_to_all | solution.py:147
  76.9 1.0 multiply_subtract_fusion
  78.2 0.7 copy.54
  78.9 5.1 %all-to-all-start.1 = ((bf16[8,2,24,256]{3,2,1,0:T(8,128)(2,1)}), bf16[8,2,24,256]{3,2,1,0:T(8,128)(2,1)S(1)}, u32[]{:S(2)}, u32[]{:S(2)}) async-start(bf16[8,2,24,256]{3,2,1,0:T(8,128)(2,1)} %copy.54), calls=%async_computation.1 | async-start | bytes 393216 | tf_op jit(solution)/shard_map/all_to_all | solution.py:161
  84.9 0.7 slice.260
  85.6 0.7 fusion.19
  86.4 0.9 fusion.24
  87.4 3.2 %all-to-all-done.1 = bf16[8,2,24,256]{3,2,1,0:T(8,128)(2,1)S(1)} async-done(((bf16[8,2,24,256]{3,2,1,0:T(8,128)(2,1)}), bf16[8,2,24,256]{3,2,1,0:T(8,128)(2,1)S(1)}, u32[]{:S(2)}, u32[]{:S(2)}) %all-to-all-start.1) | async-done | bytes 196640 | tf_op jit(solution)/shard_map/all_to_all | solution.py:161
  90.7 3.0 %collective-permute-start.4 = (bf16[999,128]{1,0:T(8,128)(2,1)S(1)}, bf16[999,128]{1,0:T(8,128)(2,1)S(1)}, u32[]{:S(2)}, u32[]{:S(2)}) collective-permute-start(bf16[999,128]{1,0:T(8,128)(2,1)S(1)} %pad_maximum_fusion.4), channel_id=1, source_target_pairs={{0,384},{128,0},{256,128},{384,256},{1,385},{129,1},{257,129},{385... | collective-permute-start | bytes 767240 | tf_op jit(solution)/shard_map/ppermute | solution.py:26
  93.7 6.2 %collective-permute-start.5 = (bf16[999,128]{1,0:T(8,128)(2,1)S(1)}, bf16[999,128]{1,0:T(8,128)(2,1)S(1)}, u32[]{:S(2)}, u32[]{:S(2)}) collective-permute-start(bf16[999,128]{1,0:T(8,128)(2,1)S(1)} %pad_maximum_fusion.4), channel_id=1, source_target_pairs={{0,128},{128,256},{256,384},{384,0},{1,129},{129,257},{257,385},{3... | collective-permute-start | bytes 767240 | tf_op jit(solution)/shard_map/ppermute | solution.py:22
  99.9 22.0 %collective-permute-done.4 = bf16[999,128]{1,0:T(8,128)(2,1)S(1)} collective-permute-done((bf16[999,128]{1,0:T(8,128)(2,1)S(1)}, bf16[999,128]{1,0:T(8,128)(2,1)S(1)}, u32[]{:S(2)}, u32[]{:S(2)}) %collective-permute-start.4) | collective-permute-done | bytes 255776 | tf_op jit(solution)/shard_map/ppermute | solution.py:26
  122.0 3.0 %collective-permute-start.7 = (bf16[500,128]{1,0:T(8,128)(2,1)S(1)}, bf16[500,128]{1,0:T(8,128)(2,1)S(1)}, u32[]{:S(2)}, u32[]{:S(2)}) collective-permute-start(bf16[500,128]{1,0:T(8,128)(2,1)S(1)} %slice.264), channel_id=1, source_target_pairs={{0,384},{128,0},{256,128},{384,256},{1,385},{129,1},{257,129},{385... | collective-permute-start | bytes 384008 | tf_op jit(solution)/shard_map/ppermute | solution.py:26
  125.0 6.2 %collective-permute-start.6 = (bf16[499,128]{1,0:T(8,128)(2,1)S(1)}, bf16[499,128]{1,0:T(8,128)(2,1)S(1)}, u32[]{:S(2)}, u32[]{:S(2)}) collective-permute-start(bf16[499,128]{1,0:T(8,128)(2,1)S(1)} %slice.263), channel_id=1, source_target_pairs={{0,128},{128,256},{256,384},{384,0},{1,129},{129,257},{257,385},{3... | collective-permute-start | bytes 383240 | tf_op jit(solution)/shard_map/ppermute | solution.py:22
  131.3 5.0 %collective-permute-done.6 = bf16[499,128]{1,0:T(8,128)(2,1)S(1)} collective-permute-done((bf16[499,128]{1,0:T(8,128)(2,1)S(1)}, bf16[499,128]{1,0:T(8,128)(2,1)S(1)}, u32[]{:S(2)}, u32[]{:S(2)}) %collective-permute-start.6) | collective-permute-done | bytes 127776 | tf_op jit(solution)/shard_map/ppermute | solution.py:22
  138.2 0.7 pad_maximum_fusion.10
  138.9 0.7 pad_maximum_fusion.9
  139.6 0.7 pad_maximum_fusion.8
  140.3 0.9 maximum_bitcast_fusion
  (108 shorter events, 5.8 us)
Async XLA Ops:
  0.6 2.6 %copy-start.8 = (bf16[1,64,768]{2,1,0:T(8,128)(2,1)S(1)}, bf16[1,64,768]{2,1,0:T(8,128)(2,1)}, u32[]{:S(2)}) copy-start(bf16[1,64,768]{2,1,0:T(8,128)(2,1)} %param.16) | copy-start | bytes 294916
  0.7 2.6 %copy-start.3 = (f32[768,64]{0,1:T(8,128)S(1)}, f32[768,64]{0,1:T(8,128)}, u32[]{:S(2)}) copy-start(f32[768,64]{0,1:T(8,128)} %param.25) | copy-start | bytes 589828
  0.7 2.7 %copy-start.4 = (f32[64,192]{1,0:T(8,128)S(1)}, f32[64,192]{1,0:T(8,128)}, u32[]{:S(2)}) copy-start(f32[64,192]{1,0:T(8,128)} %param.20) | copy-start | bytes 147460
  1.7 2.3 %copy-start.1 = (bf16[1,1,2,768,256]{4,3,2,1,0:T(8,128)(2,1)S(1)}, bf16[1,1,2,768,256]{4,3,2,1,0:T(8,128)(2,1)}, u32[]{:S(2)}) copy-start(bf16[1,1,2,768,256]{4,3,2,1,0:T(8,128)(2,1)} %param.13) | copy-start | bytes 2359300
  4.7 20.5 %collective-permute-start = (bf16[999,128]{1,0:T(8,128)(2,1)S(1)}, bf16[999,128]{1,0:T(8,128)(2,1)S(1)}, u32[]{:S(2)}, u32[]{:S(2)}) collective-permute-start(bf16[999,128]{1,0:T(8,128)(2,1)S(1)} %pad_maximum_fusion.2), channel_id=1, source_target_pairs={{0,128},{128,256},{256,384},{384,0},{1,129},{129,257},{257,385},{3... | collective-permute-start | bytes 767240 | tf_op jit(solution)/shard_map/ppermute | solution.py:22
  14.4 31.5 %collective-permute-start.2 = (bf16[999,128]{1,0:T(8,128)(2,1)S(1)}, bf16[999,128]{1,0:T(8,128)(2,1)S(1)}, u32[]{:S(2)}, u32[]{:S(2)}) collective-permute-start(bf16[999,128]{1,0:T(8,128)(2,1)S(1)} %pad_maximum_fusion.3), channel_id=1, source_target_pairs={{0,384},{128,0},{256,128},{384,256},{1,385},{129,1},{257,129},{385... | collective-permute-start | bytes 767240 | tf_op jit(solution)/shard_map/ppermute | solution.py:26
  25.3 35.3 %copy-start.5 = (bf16[999,128]{1,0:T(8,128)(2,1)}, bf16[999,128]{1,0:T(8,128)(2,1)S(1)}, u32[]{:S(2)}) copy-start(bf16[999,128]{1,0:T(8,128)(2,1)S(1)} %collective-permute-done) | copy-start | bytes 767236
  25.3 24.8 %collective-permute-start.1 = (bf16[483,128]{1,0:T(8,128)(2,1)S(1)}, bf16[483,128]{1,0:T(8,128)(2,1)S(1)}, u32[]{:S(2)}, u32[]{:S(2)}) collective-permute-start(bf16[483,128]{1,0:T(8,128)(2,1)S(1)} %pad_maximum_fusion.6), channel_id=1, source_target_pairs={{0,128},{128,256},{256,384},{384,0},{1,129},{129,257},{257,385},{3... | collective-permute-start | bytes 370952 | tf_op jit(solution)/shard_map/ppermute | solution.py:22
  46.1 13.8 %collective-permute-start.3 = (bf16[484,128]{1,0:T(8,128)(2,1)S(1)}, bf16[484,128]{1,0:T(8,128)(2,1)S(1)}, u32[]{:S(2)}, u32[]{:S(2)}) collective-permute-start(bf16[484,128]{1,0:T(8,128)(2,1)S(1)} %pad_maximum_fusion.7), channel_id=1, source_target_pairs={{0,384},{128,0},{256,128},{384,256},{1,385},{129,1},{257,129},{385... | collective-permute-start | bytes 371720 | tf_op jit(solution)/shard_map/ppermute | solution.py:26
  50.2 20.0 %copy-start = (f32[1,2,24,2048]{3,2,1,0:T(8,128)S(1)}, f32[1,2,24,2048]{3,2,1,0:T(8,128)}, u32[]{:S(2)}) copy-start(f32[1,2,24,2048]{3,2,1,0:T(8,128)} %param.17) | copy-start | bytes 1179652
  59.8 0.6 copy-start.7
  60.6 10.5 %copy-start.10 = (f32[72,192]{1,0:T(8,128)S(1)}, f32[72,192]{1,0:T(8,128)}, u32[]{:S(2)}) copy-start(f32[72,192]{1,0:T(8,128)} %param.18) | copy-start | bytes 165892
  60.6 10.5 %copy-start.11 = (f32[72,192]{1,0:T(8,128)S(1)}, f32[72,192]{1,0:T(8,128)}, u32[]{:S(2)}) copy-start(f32[72,192]{1,0:T(8,128)} %param.22) | copy-start | bytes 165892
  61.4 15.4 %all-to-all-start = ((bf16[8,2,24,256]{3,2,1,0:T(8,128)(2,1)}), bf16[8,2,24,256]{3,2,1,0:T(8,128)(2,1)S(1)}, u32[]{:S(2)}, u32[]{:S(2)}) async-start(bf16[8,2,24,256]{3,2,1,0:T(8,128)(2,1)} %convert_element_type.116), calls=%async_computation | async-start | bytes 393216 | tf_op jit(solution)/shard_map/all_to_all | solution.py:147
  70.4 6.5 %copy-start.2 = (f32[1,2,24,2048]{3,2,1,0:T(8,128)S(1)}, f32[1,2,24,2048]{3,2,1,0:T(8,128)}, u32[]{:S(2)}) copy-start(f32[1,2,24,2048]{3,2,1,0:T(8,128)} %param.21) | copy-start | bytes 1179652
  78.0 6.0 %copy-start.9 = (f32[18,192]{1,0:T(8,128)S(1)}, f32[18,192]{1,0:T(8,128)}, u32[]{:S(2)}) copy-start(f32[18,192]{1,0:T(8,128)} %div.35) | copy-start | bytes 41476
  78.0 6.0 %copy-start.13 = (f32[18,192]{1,0:T(8,128)S(1)}, f32[18,192]{1,0:T(8,128)}, u32[]{:S(2)}) copy-start(f32[18,192]{1,0:T(8,128)} %param.19) | copy-start | bytes 41476
  78.1 6.0 %copy-start.14 = (f32[18,192]{1,0:T(8,128)S(1)}, f32[18,192]{1,0:T(8,128)}, u32[]{:S(2)}) copy-start(f32[18,192]{1,0:T(8,128)} %param.23) | copy-start | bytes 41476
  78.1 6.7 %copy-start.6 = (bf16[72,192]{1,0:T(8,128)(2,1)S(1)}, bf16[72,192]{1,0:T(8,128)(2,1)}, u32[]{:S(2)}) copy-start(bf16[72,192]{1,0:T(8,128)(2,1)} %get-tuple-element.12) | copy-start | bytes 82948
  78.1 8.3 %copy-start.12 = (f32[64,192]{1,0:T(8,128)S(1)}, f32[64,192]{1,0:T(8,128)}, u32[]{:S(2)}) copy-start(f32[64,192]{1,0:T(8,128)} %param.24) | copy-start | bytes 147460
  78.9 11.6 %all-to-all-start.1 = ((bf16[8,2,24,256]{3,2,1,0:T(8,128)(2,1)}), bf16[8,2,24,256]{3,2,1,0:T(8,128)(2,1)S(1)}, u32[]{:S(2)}, u32[]{:S(2)}) async-start(bf16[8,2,24,256]{3,2,1,0:T(8,128)(2,1)} %copy.54), calls=%async_computation.1 | async-start | bytes 393216 | tf_op jit(solution)/shard_map/all_to_all | solution.py:161
  90.7 31.3 %collective-permute-start.4 = (bf16[999,128]{1,0:T(8,128)(2,1)S(1)}, bf16[999,128]{1,0:T(8,128)(2,1)S(1)}, u32[]{:S(2)}, u32[]{:S(2)}) collective-permute-start(bf16[999,128]{1,0:T(8,128)(2,1)S(1)} %pad_maximum_fusion.4), channel_id=1, source_target_pairs={{0,384},{128,0},{256,128},{384,256},{1,385},{129,1},{257,129},{385... | collective-permute-start | bytes 767240 | tf_op jit(solution)/shard_map/ppermute | solution.py:26
  93.7 31.3 %collective-permute-start.5 = (bf16[999,128]{1,0:T(8,128)(2,1)S(1)}, bf16[999,128]{1,0:T(8,128)(2,1)S(1)}, u32[]{:S(2)}, u32[]{:S(2)}) collective-permute-start(bf16[999,128]{1,0:T(8,128)(2,1)S(1)} %pad_maximum_fusion.4), channel_id=1, source_target_pairs={{0,128},{128,256},{256,384},{384,0},{1,129},{129,257},{257,385},{3... | collective-permute-start | bytes 767240 | tf_op jit(solution)/shard_map/ppermute | solution.py:22
  122.0 14.3 %collective-permute-start.7 = (bf16[500,128]{1,0:T(8,128)(2,1)S(1)}, bf16[500,128]{1,0:T(8,128)(2,1)S(1)}, u32[]{:S(2)}, u32[]{:S(2)}) collective-permute-start(bf16[500,128]{1,0:T(8,128)(2,1)S(1)} %slice.264), channel_id=1, source_target_pairs={{0,384},{128,0},{256,128},{384,256},{1,385},{129,1},{257,129},{385... | collective-permute-start | bytes 384008 | tf_op jit(solution)/shard_map/ppermute | solution.py:26
  125.0 11.2 %collective-permute-start.6 = (bf16[499,128]{1,0:T(8,128)(2,1)S(1)}, bf16[499,128]{1,0:T(8,128)(2,1)S(1)}, u32[]{:S(2)}, u32[]{:S(2)}) collective-permute-start(bf16[499,128]{1,0:T(8,128)(2,1)S(1)} %slice.263), channel_id=1, source_target_pairs={{0,128},{128,256},{256,384},{384,0},{1,129},{129,257},{257,385},{3... | collective-permute-start | bytes 383240 | tf_op jit(solution)/shard_map/ppermute | solution.py:22

commit v12 on v10

--- a/solution.py
+++ b/solution.py
@@ -71,8 +71,16 @@
     far_a = to_next(from_prev[:half], groups)
     far_b = to_prev(from_next[half:], groups)
     far = jnp.concatenate([far_a, far_b])
-    rel = jnp.stack([flat, from_next, far, from_prev])
-    return [lax.dynamic_index_in_dim(rel, (j - me) % groups, 0, False) for j in range(groups)]
+    rel = [flat, from_next, far, from_prev]
+
+    def pick(j):
+        d_of_j = (j - me) % groups
+        out = rel[0]
+        for d in range(1, groups):
+            out = jnp.where(d_of_j == d, rel[d], out)
+        return out
+
+    return [pick(j) for j in range(groups)]
 
 
 def on_device(

time: 142 us -> 143 us (level)
  no operation moved by 1% of the time
where the time goes in v12:
time: 143 us; the launch traced here: 141 us
  starting transfers between devices  71.1 us (50%)
  waiting for transfers between devices  53 us (37%)
  local copies, waits for them, and re-layouts  7.77 us (5%)
  other arithmetic  6.68 us (5%)
  between operations  1.53 us (1%)
    ppermute x4, starting transfers between devices, to_next(): lax.ppermute(x, 'rep', [(i, (i + 1) % groups) for i in range(groups)])  41.5 us
    ppermute x4, waiting for transfers between devices, to_prev(): lax.ppermute(x, 'rep', [(i, (i - 1) % groups) for i in range(groups)])  32.8 us
    ppermute x4, starting transfers between devices, to_prev(): lax.ppermute(x, 'rep', [(i, (i - 1) % groups) for i in range(groups)])  15.6 us
    ppermute x4, waiting for transfers between devices, to_next(): lax.ppermute(x, 'rep', [(i, (i + 1) % groups) for i in range(groups)])  10 us
    all_to_all x1, starting transfers between devices, on_device(): lax.all_to_all(ex_sum.astype(jnp.bfloat16), 'mdl', split_axis=0, concat_a...  8.85 us
    all_to_all x1, waiting for transfers between devices, on_device(): lax.all_to_all(ex_sum.astype(jnp.bfloat16), 'mdl', split_axis=0, concat_a...  6.23 us
    all_to_all x1, starting transfers between devices, on_device(): lax.all_to_all(expert_outer.astype(jnp.bfloat16).reshape(halves, own_rows...  5.08 us
    all_to_all x1, waiting for transfers between devices, on_device(): lax.all_to_all(expert_outer.astype(jnp.bfloat16).reshape(halves, own_rows...  4.03 us
  transfers between devices with their start and end apart: 10, of which 7 were waited for; matrix products, arithmetic and copies ran while one was open for 2% of the time, Pallas kernels for 0%

profile of v12, /device:TPU:1, one launch (start us, length us, event | category | flops | bytes accessed | tf_op | source)
XLA Modules:
  0.0 141.4 jit_solution(8142464287271225195)
XLA Ops:
  0.7 1.0 reshape_squeeze.11
  1.8 1.1 reshape_squeeze.10
  3.3 0.5 subtract_convert_fusion
  4.7 9.6 %collective-permute-start = (bf16[999,128]{1,0:T(8,128)(2,1)S(1)}, bf16[999,128]{1,0:T(8,128)(2,1)S(1)}, u32[]{:S(2)}, u32[]{:S(2)}) collective-permute-start(bf16[999,128]{1,0:T(8,128)(2,1)S(1)} %pad_maximum_fusion.1), channel_id=1, source_target_pairs={{0,128},{128,256},{256,384},{384,0},{1,129},{129,257},{257,385},{3... | collective-permute-start | bytes 767240 | tf_op jit(solution)/shard_map/ppermute | solution.py:22
  14.4 5.6 %collective-permute-start.2 = (bf16[999,128]{1,0:T(8,128)(2,1)S(1)}, bf16[999,128]{1,0:T(8,128)(2,1)S(1)}, u32[]{:S(2)}, u32[]{:S(2)}) collective-permute-start(bf16[999,128]{1,0:T(8,128)(2,1)S(1)} %pad_maximum_fusion.2), channel_id=1, source_target_pairs={{0,384},{128,0},{256,128},{384,256},{1,385},{129,1},{257,129},{385... | collective-permute-start | bytes 767240 | tf_op jit(solution)/shard_map/ppermute | solution.py:26
  20.2 5.1 %collective-permute-done = bf16[999,128]{1,0:T(8,128)(2,1)S(1)} collective-permute-done((bf16[999,128]{1,0:T(8,128)(2,1)S(1)}, bf16[999,128]{1,0:T(8,128)(2,1)S(1)}, u32[]{:S(2)}, u32[]{:S(2)}) %collective-permute-start) | collective-permute-done | bytes 255776 | tf_op jit(solution)/shard_map/ppermute | solution.py:22
  25.3 19.6 %collective-permute-start.1 = (bf16[483,128]{1,0:T(8,128)(2,1)S(1)}, bf16[483,128]{1,0:T(8,128)(2,1)S(1)}, u32[]{:S(2)}, u32[]{:S(2)}) collective-permute-start(bf16[483,128]{1,0:T(8,128)(2,1)S(1)} %pad_maximum_fusion.6), channel_id=1, source_target_pairs={{0,128},{128,256},{256,384},{384,0},{1,129},{129,257},{257,385},{3... | collective-permute-start | bytes 370952 | tf_op jit(solution)/shard_map/ppermute | solution.py:22
  44.9 1.1 collective-permute-done.2
  46.1 4.0 %collective-permute-start.3 = (bf16[484,128]{1,0:T(8,128)(2,1)S(1)}, bf16[484,128]{1,0:T(8,128)(2,1)S(1)}, u32[]{:S(2)}, u32[]{:S(2)}) collective-permute-start(bf16[484,128]{1,0:T(8,128)(2,1)S(1)} %pad_maximum_fusion.7), channel_id=1, source_target_pairs={{0,384},{128,0},{256,128},{384,256},{1,385},{129,1},{257,129},{385... | collective-permute-start | bytes 371720 | tf_op jit(solution)/shard_map/ppermute | solution.py:26
  50.2 9.6 %collective-permute-done.3 = bf16[484,128]{1,0:T(8,128)(2,1)S(1)} collective-permute-done((bf16[484,128]{1,0:T(8,128)(2,1)S(1)}, bf16[484,128]{1,0:T(8,128)(2,1)S(1)}, u32[]{:S(2)}, u32[]{:S(2)}) %collective-permute-start.3) | collective-permute-done | bytes 123936 | tf_op jit(solution)/shard_map/ppermute | solution.py:26
  60.0 0.7 convert_element_type.116
  60.7 8.8 %all-to-all-start = ((bf16[8,2,24,256]{3,2,1,0:T(8,128)(2,1)}), bf16[8,2,24,256]{3,2,1,0:T(8,128)(2,1)S(1)}, u32[]{:S(2)}, u32[]{:S(2)}) async-start(bf16[8,2,24,256]{3,2,1,0:T(8,128)(2,1)} %convert_element_type.116), calls=%async_computation | async-start | bytes 393216 | tf_op jit(solution)/shard_map/all_to_all | solution.py:146
  69.9 6.2 %all-to-all-done = bf16[8,2,24,256]{3,2,1,0:T(8,128)(2,1)S(1)} async-done(((bf16[8,2,24,256]{3,2,1,0:T(8,128)(2,1)}), bf16[8,2,24,256]{3,2,1,0:T(8,128)(2,1)S(1)}, u32[]{:S(2)}, u32[]{:S(2)}) %all-to-all-start) | async-done | bytes 196640 | tf_op jit(solution)/shard_map/all_to_all | solution.py:146
  76.2 1.0 multiply_subtract_fusion
  77.6 0.7 copy.54
  78.3 5.1 %all-to-all-start.1 = ((bf16[8,2,24,256]{3,2,1,0:T(8,128)(2,1)}), bf16[8,2,24,256]{3,2,1,0:T(8,128)(2,1)S(1)}, u32[]{:S(2)}, u32[]{:S(2)}) async-start(bf16[8,2,24,256]{3,2,1,0:T(8,128)(2,1)} %copy.54), calls=%async_computation.1 | async-start | bytes 393216 | tf_op jit(solution)/shard_map/all_to_all | solution.py:160
  83.4 0.6 fusion.23
  84.1 0.9 fusion.24
  85.1 0.7 fusion.22
  85.9 4.0 %all-to-all-done.1 = bf16[8,2,24,256]{3,2,1,0:T(8,128)(2,1)S(1)} async-done(((bf16[8,2,24,256]{3,2,1,0:T(8,128)(2,1)}), bf16[8,2,24,256]{3,2,1,0:T(8,128)(2,1)S(1)}, u32[]{:S(2)}, u32[]{:S(2)}) %all-to-all-start.1) | async-done | bytes 196640 | tf_op jit(solution)/shard_map/all_to_all | solution.py:160
  90.0 3.0 %collective-permute-start.6 = (bf16[999,128]{1,0:T(8,128)(2,1)S(1)}, bf16[999,128]{1,0:T(8,128)(2,1)S(1)}, u32[]{:S(2)}, u32[]{:S(2)}) collective-permute-start(bf16[999,128]{1,0:T(8,128)(2,1)S(1)} %pad_maximum_fusion.3), channel_id=1, source_target_pairs={{0,384},{128,0},{256,128},{384,256},{1,385},{129,1},{257,129},{385... | collective-permute-start | bytes 767240 | tf_op jit(solution)/shard_map/ppermute | solution.py:26
  93.0 6.2 %collective-permute-start.4 = (bf16[999,128]{1,0:T(8,128)(2,1)S(1)}, bf16[999,128]{1,0:T(8,128)(2,1)S(1)}, u32[]{:S(2)}, u32[]{:S(2)}) collective-permute-start(bf16[999,128]{1,0:T(8,128)(2,1)S(1)} %pad_maximum_fusion.3), channel_id=1, source_target_pairs={{0,128},{128,256},{256,384},{384,0},{1,129},{129,257},{257,385},{3... | collective-permute-start | bytes 767240 | tf_op jit(solution)/shard_map/ppermute | solution.py:22
  99.2 22.1 %collective-permute-done.6 = bf16[999,128]{1,0:T(8,128)(2,1)S(1)} collective-permute-done((bf16[999,128]{1,0:T(8,128)(2,1)S(1)}, bf16[999,128]{1,0:T(8,128)(2,1)S(1)}, u32[]{:S(2)}, u32[]{:S(2)}) %collective-permute-start.6) | collective-permute-done | bytes 255776 | tf_op jit(solution)/shard_map/ppermute | solution.py:26
  121.3 3.0 %collective-permute-start.7 = (bf16[500,128]{1,0:T(8,128)(2,1)S(1)}, bf16[500,128]{1,0:T(8,128)(2,1)S(1)}, u32[]{:S(2)}, u32[]{:S(2)}) collective-permute-start(bf16[500,128]{1,0:T(8,128)(2,1)S(1)} %slice.247), channel_id=1, source_target_pairs={{0,384},{128,0},{256,128},{384,256},{1,385},{129,1},{257,129},{385... | collective-permute-start | bytes 384008 | tf_op jit(solution)/shard_map/ppermute | solution.py:26
  124.4 6.2 %collective-permute-start.5 = (bf16[499,128]{1,0:T(8,128)(2,1)S(1)}, bf16[499,128]{1,0:T(8,128)(2,1)S(1)}, u32[]{:S(2)}, u32[]{:S(2)}) collective-permute-start(bf16[499,128]{1,0:T(8,128)(2,1)S(1)} %slice.246), channel_id=1, source_target_pairs={{0,128},{128,256},{256,384},{384,0},{1,129},{129,257},{257,385},{3... | collective-permute-start | bytes 383240 | tf_op jit(solution)/shard_map/ppermute | solution.py:22
  130.6 4.9 %collective-permute-done.5 = bf16[499,128]{1,0:T(8,128)(2,1)S(1)} collective-permute-done((bf16[499,128]{1,0:T(8,128)(2,1)S(1)}, bf16[499,128]{1,0:T(8,128)(2,1)S(1)}, u32[]{:S(2)}, u32[]{:S(2)}) %collective-permute-start.5) | collective-permute-done | bytes 127776 | tf_op jit(solution)/shard_map/ppermute | solution.py:22
  135.6 0.3 select_select_fusion.3
  137.7 0.4 slice-done.1
  138.3 0.7 pad_maximum_fusion.10
  139.0 0.7 pad_maximum_fusion.9
  139.8 0.9 maximum_bitcast_fusion
  140.7 0.7 pad_maximum_fusion.8
  (114 shorter events, 4.8 us)
Async XLA Ops:
  0.6 2.6 %copy-start.6 = (bf16[1,64,768]{2,1,0:T(8,128)(2,1)S(1)}, bf16[1,64,768]{2,1,0:T(8,128)(2,1)}, u32[]{:S(2)}) copy-start(bf16[1,64,768]{2,1,0:T(8,128)(2,1)} %param.16) | copy-start | bytes 294916
  0.7 2.6 %copy-start.4 = (f32[768,64]{0,1:T(8,128)S(1)}, f32[768,64]{0,1:T(8,128)}, u32[]{:S(2)}) copy-start(f32[768,64]{0,1:T(8,128)} %param.25) | copy-start | bytes 589828
  0.7 2.7 %copy-start.5 = (f32[64,192]{1,0:T(8,128)S(1)}, f32[64,192]{1,0:T(8,128)}, u32[]{:S(2)}) copy-start(f32[64,192]{1,0:T(8,128)} %param.20) | copy-start | bytes 147460
  1.7 2.3 %copy-start.2 = (bf16[1,1,2,768,256]{4,3,2,1,0:T(8,128)(2,1)S(1)}, bf16[1,1,2,768,256]{4,3,2,1,0:T(8,128)(2,1)}, u32[]{:S(2)}) copy-start(bf16[1,1,2,768,256]{4,3,2,1,0:T(8,128)(2,1)} %param.13) | copy-start | bytes 2359300
  4.5 15.5 %copy-start = (f32[1,2,24,2048]{3,2,1,0:T(8,128)S(1)}, f32[1,2,24,2048]{3,2,1,0:T(8,128)}, u32[]{:S(2)}) copy-start(f32[1,2,24,2048]{3,2,1,0:T(8,128)} %param.17) | copy-start | bytes 1179652
  4.7 20.5 %collective-permute-start = (bf16[999,128]{1,0:T(8,128)(2,1)S(1)}, bf16[999,128]{1,0:T(8,128)(2,1)S(1)}, u32[]{:S(2)}, u32[]{:S(2)}) collective-permute-start(bf16[999,128]{1,0:T(8,128)(2,1)S(1)} %pad_maximum_fusion.1), channel_id=1, source_target_pairs={{0,128},{128,256},{256,384},{384,0},{1,129},{129,257},{257,385},{3... | collective-permute-start | bytes 767240 | tf_op jit(solution)/shard_map/ppermute | solution.py:22
  14.4 31.5 %collective-permute-start.2 = (bf16[999,128]{1,0:T(8,128)(2,1)S(1)}, bf16[999,128]{1,0:T(8,128)(2,1)S(1)}, u32[]{:S(2)}, u32[]{:S(2)}) collective-permute-start(bf16[999,128]{1,0:T(8,128)(2,1)S(1)} %pad_maximum_fusion.2), channel_id=1, source_target_pairs={{0,384},{128,0},{256,128},{384,256},{1,385},{129,1},{257,129},{385... | collective-permute-start | bytes 767240 | tf_op jit(solution)/shard_map/ppermute | solution.py:26
  25.3 24.8 %collective-permute-start.1 = (bf16[483,128]{1,0:T(8,128)(2,1)S(1)}, bf16[483,128]{1,0:T(8,128)(2,1)S(1)}, u32[]{:S(2)}, u32[]{:S(2)}) collective-permute-start(bf16[483,128]{1,0:T(8,128)(2,1)S(1)} %pad_maximum_fusion.6), channel_id=1, source_target_pairs={{0,128},{128,256},{256,384},{384,0},{1,129},{129,257},{257,385},{3... | collective-permute-start | bytes 370952 | tf_op jit(solution)/shard_map/ppermute | solution.py:22
  46.1 13.8 %collective-permute-start.3 = (bf16[484,128]{1,0:T(8,128)(2,1)S(1)}, bf16[484,128]{1,0:T(8,128)(2,1)S(1)}, u32[]{:S(2)}, u32[]{:S(2)}) collective-permute-start(bf16[484,128]{1,0:T(8,128)(2,1)S(1)} %pad_maximum_fusion.7), channel_id=1, source_target_pairs={{0,384},{128,0},{256,128},{384,256},{1,385},{129,1},{257,129},{385... | collective-permute-start | bytes 371720 | tf_op jit(solution)/shard_map/ppermute | solution.py:26
  60.7 15.4 %all-to-all-start = ((bf16[8,2,24,256]{3,2,1,0:T(8,128)(2,1)}), bf16[8,2,24,256]{3,2,1,0:T(8,128)(2,1)S(1)}, u32[]{:S(2)}, u32[]{:S(2)}) async-start(bf16[8,2,24,256]{3,2,1,0:T(8,128)(2,1)} %convert_element_type.116), calls=%async_computation | async-start | bytes 393216 | tf_op jit(solution)/shard_map/all_to_all | solution.py:146
  69.6 6.7 %copy-start.3 = (f32[1,2,24,2048]{3,2,1,0:T(8,128)S(1)}, f32[1,2,24,2048]{3,2,1,0:T(8,128)}, u32[]{:S(2)}) copy-start(f32[1,2,24,2048]{3,2,1,0:T(8,128)} %param.21) | copy-start | bytes 1179652
  77.4 6.0 %copy-start.10 = (f32[18,192]{1,0:T(8,128)S(1)}, f32[18,192]{1,0:T(8,128)}, u32[]{:S(2)}) copy-start(f32[18,192]{1,0:T(8,128)} %param.19) | copy-start | bytes 41476
  77.4 6.0 %copy-start.11 = (f32[18,192]{1,0:T(8,128)S(1)}, f32[18,192]{1,0:T(8,128)}, u32[]{:S(2)}) copy-start(f32[18,192]{1,0:T(8,128)} %param.23) | copy-start | bytes 41476
  77.4 6.7 %copy-start.9 = (f32[64,192]{1,0:T(8,128)S(1)}, f32[64,192]{1,0:T(8,128)}, u32[]{:S(2)}) copy-start(f32[64,192]{1,0:T(8,128)} %param.24) | copy-start | bytes 147460
  77.6 7.5 %copy-start.7 = (f32[72,192]{1,0:T(8,128)S(1)}, f32[72,192]{1,0:T(8,128)}, u32[]{:S(2)}) copy-start(f32[72,192]{1,0:T(8,128)} %param.18) | copy-start | bytes 165892
  77.6 7.5 %copy-start.8 = (f32[72,192]{1,0:T(8,128)S(1)}, f32[72,192]{1,0:T(8,128)}, u32[]{:S(2)}) copy-start(f32[72,192]{1,0:T(8,128)} %param.22) | copy-start | bytes 165892
  78.3 11.6 %all-to-all-start.1 = ((bf16[8,2,24,256]{3,2,1,0:T(8,128)(2,1)}), bf16[8,2,24,256]{3,2,1,0:T(8,128)(2,1)S(1)}, u32[]{:S(2)}, u32[]{:S(2)}) async-start(bf16[8,2,24,256]{3,2,1,0:T(8,128)(2,1)} %copy.54), calls=%async_computation.1 | async-start | bytes 393216 | tf_op jit(solution)/shard_map/all_to_all | solution.py:160
  90.0 31.3 %collective-permute-start.6 = (bf16[999,128]{1,0:T(8,128)(2,1)S(1)}, bf16[999,128]{1,0:T(8,128)(2,1)S(1)}, u32[]{:S(2)}, u32[]{:S(2)}) collective-permute-start(bf16[999,128]{1,0:T(8,128)(2,1)S(1)} %pad_maximum_fusion.3), channel_id=1, source_target_pairs={{0,384},{128,0},{256,128},{384,256},{1,385},{129,1},{257,129},{385... | collective-permute-start | bytes 767240 | tf_op jit(solution)/shard_map/ppermute | solution.py:26
  93.0 31.3 %collective-permute-start.4 = (bf16[999,128]{1,0:T(8,128)(2,1)S(1)}, bf16[999,128]{1,0:T(8,128)(2,1)S(1)}, u32[]{:S(2)}, u32[]{:S(2)}) collective-permute-start(bf16[999,128]{1,0:T(8,128)(2,1)S(1)} %pad_maximum_fusion.3), channel_id=1, source_target_pairs={{0,128},{128,256},{256,384},{384,0},{1,129},{129,257},{257,385},{3... | collective-permute-start | bytes 767240 | tf_op jit(solution)/shard_map/ppermute | solution.py:22
  121.3 14.2 %collective-permute-start.7 = (bf16[500,128]{1,0:T(8,128)(2,1)S(1)}, bf16[500,128]{1,0:T(8,128)(2,1)S(1)}, u32[]{:S(2)}, u32[]{:S(2)}) collective-permute-start(bf16[500,128]{1,0:T(8,128)(2,1)S(1)} %slice.247), channel_id=1, source_target_pairs={{0,384},{128,0},{256,128},{384,256},{1,385},{129,1},{257,129},{385... | collective-permute-start | bytes 384008 | tf_op jit(solution)/shard_map/ppermute | solution.py:26
  124.4 11.2 %collective-permute-start.5 = (bf16[499,128]{1,0:T(8,128)(2,1)S(1)}, bf16[499,128]{1,0:T(8,128)(2,1)S(1)}, u32[]{:S(2)}, u32[]{:S(2)}) collective-permute-start(bf16[499,128]{1,0:T(8,128)(2,1)S(1)} %slice.246), channel_id=1, source_target_pairs={{0,128},{128,256},{256,384},{384,0},{1,129},{129,257},{257,385},{3... | collective-permute-start | bytes 383240 | tf_op jit(solution)/shard_map/ppermute | solution.py:22
  136.1 0.7 copy-start.1
  137.2 0.9 slice-start.1
  137.4 0.8 slice-start
